TPU v7x, 128 devices: a whole 4x4x4 slice. The times are simulated.
128 devices in a mesh: row: 16 (over x, z), col: 8 (over y, core).
Axes of the slice: x: 4, y: 4, z: 4, core: 2. Of those that a mesh axis runs over, the one named last changes fastest.
Arguments:
- a_vals: float32 [16, 8, 448, 4096], P('row', 'col'), may hold values from -0.1875 to 0.1875
- a_row: int32 [16, 8, 448], P('row', 'col'), may hold values from 0 to 63
- a_col: int32 [16, 8, 448], P('row', 'col'), may hold values from 0 to 127
- a_slot: int32 [16, 8, 3, 448], P('row', 'col'), may hold values from 0 to 5
- a_count: int32 [16, 8], P('row', 'col'), may hold values from 1 to 448, as said below
- p_vals: float32 [1024, 3, 4096], P(('row', 'col')), may hold values from -0.75 to 0.75
- p_owner: int32 [1024, 3], P(('row', 'col')), may hold values from 0 to 15, all different within a row; in each aligned block of 8 rows (0 to 7, 8 to 15, ...) at most 2 rows name the same one
- p_sub: int32 [1024, 3], P(('row', 'col')), may hold values from 0 to 7
- ap_cslot: int32 [1024, 3, 6], P(('row', 'col')), may hold values from 0 to 26
Outputs:
- coarse: float32 [128, 27, 4096], P(('row', 'col'))
Inputs may be any that keep to these rules, and one draw needn't show every extreme that they name: `a_count`: at least one device holds exactly 448 listed blocks. `p_owner`: the 3 entries of a fine block row differ; among the rows of one device each row group is named at most 2 times.
All inputs are finite; a program needn't handle non-finite values.
Results may differ from a plain program's by a relative error of at most 0.0001.
Values sent between devices are 32-bit elements; how exact they have to be, the bound alone decides.
No kernel may reach another device: no remote copies, remote signals or barrier semaphores. Data moves between devices by JAX's collectives and lax.ppermute only.
A program may use at most 128 MiB of HBM per device.

v0:
```python
import jax
import jax.numpy as jnp
from jax import lax
from jax.sharding import PartitionSpec as P

BLOCK = 64
CPD = 1
TAP = 6
TC = 27


highest = lax.Precision.HIGHEST
tile_batch = 16


def on_device(a_vals, a_row, a_col, a_slot, a_count, p_vals, p_owner, p_sub, ap_cslot):
    row_devices = lax.axis_size("row")
    col_devices = lax.axis_size("col")
    capacity = a_vals.shape[2]
    rows_dev = p_vals.shape[0]
    branches = p_vals.shape[1]
    tile_len = p_vals.shape[2]
    group_rows = rows_dev * col_devices
    group_coarse = CPD * col_devices
    per_peer = max(2, 3 * rows_dev * branches // (2 * row_devices))
    matrix_tiles = a_vals.reshape(capacity, BLOCK, BLOCK)
    tile_rows = a_row.reshape(capacity)
    tile_cols = a_col.reshape(capacity)
    tile_slots = a_slot.reshape(branches, capacity)
    tile_count = a_count.reshape(())
    panel = lax.all_gather(p_vals, "row", axis=0, tiled=True)
    panel_tiles = panel.reshape(rows_dev * row_devices, branches, BLOCK, BLOCK)

    def add_batch(batch_index, partial_value):
        first_tile = batch_index * tile_batch
        block_tiles = lax.dynamic_slice_in_dim(matrix_tiles, first_tile, tile_batch, 0)
        block_rows = lax.dynamic_slice_in_dim(tile_rows, first_tile, tile_batch, 0)
        block_cols = lax.dynamic_slice_in_dim(tile_cols, first_tile, tile_batch, 0)
        block_slots = lax.dynamic_slice_in_dim(tile_slots, first_tile, tile_batch, 1)
        right_tiles = jnp.take(panel_tiles, block_cols, axis=0)
        products = jnp.einsum("tij,tsjk->tsik", block_tiles, right_tiles, precision=highest)
        is_live = first_tile + jnp.arange(tile_batch, dtype=jnp.int32) < tile_count
        products = jnp.where(is_live[:, None, None, None], products, 0.0)
        target = block_rows[:, None] * TAP + block_slots.T
        return partial_value.at[target.reshape(-1)].add(
            products.reshape(tile_batch * branches, tile_len)
        )

    batches = (tile_count + tile_batch - 1) // tile_batch
    partial_value = lax.fori_loop(
        0, batches, add_batch, jnp.zeros((group_rows * TAP, tile_len), jnp.float32)
    )
    ap_rows = lax.psum_scatter(
        partial_value.reshape(group_rows, TAP, tile_len), "col", scatter_dimension=0, tiled=True
    )
    item_count = rows_dev * branches
    owners = p_owner.reshape(item_count)
    serial = jnp.arange(item_count, dtype=jnp.int32)
    earlier = (owners[:, None] == owners[None, :]) & (serial[None, :] < serial[:, None])
    placed = owners * per_peer + jnp.sum(earlier.astype(jnp.int32), axis=1)
    slots_total = row_devices * per_peer
    metadata = jnp.concatenate(
        [p_sub.reshape(item_count, 1), ap_cslot.reshape(item_count, TAP)], axis=1
    ).astype(jnp.float32)
    meta_send = jnp.zeros((slots_total, TAP + 1), jnp.float32).at[placed].set(metadata)
    ap_items = jnp.broadcast_to(ap_rows[:, None], (rows_dev, branches, TAP, tile_len)).reshape(
        item_count, TAP, tile_len
    )
    packed = jnp.concatenate([p_vals.reshape(item_count, 1, tile_len), ap_items], axis=1)
    outgoing = jnp.zeros((slots_total, TAP + 1, tile_len), jnp.float32).at[placed].set(packed)
    incoming, meta_in = (
        lax.all_to_all(outgoing, "row", split_axis=0, concat_axis=0, tiled=True),
        lax.all_to_all(meta_send, "row", split_axis=0, concat_axis=0, tiled=True),
    )
    left_in = incoming[:, 0].reshape(slots_total, BLOCK, BLOCK)
    right_in = incoming[:, 1:].reshape(slots_total, TAP, BLOCK, BLOCK)
    arrived = jnp.einsum("ejk,eqjl->eqkl", left_in, right_in, precision=highest).reshape(
        slots_total, TAP, tile_len
    )
    arrived_index = meta_in.astype(jnp.int32)
    target = arrived_index[:, :1] * TC + arrived_index[:, 1:]
    coarse_part = (
        jnp.zeros((group_coarse * TC, tile_len), jnp.float32)
        .at[target.reshape(-1)]
        .add(arrived.reshape(slots_total * TAP, tile_len))
    )
    coarse = lax.psum_scatter(
        coarse_part.reshape(group_coarse, TC, tile_len), "col", scatter_dimension=0, tiled=True
    )
    return coarse


def solution(mesh):
    placed = (
        P("row", "col", None, None),
        P("row", "col", None),
        P("row", "col", None),
        P("row", "col", None, None),
        P("row", "col"),
        P(("row", "col"), None, None),
        P(("row", "col"), None),
        P(("row", "col"), None),
        P(("row", "col"), None, None),
    )
    return jax.shard_map(
        on_device,
        mesh=mesh,
        in_specs=placed,
        out_specs=P(("row", "col"), None, None),
        check_vma=False,
    )
```

profile of v0, /device:TPU:0, one launch (start us, length us, event | category | flops | bytes accessed | tf_op | source)
XLA Modules:
  0.0 882.7 jit_solution(11410659418948693144)
XLA Ops:
  8.0 9.0 %copy.84 = f32[1,1,448,4096]{2,3,1,0:T(8,128)} copy(f32[1,1,448,4096]{3,2,1,0:T(8,128)} %param.11) | data formatting | bytes 14680064 | tf_op args[0]
  17.0 11.9 %copy.86 = f32[448,64,64]{2,1,0:T(8,128)} copy(f32[448,64,64]{0,2,1:T(8,128)} %bitcast.49) | data formatting | bytes 14680064 | tf_op jit(solution)/shard_map/while | solution.py:50
  29.0 44.5 %all-gather.2.cloned.1.call-done = f32[128,3,4096]{2,0,1:T(8,128)} async-done(((f32[8,3,4096]{2,0,1:T(8,128)}), f32[128,3,4096]{2,0,1:T(8,128)}) %all-gather.2.cloned.1.call-update) | async-done | bytes 6291472 | tf_op jit(solution)/shard_map/all_gather | solution.py:31
  73.5 6.6 copy.83
  80.1 12.7 %copy.85 = f32[128,3,64,64]{3,2,1,0:T(8,128)} copy(f32[128,3,64,64]{0,3,2,1:T(8,128)} %bitcast.50) | data formatting | bytes 12582912 | tf_op jit(solution)/shard_map/while | solution.py:50
  96.2 309.5 %while.10 = (s32[]{:T(128)}, f32[384,4096]{1,0:T(8,128)}, s32[]{:T(128)}, s32[448]{0:T(512)}, s32[3,448]{0,1:T(8,128)S(1)}, /*index=5*/s32[]{:T(128)}, s32[448]{...) while((s32[]{:T(128)}, f32[384,4096]{1,0:T(8,128)}, ...), condition=%wide.region_4.5_spmd, body=%wide.region_2.4_spmd.sunk | while | flops 151586128 | bytes 9181187 | solution.py:50
  97.6 5.2 gather_fusion
  108.6 6.9 scatter_fusion
  116.9 5.2 gather_fusion
  128.0 6.9 scatter_fusion
  136.3 5.2 gather_fusion
  147.3 6.9 scatter_fusion
  155.6 5.2 gather_fusion
  166.7 6.9 scatter_fusion
  175.0 5.2 gather_fusion
  186.0 6.9 scatter_fusion
  194.3 5.2 gather_fusion
  205.3 6.9 scatter_fusion
  213.7 5.2 gather_fusion
  224.7 6.9 scatter_fusion
  233.0 5.2 gather_fusion
  244.0 6.9 scatter_fusion
  252.3 5.2 gather_fusion
  263.4 6.9 scatter_fusion
  271.7 5.2 gather_fusion
  282.7 6.9 scatter_fusion
  291.0 5.2 gather_fusion
  302.1 6.9 scatter_fusion
  310.4 5.2 gather_fusion
  321.4 6.9 scatter_fusion
  329.7 5.2 gather_fusion
  340.8 6.9 scatter_fusion
  360.1 6.9 scatter_fusion
  368.4 5.2 gather_fusion
  379.5 6.9 scatter_fusion
  398.8 6.9 scatter_fusion
  405.7 7.5 reshape.161
  416.2 236.4 %all-to-all-start = ((f32[16,2,7]{2,1,0:T(2,128)}), f32[16,2,7]{2,1,0:T(2,128)S(1)}, u32[]{:S(2)}, u32[]{:S(2)}) async-start(f32[16,2,7]{2,1,0:T(2,128)} %bitcast.7), calls=%async_computation | async-start | bytes 32768 | tf_op jit(solution)/shard_map/all_to_all | solution.py:73
  653.1 44.3 %reduce-scatter.3.cloned.1.call-done = f32[8,6,4096]{2,1,0:T(8,128)} async-done(((f32[64,6,4096]{2,1,0:T(8,128)}), f32[8,6,4096]{2,1,0:T(8,128)}) %reduce-scatter.3.cloned.1.call-update) | async-done | bytes 786448 | tf_op jit(solution)/shard_map/reduce_scatter | solution.py:53
  708.4 6.5 scatter_fusion.1
  714.9 7.1 all-to-all-start.1
  722.4 55.9 %all-to-all-done.1 = f32[32,7,4096]{2,1,0:T(8,128)} async-done(((f32[32,7,4096]{2,1,0:T(8,128)}), f32[32,7,4096]{2,1,0:T(8,128)}, u32[]{:S(2)}, u32[]{:S(2)}) %all-to-all-start.1) | async-done | bytes 3670048 | tf_op jit(solution)/shard_map/all_to_all | solution.py:72
  783.3 6.8 reshape.208
  794.1 13.3 %convolution_bitcast_fusion = f32[32,6,64,64]{2,3,1,0:T(8,128)} fusion(f32[32,6,64,64]{3,2,1,0:T(8,128)} %reshape.208, f32[32,64,64,1]{2,1,0,3:T(8,128)S(1)} %reshape.207), kind=kOutput, calls=%fused_computation.23 | convolution fusion | flops 603979776 | bytes 6815744 | tf_op jit(solution)/shard_map/ejk,eqjl->eqkl/dot_general | solution.py:77
  807.4 6.6 copy.91
  814.0 5.9 reshape.201
  819.9 6.7 scatter_custom_fusion.3
  829.1 44.9 %reduce-scatter.5.cloned.1.call-done = f32[1,27,4096]{2,1,0:T(8,128)} async-done(((f32[8,27,4096]{2,1,0:T(8,128)}), f32[1,27,4096]{2,1,0:T(8,128)}) %reduce-scatter.5.cloned.1.call-update) | async-done | bytes 442384 | tf_op jit(solution)/shard_map/reduce_scatter | solution.py:87
  (201 shorter events, 158.2 us)
Async XLA Ops:
  6.5 66.9 %all-gather.2.cloned.1.call-start = ((), (), s32[]{:S(2)}) async-start(), calls=%async_computation.4 | async-start | bytes 6684672 | tf_op jit(solution)/shard_map/all_gather | solution.py:31
  7.3 690.1 %reduce-scatter.3.cloned.1.call-start = ((), (), s32[]{:S(2)}) async-start(), calls=%async_computation.5 | async-start | bytes 9437184 | tf_op jit(solution)/shard_map/reduce_scatter | solution.py:53
  17.0 11.9 %copy-start.3 = (s32[1,1,3,448]{3,1,2,0:T(1,128)S(1)}, s32[1,1,3,448]{3,1,2,0:T(1,128)}, u32[]{:S(2)}) copy-start(s32[1,1,3,448]{3,1,2,0:T(1,128)} %param.14) | copy-start | bytes 16132
  413.2 0.7 copy-start.2
  413.2 1.0 copy-start.1
  413.2 1.2 copy-start.4
  413.2 239.4 %copy-start = (f32[8,3,4096]{2,0,1:T(8,128)S(1)}, f32[8,3,4096]{2,0,1:T(8,128)}, u32[]{:S(2)}) copy-start(f32[8,3,4096]{2,0,1:T(8,128)} %param.16) | copy-start | bytes 1179652
  414.9 1.2 copy-start.5
  416.2 298.7 %all-to-all-start = ((f32[16,2,7]{2,1,0:T(2,128)}), f32[16,2,7]{2,1,0:T(2,128)S(1)}, u32[]{:S(2)}, u32[]{:S(2)}) async-start(f32[16,2,7]{2,1,0:T(2,128)} %bitcast.7), calls=%async_computation | async-start | bytes 32768 | tf_op jit(solution)/shard_map/all_to_all | solution.py:73
  705.9 2.4 copy-start.6
  714.9 63.3 %all-to-all-start.1 = ((f32[32,7,4096]{2,1,0:T(8,128)}), f32[32,7,4096]{2,1,0:T(8,128)}, u32[]{:S(2)}, u32[]{:S(2)}) async-start(f32[32,7,4096]{2,1,0:T(8,128)} %scatter_fusion.1), calls=%async_computation.2 | async-start | bytes 8388608 | tf_op jit(solution)/shard_map/all_to_all | solution.py:72
  722.0 152.0 %reduce-scatter.5.cloned.1.call-start = ((), (), s32[]{:S(2)}) async-start(), calls=%async_computation.6 | async-start | bytes 4718592 | tf_op jit(solution)/shard_map/reduce_scatter | solution.py:87
Sparse Core Ops, SparseCore 0:
  9.5 63.8 all-gather.1
  413.4 283.9 reduce-scatter.2
  829.2 44.6 reduce-scatter.4
where the time goes:
time: 889 us; the launch traced here: 883 us
  starting transfers between devices  244 us (27%)
  local copies, waits for them, and re-layouts  204 us (23%)
  waiting for transfers between devices  190 us (21%)
  other arithmetic  155 us (17%)
  matrix products  75.4 us (8%)
  between operations  14 us (2%)
    all_to_all x1, starting transfers between devices, on_device(): lax.all_to_all(meta_send, 'row', split_axis=0, concat_axis=0, tiled=True)  236 us
    scatter-add x16, other arithmetic, add_batch(): partial_value.at[target.reshape(-1)]  110 us
    gather x16, local copies, waits for them, and re-layouts, add_batch(): right_tiles = jnp.take(panel_tiles, block_cols, axis=0)  83.6 us
    dot_general x16, matrix products, add_batch(): jnp.einsum('tij,tsjk->tsik', block_tiles, right_tiles, precision=highest)  62.1 us
    all_to_all x1, waiting for transfers between devices, on_device(): lax.all_to_all(outgoing, 'row', split_axis=0, concat_axis=0, tiled=True)  55.9 us
    reduce_scatter x1, waiting for transfers between devices, on_device(): lax.psum_scatter(coarse_part.reshape(group_coarse, TC, tile_len), 'col',...  44.9 us
    all_gather x1, waiting for transfers between devices, on_device(): panel = lax.all_gather(p_vals, 'row', axis=0, tiled=True)  44.5 us
    reduce_scatter x1, waiting for transfers between devices, on_device(): lax.psum_scatter(partial_value.reshape(group_rows, TAP, tile_len), 'col',...  44.3 us
  transfers between devices with their start and end apart: 5, of which 4 were waited for; matrix products, arithmetic and copies ran while one was open for 5% of the time, Pallas kernels for 0%

commit v1 on v0

--- a/solution.py
+++ b/solution.py
@@ -1,6 +1,10 @@
+import functools
+
 import jax
 import jax.numpy as jnp
 from jax import lax
+from jax.experimental import pallas as pl
+from jax.experimental.pallas import tpu as pltpu
 from jax.sharding import PartitionSpec as P
 
 BLOCK = 64
@@ -10,7 +14,65 @@
 
 
 highest = lax.Precision.HIGHEST
-tile_batch = 16
+chunk = 32
+
+
+def ap_kernel(rows_ref, cols_ref, slots_ref, cnt_ref, a_ref, p_ref, o_ref):
+    c = pl.program_id(0)
+    capacity = rows_ref.shape[0]
+    branches = p_ref.shape[1]
+
+    @pl.when(c == 0)
+    def _():
+        o_ref[...] = jnp.zeros(o_ref.shape, o_ref.dtype)
+
+    count = cnt_ref[0]
+
+    def body(u, carry):
+        t = c * chunk + u
+
+        @pl.when(t < count)
+        def _():
+            a = a_ref[u]
+            col = cols_ref[t]
+            row = rows_ref[t]
+            for s in range(branches):
+                prod = jnp.dot(
+                    a, p_ref[col, s], preferred_element_type=jnp.float32, precision=highest
+                )
+                idx = row * TAP + slots_ref[s * capacity + t]
+                o_ref[idx] += prod
+
+        return carry
+
+    lax.fori_loop(0, chunk, body, 0)
+
+
+def ap_partial(tiles, rows, cols, slots, count, panel, out_rows):
+    capacity = tiles.shape[0]
+    chunks = capacity // chunk
+
+    def a_map(c, rows_ref, cols_ref, slots_ref, cnt_ref):
+        last = (cnt_ref[0] - 1) // chunk
+        return (jnp.minimum(c, last), 0, 0)
+
+    grid_spec = pltpu.PrefetchScalarGridSpec(
+        num_scalar_prefetch=4,
+        grid=(chunks,),
+        in_specs=[
+            pl.BlockSpec((chunk, BLOCK, BLOCK), a_map),
+            pl.BlockSpec(memory_space=pltpu.VMEM),
+        ],
+        out_specs=pl.BlockSpec(memory_space=pltpu.VMEM),
+    )
+    return pl.pallas_call(
+        ap_kernel,
+        out_shape=jax.ShapeDtypeStruct((out_rows * TAP, BLOCK, BLOCK), jnp.float32),
+        grid_spec=grid_spec,
+        compiler_params=pltpu.CompilerParams(
+            dimension_semantics=("arbitrary",), vmem_limit_bytes=56 * 1024 * 1024
+        ),
+    )(rows, cols, slots, count, tiles, panel)
 
 
 def on_device(a_vals, a_row, a_col, a_slot, a_count, p_vals, p_owner, p_sub, ap_cslot):
@@ -26,29 +88,13 @@
     matrix_tiles = a_vals.reshape(capacity, BLOCK, BLOCK)
     tile_rows = a_row.reshape(capacity)
     tile_cols = a_col.reshape(capacity)
-    tile_slots = a_slot.reshape(branches, capacity)
-    tile_count = a_count.reshape(())
+    tile_slots = a_slot.reshape(branches * capacity)
+    tile_count = a_count.reshape(1)
     panel = lax.all_gather(p_vals, "row", axis=0, tiled=True)
     panel_tiles = panel.reshape(rows_dev * row_devices, branches, BLOCK, BLOCK)
 
-    def add_batch(batch_index, partial_value):
-        first_tile = batch_index * tile_batch
-        block_tiles = lax.dynamic_slice_in_dim(matrix_tiles, first_tile, tile_batch, 0)
-        block_rows = lax.dynamic_slice_in_dim(tile_rows, first_tile, tile_batch, 0)
-        block_cols = lax.dynamic_slice_in_dim(tile_cols, first_tile, tile_batch, 0)
-        block_slots = lax.dynamic_slice_in_dim(tile_slots, first_tile, tile_batch, 1)
-        right_tiles = jnp.take(panel_tiles, block_cols, axis=0)
-        products = jnp.einsum("tij,tsjk->tsik", block_tiles, right_tiles, precision=highest)
-        is_live = first_tile + jnp.arange(tile_batch, dtype=jnp.int32) < tile_count
-        products = jnp.where(is_live[:, None, None, None], products, 0.0)
-        target = block_rows[:, None] * TAP + block_slots.T
-        return partial_value.at[target.reshape(-1)].add(
-            products.reshape(tile_batch * branches, tile_len)
-        )
-
-    batches = (tile_count + tile_batch - 1) // tile_batch
-    partial_value = lax.fori_loop(
-        0, batches, add_batch, jnp.zeros((group_rows * TAP, tile_len), jnp.float32)
+    partial_value = ap_partial(
+        matrix_tiles, tile_rows, tile_cols, tile_slots, tile_count, panel_tiles, group_rows
     )
     ap_rows = lax.psum_scatter(
         partial_value.reshape(group_rows, TAP, tile_len), "col", scatter_dimension=0, tiled=True

time: 889 us -> 464 us (0.52)
  starting transfers between devices: 244 us -> 58.5 us
  other arithmetic: 155 us -> 9.01 us
  local copies, waits for them, and re-layouts: 204 us -> 106 us
  Pallas kernels: 0 us -> 72.4 us
  matrix products: 75.4 us -> 13.3 us
    all_to_all x1, starting transfers between devices: 236 us -> 51.3 us  [on_device(): lax.all_to_all(meta_send, 'row', split_axis=0, concat_axis=0, tiled=True)]
    scatter-add x16 -> x0, other arithmetic: 110 us -> none  [add_batch(): partial_value.at[target.reshape(-1)]]
    gather x16 -> x0, local copies, waits for them, and re-layouts: 83.6 us -> none  [add_batch(): right_tiles = jnp.take(panel_tiles, block_cols, axis=0)]
    pallas_call x0 -> x1, Pallas kernels: none -> 72.4 us  [ap_partial(): pl.pallas_call(ap_kernel, out_shape=jax.ShapeDtypeStruct((out_rows * TAP,...]
    dot_general x16 -> x0, matrix products: 62.1 us -> none  [add_batch(): jnp.einsum('tij,tsjk->tsik', block_tiles, right_tiles, precision=highest)]
    while x2 -> x0, local copies, waits for them, and re-layouts: 24.6 us -> none  [on_device(): lax.fori_loop(0, batches, add_batch, jnp.zeros((group_rows * TAP, tile_le...]
    and x16 -> x0, other arithmetic: 22.5 us -> none  [add_batch(): right_tiles = jnp.take(panel_tiles, block_cols, axis=0)]
    reshape x32 -> x3, local copies, waits for them, and re-layouts: 9.5 us -> 25.3 us  [the longest x1 12.7 us: on_device(): panel_tiles = panel.reshape(rows_dev * row_devices, branches, BLOCK, BLOCK)]
  transfers between devices with their start and end apart: 5 -> 5, of which waited for: 4 -> 4; matrix products, arithmetic and copies ran while one was open for 5% -> 9% of each run, Pallas kernels for 0% -> 0%
where the time goes in v1:
time: 464 us; the launch traced here: 463 us
  waiting for transfers between devices  190 us (41%)
  local copies, waits for them, and re-layouts  106 us (23%)
  Pallas kernels  72.4 us (16%)
  starting transfers between devices  58.5 us (13%)
  between operations  13.9 us (3%)
  matrix products  13.3 us (3%)
  other arithmetic  9.01 us (2%)
    pallas_call x1, Pallas kernels, ap_partial(): pl.pallas_call(ap_kernel, out_shape=jax.ShapeDtypeStruct((out_rows * TAP,...  72.4 us
    all_to_all x1, waiting for transfers between devices, on_device(): lax.all_to_all(outgoing, 'row', split_axis=0, concat_axis=0, tiled=True)  54 us
    all_to_all x1, starting transfers between devices, on_device(): lax.all_to_all(meta_send, 'row', split_axis=0, concat_axis=0, tiled=True)  51.3 us
    reduce_scatter x1, waiting for transfers between devices, on_device(): lax.psum_scatter(coarse_part.reshape(group_coarse, TC, tile_len), 'col',...  47.7 us
    reduce_scatter x1, waiting for transfers between devices, on_device(): lax.psum_scatter(partial_value.reshape(group_rows, TAP, tile_len), 'col',...  44.1 us
    all_gather x1, waiting for transfers between devices, on_device(): panel = lax.all_gather(p_vals, 'row', axis=0, tiled=True)  43.9 us
    dot_general x1, matrix products, on_device(): jnp.einsum('ejk,eqjl->eqkl', left_in, right_in, precision=highest)  13.3 us
    reshape x1, local copies, waits for them, and re-layouts, on_device(): panel_tiles = panel.reshape(rows_dev * row_devices, branches, BLOCK, BLOCK)  12.7 us
  transfers between devices with their start and end apart: 5, of which 4 were waited for; matrix products, arithmetic and copies ran while one was open for 9% of the time, Pallas kernels for 0%

profile of v1, /device:TPU:0, one launch (start us, length us, event | category | flops | bytes accessed | tf_op | source)
XLA Modules:
  0.0 463.2 jit_solution(15404420464246889183)
XLA Ops:
  6.5 0.7 all-gather.2.cloned.1.call-update
  7.3 9.0 %copy.69 = f32[1,1,448,4096]{2,3,1,0:T(8,128)} copy(f32[1,1,448,4096]{3,2,1,0:T(8,128)} %param.9) | data formatting | bytes 14680064 | tf_op args[0]
  16.3 11.9 %copy.71.a_ref = f32[448,64,64]{2,1,0:T(8,128)} copy(f32[448,64,64]{0,2,1:T(8,128)} %bitcast.27) | data formatting | bytes 14680064 | tf_op jit(solution)/shard_map/reshape | solution.py:88
  28.3 0.7 reshape.111.slots_ref
  29.6 43.9 %all-gather.2.cloned.1.call-done = f32[128,3,4096]{2,0,1:T(8,128)} async-done(((f32[8,3,4096]{2,0,1:T(8,128)}), f32[128,3,4096]{2,0,1:T(8,128)}) %all-gather.2.cloned.1.call-update) | async-done | bytes 6291472 | tf_op jit(solution)/shard_map/all_gather | solution.py:93
  73.5 6.6 %copy.70 = f32[128,3,4096]{0,2,1:T(8,128)} copy(f32[128,3,4096]{2,0,1:T(8,128)} %all-gather.2.cloned.1.call-done) | data formatting | bytes 12582912 | tf_op jit(solution)/shard_map/all_gather | solution.py:93
  80.1 12.7 %copy.72.p_ref = f32[128,3,64,64]{3,2,1,0:T(8,128)} copy(f32[128,3,64,64]{0,3,2,1:T(8,128)} %bitcast.28) | data formatting | bytes 12582912 | tf_op jit(solution)/shard_map/reshape | solution.py:94
  92.8 72.4 %shard_map.91 = f32[384,64,64]{2,1,0:T(8,128)} custom-call(s32[448]{0:T(512)} %bitcast.31, s32[448]{0:T(512)} %bitcast.32, s32[1344]{0:T(1024)} %reshape.111.slots_ref, s32[1]{0:T(128)} %bitcast.26.cnt_ref, f32[448,64,64]{2,1,0:T(8,128)} %copy.71.a_ref, f32[128,3,64,64]{3,2,1,0:T(8,128)} %copy.72.p_ref), custom_call_target="tpu_custom_call" | custom-call | tf_op jit(solution)/shard_map/pallas_call | solution.py:68
  165.2 12.7 %reshape.115 = f32[64,6,4096]{2,1,0:T(8,128)} reshape(f32[384,64,64]{2,1,0:T(8,128)} %shard_map.91) | data formatting | bytes 12582912 | tf_op jit(solution)/shard_map/reshape | solution.py:100
  177.9 0.6 copy-done.2
  178.5 0.1 copy.64
  178.6 0.1 copy.63
  178.7 0.1 mul.20
  178.8 0.1 eq.15
  178.9 0.1 copy.66
  179.0 0.1 reshape.106
  179.1 0.1 copy.65
  179.2 0.1 reshape.105
  179.3 0.1 copy.67
  179.4 0.2 convert_reduce_fusion
  179.6 1.2 scatter_custom_fusion
  180.8 51.3 %all-to-all-start = ((f32[16,2,7]{2,1,0:T(2,128)}), f32[16,2,7]{2,1,0:T(2,128)S(1)}, u32[]{:S(2)}, u32[]{:S(2)}) async-start(f32[16,2,7]{2,1,0:T(2,128)} %bitcast.2), calls=%async_computation | async-start | bytes 32768 | tf_op jit(solution)/shard_map/all_to_all | solution.py:119
  232.1 0.3 copy.68
  232.4 0.2 reshape.108
  232.6 44.1 %reduce-scatter.3.cloned.1.call-done = f32[8,6,4096]{2,1,0:T(8,128)} async-done(((f32[64,6,4096]{2,1,0:T(8,128)}), f32[8,6,4096]{2,1,0:T(8,128)}) %reduce-scatter.3.cloned.1.call-update) | async-done | bytes 786448 | tf_op jit(solution)/shard_map/reduce_scatter | solution.py:99
  276.7 1.7 copy.73
  278.4 0.8 broadcast_in_dim.11
  279.2 2.6 reshape.116
  281.8 1.8 pad_maximum_fusion
  283.7 1.6 copy.74
  285.3 2.4 broadcast_in_dim.10
  287.7 6.5 %scatter_fusion = f32[32,7,4096]{2,1,0:T(8,128)} fusion(f32[32,7,4096]{2,1,0:T(8,128)} %broadcast_in_dim.10, s32[24]{0:T(128)S(1)} %copy-done.6, f32[24,7,4096]{2,1,0:T(8,128)S(1)} %copy.74), kind=kCustom, calls=%fused_computation.1 | custom fusion | bytes 8257632 | tf_op jit(solution)/shard_map/scatter | solution.py:116
  294.2 7.1 %all-to-all-start.1 = ((f32[32,7,4096]{2,1,0:T(8,128)}), f32[32,7,4096]{2,1,0:T(8,128)}, u32[]{:S(2)}, u32[]{:S(2)}) async-start(f32[32,7,4096]{2,1,0:T(8,128)} %scatter_fusion), calls=%async_computation.2 | async-start | bytes 8388608 | tf_op jit(solution)/shard_map/all_to_all | solution.py:118
  301.5 0.1 fusion.3
  301.6 0.1 slice_add_fusion
  301.6 0.1 reshape.107
  301.8 54.0 %all-to-all-done.1 = f32[32,7,4096]{2,1,0:T(8,128)} async-done(((f32[32,7,4096]{2,1,0:T(8,128)}), f32[32,7,4096]{2,1,0:T(8,128)}, u32[]{:S(2)}, u32[]{:S(2)}) %all-to-all-start.1) | async-done | bytes 3670048 | tf_op jit(solution)/shard_map/all_to_all | solution.py:118
  355.8 5.1 %slice.18 = f32[32,6,4096]{2,1,0:T(8,128)} slice(f32[32,7,4096]{2,1,0:T(8,128)} %all-to-all-done.1), slice={[0:32], [1:7], [0:4096]} | slice | bytes 6291456 | tf_op jit(solution)/shard_map/slice | solution.py:122
  360.9 6.8 %reshape.144 = f32[32,6,64,64]{3,2,1,0:T(8,128)} reshape(f32[32,6,4096]{2,1,0:T(8,128)} %slice.18) | data formatting | bytes 6291456 | tf_op jit(solution)/shard_map/reshape | solution.py:122
  367.7 3.6 slice_reduce_fusion
  371.3 0.4 reshape.143
  371.7 13.3 %convolution_bitcast_fusion = f32[32,6,64,64]{2,3,1,0:T(8,128)} fusion(f32[32,6,64,64]{3,2,1,0:T(8,128)} %reshape.144, f32[32,64,64,1]{2,1,0,3:T(8,128)S(1)} %reshape.143), kind=kOutput, calls=%fused_computation.4 | convolution fusion | flops 603979776 | bytes 6815744 | tf_op jit(solution)/shard_map/ejk,eqjl->eqkl/dot_general | solution.py:123
  385.0 6.6 %copy.77 = f32[32,6,64,64]{3,2,1,0:T(8,128)} copy(f32[32,6,64,64]{2,3,1,0:T(8,128)} %convolution_bitcast_fusion) | data formatting | bytes 6291456 | tf_op jit(solution)/shard_map/ejk,eqjl->eqkl/transpose | solution.py:123
  391.6 5.9 %reshape.139 = f32[192,4096]{1,0:T(8,128)} reshape(f32[32,6,64,64]{3,2,1,0:T(8,128)} %copy.77) | data formatting | bytes 6291456 | tf_op jit(solution)/shard_map/reshape;reshape | solution.py:131
  397.5 6.7 %scatter_custom_fusion.2 = f32[216,4096]{1,0:T(8,128)S(1)} fusion(s32[192]{0:T(256)S(1)} %bitcast.33, f32[192,4096]{1,0:T(8,128)} %reshape.139, f32[]{:T(128)} %constant.6.clone.1), kind=kCustom, calls=%fused_computation.5 | custom fusion | flops 786432 | bytes 3539456 | tf_op jit(solution)/shard_map/scatter-add | solution.py:131
  404.2 2.4 reshape.118
  406.6 47.7 %reduce-scatter.5.cloned.1.call-done = f32[1,27,4096]{2,1,0:T(8,128)} async-done(((f32[8,27,4096]{2,1,0:T(8,128)}), f32[1,27,4096]{2,1,0:T(8,128)}) %reduce-scatter.5.cloned.1.call-update) | async-done | bytes 442384 | tf_op jit(solution)/shard_map/reduce_scatter | solution.py:133
  454.4 2.3 copy.78
  (25 shorter events, 0.2 us)
Async XLA Ops:
  6.5 66.9 %all-gather.2.cloned.1.call-start = ((), (), s32[]{:S(2)}) async-start(), calls=%async_computation.4 | async-start | bytes 6684672 | tf_op jit(solution)/shard_map/all_gather | solution.py:93
  7.3 269.5 %reduce-scatter.3.cloned.1.call-start = ((), (), s32[]{:S(2)}) async-start(), calls=%async_computation.5 | async-start | bytes 9437184 | tf_op jit(solution)/shard_map/reduce_scatter | solution.py:99
  16.3 11.9 %copy-start.3 = (s32[1,1,3,448]{3,1,2,0:T(1,128)S(1)}, s32[1,1,3,448]{3,1,2,0:T(1,128)}, u32[]{:S(2)}) copy-start(s32[1,1,3,448]{3,1,2,0:T(1,128)} %param.12) | copy-start | bytes 16132
  177.9 0.7 copy-start.2
  177.9 1.0 copy-start.1
  177.9 1.2 copy-start.4
  177.9 54.2 %copy-start = (f32[8,3,4096]{2,0,1:T(8,128)S(1)}, f32[8,3,4096]{2,0,1:T(8,128)}, u32[]{:S(2)}) copy-start(f32[8,3,4096]{2,0,1:T(8,128)} %param.14) | copy-start | bytes 1179652
  179.6 1.2 copy-start.5
  180.8 113.5 %all-to-all-start = ((f32[16,2,7]{2,1,0:T(2,128)}), f32[16,2,7]{2,1,0:T(2,128)S(1)}, u32[]{:S(2)}, u32[]{:S(2)}) async-start(f32[16,2,7]{2,1,0:T(2,128)} %bitcast.2), calls=%async_computation | async-start | bytes 32768 | tf_op jit(solution)/shard_map/all_to_all | solution.py:119
  283.6 4.1 copy-start.6
  294.2 61.5 %all-to-all-start.1 = ((f32[32,7,4096]{2,1,0:T(8,128)}), f32[32,7,4096]{2,1,0:T(8,128)}, u32[]{:S(2)}, u32[]{:S(2)}) async-start(f32[32,7,4096]{2,1,0:T(8,128)} %scatter_fusion), calls=%async_computation.2 | async-start | bytes 8388608 | tf_op jit(solution)/shard_map/all_to_all | solution.py:118
  301.4 153.0 %reduce-scatter.5.cloned.1.call-start = ((), (), s32[]{:S(2)}) async-start(), calls=%async_computation.6 | async-start | bytes 4718592 | tf_op jit(solution)/shard_map/reduce_scatter | solution.py:133
Sparse Core Ops, SparseCore 0:
  9.5 63.8 all-gather.1
  178.0 98.6 reduce-scatter.2
  406.8 47.5 reduce-scatter.4

commit v2 on v1

v2 whole, which is shorter than its diff:
```python
import jax
import jax.numpy as jnp
from jax import lax
from jax.experimental import pallas as pl
from jax.experimental.pallas import tpu as pltpu
from jax.sharding import PartitionSpec as P

BLOCK = 64
TAP = 6
TC = 27
LANES = 128
HALF = BLOCK * BLOCK // LANES

highest = lax.Precision.HIGHEST
chunk = 32


def ap_kernel(rows_ref, cols_ref, slots_ref, cnt_ref, a_ref, p_ref, o_ref):
    c = pl.program_id(0)
    capacity = rows_ref.shape[0]
    branches = p_ref.shape[2] // LANES

    @pl.when(c == 0)
    def _():
        o_ref[...] = jnp.zeros(o_ref.shape, o_ref.dtype)

    count = cnt_ref[0]

    def body(u, carry):
        t = c * chunk + u

        @pl.when(t < count)
        def _():
            col = cols_ref[t]
            row = rows_ref[t]
            prod = jnp.dot(
                a_ref[u], p_ref[col], preferred_element_type=jnp.float32, precision=highest
            )
            for s in range(branches):
                idx = row * TAP + slots_ref[s * capacity + t]
                o_ref[idx] += prod[:, s * LANES:(s + 1) * LANES]

        return carry

    lax.fori_loop(0, chunk, body, 0)


def ap_partial(tiles, rows, cols, slots, count, pdiag, out_rows):
    capacity = tiles.shape[0]
    chunks = capacity // chunk

    def a_map(c, rows_ref, cols_ref, slots_ref, cnt_ref):
        last = (cnt_ref[0] - 1) // chunk
        return (jnp.minimum(c, last), 0, 0)

    grid_spec = pltpu.PrefetchScalarGridSpec(
        num_scalar_prefetch=4,
        grid=(chunks,),
        in_specs=[
            pl.BlockSpec((chunk, HALF, LANES), a_map),
            pl.BlockSpec(memory_space=pltpu.VMEM),
        ],
        out_specs=pl.BlockSpec(memory_space=pltpu.VMEM),
    )
    return pl.pallas_call(
        ap_kernel,
        out_shape=jax.ShapeDtypeStruct((out_rows * TAP, HALF, LANES), jnp.float32),
        grid_spec=grid_spec,
        compiler_params=pltpu.CompilerParams(
            dimension_semantics=("arbitrary",), vmem_limit_bytes=60 * 1024 * 1024
        ),
    )(rows, cols, slots, count, tiles, pdiag)


def block_diagonal(panel):
    cols, branches = panel.shape[:2]
    p4 = panel.reshape(cols, branches, BLOCK, BLOCK)
    zero = jnp.zeros_like(p4)
    top = jnp.concatenate([p4, zero], axis=3)
    bottom = jnp.concatenate([zero, p4], axis=3)
    both = jnp.concatenate([top, bottom], axis=2)
    return both.transpose(0, 2, 1, 3).reshape(cols, 2 * BLOCK, branches * LANES)


def on_device(a_vals, a_row, a_col, a_slot, a_count, p_vals, p_owner, p_sub, ap_cslot):
    row_devices = lax.axis_size("row")
    col_devices = lax.axis_size("col")
    capacity = a_vals.shape[2]
    rows_dev = p_vals.shape[0]
    branches = p_vals.shape[1]
    tile_len = p_vals.shape[2]
    group_rows = rows_dev * col_devices
    per_peer = 2
    item_count = rows_dev * branches
    slots_total = row_devices * per_peer

    meta_local = jnp.concatenate(
        [p_owner.reshape(item_count, 1), p_sub.reshape(item_count, 1),
         ap_cslot.reshape(item_count, TAP)], axis=1
    ).astype(jnp.float32)
    meta_all = lax.all_gather(meta_local, "row", axis=0, tiled=False)

    panel = lax.all_gather(p_vals, "row", axis=0, tiled=True)
    pdiag = block_diagonal(panel)
    matrix_tiles = a_vals.reshape(capacity, HALF, LANES)
    partial_value = ap_partial(
        matrix_tiles, a_row.reshape(capacity), a_col.reshape(capacity),
        a_slot.reshape(branches * capacity), a_count.reshape(1), pdiag, group_rows
    )
    ap_rows = lax.psum_scatter(
        partial_value.reshape(group_rows, TAP, HALF, LANES), "col", scatter_dimension=0, tiled=True
    )

    p4 = p_vals.reshape(rows_dev, branches, BLOCK, BLOCK)
    ap4 = ap_rows.reshape(rows_dev, TAP, BLOCK, BLOCK)
    prods = jnp.einsum("isjk,iqjl->isqkl", p4, ap4, precision=highest)
    prods = prods.reshape(item_count, TAP, tile_len)
    prods = jnp.concatenate([prods, jnp.zeros((1, TAP, tile_len), jnp.float32)], axis=0)

    owners = p_owner.reshape(item_count)
    serial = jnp.arange(item_count, dtype=jnp.int32)
    earlier = (owners[:, None] == owners[None, :]) & (serial[None, :] < serial[:, None])
    placed = owners * per_peer + jnp.sum(earlier.astype(jnp.int32), axis=1)
    slot_ids = jnp.arange(slots_total, dtype=jnp.int32)
    hit = placed[None, :] == slot_ids[:, None]
    source = jnp.where(
        jnp.any(hit, axis=1), jnp.sum(jnp.where(hit, serial[None, :], 0), axis=1), item_count
    )
    outgoing = jnp.take(prods, source, axis=0)
    incoming = lax.all_to_all(outgoing, "row", split_axis=0, concat_axis=0, tiled=True)

    me = lax.axis_index("row").astype(jnp.float32)
    meta_all = meta_all.reshape(row_devices, item_count, TAP + 2)
    match = meta_all[:, :, 0] == me
    rank = jnp.cumsum(match.astype(jnp.int32), axis=1) - 1
    ranks = jnp.arange(per_peer, dtype=jnp.int32)
    pick = match[:, None, :] & (rank[:, None, :] == ranks[None, :, None])
    dest = meta_all[:, :, 1:2] * TC + meta_all[:, :, 2:]
    dest_slot = jnp.sum(jnp.where(pick[..., None], dest[:, None, :, :], 0.0), axis=2)
    valid = jnp.any(pick, axis=2)
    dest_slot = jnp.where(valid[..., None], dest_slot, -1.0).reshape(slots_total * TAP)
    group_coarse = col_devices * TC
    onehot = (
        dest_slot[:, None] == jnp.arange(group_coarse, dtype=jnp.float32)[None, :]
    ).astype(jnp.float32)
    coarse_part = jnp.einsum(
        "ec,ef->cf", onehot, incoming.reshape(slots_total * TAP, tile_len), precision=highest
    )
    coarse = lax.psum_scatter(
        coarse_part.reshape(col_devices, TC, tile_len), "col", scatter_dimension=0, tiled=True
    )
    return coarse


def solution(mesh):
    placed = (
        P("row", "col", None, None),
        P("row", "col", None),
        P("row", "col", None),
        P("row", "col", None, None),
        P("row", "col"),
        P(("row", "col"), None, None),
        P(("row", "col"), None),
        P(("row", "col"), None),
        P(("row", "col"), None, None),
    )
    return jax.shard_map(
        on_device,
        mesh=mesh,
        in_specs=placed,
        out_specs=P(("row", "col"), None, None),
        check_vma=False,
    )
```

time: 464 us -> 480 us (1.034)
  blocking collectives: 0 us -> 73.1 us
  starting transfers between devices: 58.5 us -> 7.21 us
  Pallas kernels: 72.4 us -> 44 us
  waiting for transfers between devices: 190 us -> 217 us
  local copies, waits for them, and re-layouts: 106 us -> 89.5 us
  other arithmetic: 9.01 us -> 23.9 us
    all_gather x0 -> x1, blocking collectives: none -> 73.1 us  [on_device(): meta_all = lax.all_gather(meta_local, 'row', axis=0, tiled=False)]
    reduce_scatter x2, waiting for transfers between devices: 91.8 us -> 159 us  [the longest x1 120 us: on_device(): lax.psum_scatter(partial_value.reshape(group_rows, TAP, HALF, LANES), 'co...]
    all_to_all x1, waiting for transfers between devices: 54 us -> 0.01 us  [on_device(): lax.all_to_all(outgoing, 'row', split_axis=0, concat_axis=0, tiled=True)]
    all_to_all x1 -> x0, starting transfers between devices: 51.3 us -> none  [on_device(): lax.all_to_all(meta_send, 'row', split_axis=0, concat_axis=0, tiled=True)]
    pallas_call x1, Pallas kernels: 72.4 us -> 44 us  [ap_partial(): pl.pallas_call(ap_kernel, out_shape=jax.ShapeDtypeStruct((out_rows * TAP,...]
    transpose x1, local copies, waits for them, and re-layouts: 6.6 us -> 24.8 us  [block_diagonal(): return both.transpose(0, 2, 1, 3).reshape(cols, 2 * BLOCK, branches * LANES)]
    transpose x0 -> x1, other arithmetic: none -> 18.1 us  [block_diagonal(): return both.transpose(0, 2, 1, 3).reshape(cols, 2 * BLOCK, branches * LANES)]
    all_gather x1, waiting for transfers between devices: 43.9 us -> 57.2 us  [on_device(): panel = lax.all_gather(p_vals, 'row', axis=0, tiled=True)]
  transfers between devices with their start and end apart: 5 -> 4, of which waited for: 4 -> 3; matrix products, arithmetic and copies ran while one was open for 9% -> 2% of each run, Pallas kernels for 0% -> 0%
where the time goes in v2:
time: 480 us; the launch traced here: 479 us
  waiting for transfers between devices  217 us (45%)
  local copies, waits for them, and re-layouts  89.5 us (19%)
  blocking collectives  73.1 us (15%)
  Pallas kernels  44 us (9%)
  other arithmetic  23.9 us (5%)
  between operations  13.9 us (3%)
  matrix products  9.53 us (2%)
  starting transfers between devices  7.21 us (2%)
    reduce_scatter x1, waiting for transfers between devices, on_device(): lax.psum_scatter(partial_value.reshape(group_rows, TAP, HALF, LANES), 'co...  120 us
    all_gather x1, blocking collectives, on_device(): meta_all = lax.all_gather(meta_local, 'row', axis=0, tiled=False)  73.1 us
    all_gather x1, waiting for transfers between devices, on_device(): panel = lax.all_gather(p_vals, 'row', axis=0, tiled=True)  57.2 us
    pallas_call x1, Pallas kernels, ap_partial(): pl.pallas_call(ap_kernel, out_shape=jax.ShapeDtypeStruct((out_rows * TAP,...  44 us
    reduce_scatter x1, waiting for transfers between devices, on_device(): lax.psum_scatter(coarse_part.reshape(col_devices, TC, tile_len), 'col', s...  39.9 us
    transpose x1, local copies, waits for them, and re-layouts, block_diagonal(): return both.transpose(0, 2, 1, 3).reshape(cols, 2 * BLOCK, branches * LANES)  24.8 us
    reshape x1, local copies, waits for them, and re-layouts, block_diagonal(): return both.transpose(0, 2, 1, 3).reshape(cols, 2 * BLOCK, branches * LANES)  24.7 us
    transpose x1, other arithmetic, block_diagonal(): return both.transpose(0, 2, 1, 3).reshape(cols, 2 * BLOCK, branches * LANES)  18.1 us
  transfers between devices with their start and end apart: 4, of which 3 were waited for; matrix products, arithmetic and copies ran while one was open for 2% of the time, Pallas kernels for 0%

profile of v2, /device:TPU:0, one launch (start us, length us, event | category | flops | bytes accessed | tf_op | source)
XLA Modules:
  0.0 478.6 jit_solution(219791419288647384)
XLA Ops:
  6.5 0.0 all-gather.2.cloned.1.call-start
  6.5 0.7 all-gather.2.cloned.1.call-update
  7.3 0.0 reduce-scatter.3.cloned.1.call-start
  7.3 0.0 copy-start.2
  7.3 7.6 %copy.84 = f32[56,8,32,128]{3,2,1,0:T(8,128)} copy(f32[56,8,32,128]{3,1,2,0:T(8,128)} %bitcast.46) | data formatting | bytes 14680064
  14.9 0.0 copy-done.2
  14.9 0.7 reshape.184.slots_ref
  16.2 57.2 %all-gather.2.cloned.1.call-done = f32[128,3,4096]{2,0,1:T(8,128)} async-done(((f32[8,3,4096]{2,0,1:T(8,128)}), f32[128,3,4096]{2,0,1:T(8,128)}) %all-gather.2.cloned.1.call-update) | async-done | bytes 6291472 | tf_op jit(solution)/shard_map/all_gather | solution.py:103
  73.5 6.5 %copy.67 = f32[128,3,4096]{0,2,1:T(8,128)} copy(f32[128,3,4096]{2,0,1:T(8,128)} %all-gather.2.cloned.1.call-done) | data formatting | bytes 12582912 | tf_op jit(solution)/shard_map/all_gather | solution.py:103
  80.0 18.1 %fusion = f32[128,128,3,128]{0,3,1,2:T(8,128)} fusion(f32[128,3,64,64]{0,3,2,1:T(8,128)} %bitcast.45), kind=kLoop, calls=%fused_computation.2 | loop fusion | flops 31457280 | bytes 31457280 | tf_op jit(solution)/shard_map/transpose | solution.py:82
  98.0 24.8 %copy.68 = f32[128,128,3,128]{1,3,2,0:T(8,128)} copy(f32[128,128,3,128]{0,3,1,2:T(8,128)} %fusion) | data formatting | bytes 50331648 | tf_op jit(solution)/shard_map/transpose | solution.py:82
  122.8 24.7 %copy.69.p_ref = f32[128,128,384]{2,1,0:T(8,128)} copy(f32[128,128,384]{1,2,0:T(8,128)} %bitcast.42) | data formatting | bytes 50331648 | tf_op jit(solution)/shard_map/reshape | solution.py:82
  147.5 44.0 %shard_map.91 = f32[384,32,128]{2,1,0:T(8,128)} custom-call(s32[448]{0:T(512)} %bitcast.49, s32[448]{0:T(512)} %bitcast.50, s32[1344]{0:T(1024)} %reshape.184.slots_ref, s32[1]{0:T(128)} %bitcast.41.cnt_ref, f32[448,32,128]{2,1,0:T(8,128)} %bitcast.43, f32[128,128,384]{2,1,0:T(8,128)} %copy.69.p_ref), custom_call_target="tpu_custom_call" | custom-call | tf_op jit(solution)/shard_map/pallas_call | solution.py:65
  191.5 0.0 reduce-scatter.3.cloned.1.call-update
  191.5 1.0 copy-done
  192.5 0.3 reshape.191
  192.8 0.1 copy.60
  192.9 0.1 reshape.181
  193.0 0.2 convert_reduce_fusion
  193.2 0.1 fusion.8
  193.3 0.1 select_reduce_fusion.1
  193.4 119.5 %reduce-scatter.3.cloned.1.call-done = f32[8,6,32,128]{3,2,1,0:T(8,128)} async-done(((f32[64,6,32,128]{3,2,1,0:T(8,128)}), f32[8,6,32,128]{3,2,1,0:T(8,128)}) %reduce-scatter.3.cloned.1.call-update) | async-done | bytes 786448 | tf_op jit(solution)/shard_map/reduce_scatter | solution.py:110
  313.0 1.5 reshape.190
  314.4 5.6 %convolution_bitcast_fusion = f32[8,3,6,64,64]{3,4,1,2,0:T(8,128)} fusion(f32[8,6,64,64]{3,2,1,0:T(8,128)S(1)} %reshape.190, f32[8,3,64,64]{3,2,0,1:T(8,128)S(1)} %reshape.191), kind=kOutput, calls=%fused_computation.5 | convolution fusion | flops 452984832 | bytes 3538944 | tf_op jit(solution)/shard_map/isjk,iqjl->isqkl/dot_general | solution.py:116
  320.0 6.1 %copy.81 = f32[8,3,6,64,64]{4,3,2,1,0:T(8,128)} copy(f32[8,3,6,64,64]{3,4,1,2,0:T(8,128)} %convolution_bitcast_fusion) | data formatting | bytes 4718592 | tf_op jit(solution)/shard_map/reshape | solution.py:117
  326.1 5.3 %reshape.205 = f32[24,6,4096]{2,1,0:T(8,128)} reshape(f32[8,3,6,64,64]{4,3,2,1,0:T(8,128)} %copy.81) | data formatting | bytes 4718592 | tf_op jit(solution)/shard_map/reshape | solution.py:117
  331.4 2.2 concatenate.35
  333.7 2.8 gather_fusion
  336.5 4.9 %broadcast_select_fusion = f32[32,6,4096]{2,1,0:T(8,128)} fusion(f32[32,6,4096]{2,1,0:T(8,128)} %gather_fusion, pred[32]{0:T(512)(128)(4,1)S(1)} %compare_and_fusion), kind=kLoop, calls=%fused_computation.6 | loop fusion | flops 786432 | bytes 6291488 | tf_op jit(solution)/shard_map/jit(_take)/select_n | solution.py:129
  341.4 7.1 %all-to-all-start = ((f32[32,6,4096]{2,1,0:T(8,128)}), f32[32,6,4096]{2,1,0:T(8,128)}, u32[]{:S(2)}, u32[]{:S(2)}) async-start(f32[32,6,4096]{2,1,0:T(8,128)} %broadcast_select_fusion), calls=%async_computation.1 | async-start | bytes 8388608 | tf_op jit(solution)/shard_map/all_to_all | solution.py:130
  348.5 0.0 reduce-scatter.5.cloned.1.call-start
  348.6 0.1 concatenate.28
  348.7 0.1 copy.62
  348.8 0.1 concatenate.30
  348.9 0.1 copy.61
  349.0 0.1 concatenate.29
  349.1 73.1 %all_gather.7 = f32[16,24,8]{1,2,0:T(8,128)S(1)} all-gather(f32[1,24,8]{1,2,0:T(8,128)S(1)} %add_convert_fusion), channel_id=1, replica_groups=mesh['row'=16,'col'=8] {'row'}, dimensions={0}, use_global_device_ids=true | all-gather | bytes 13056 | tf_op jit(solution)/shard_map/all_gather | solution.py:101
  422.2 0.2 reduce_window_sum.11
  422.4 0.1 fusion.11
  422.6 0.1 select_reduce_fusion
  422.7 0.1 copy.65
  422.8 0.1 select_n.57
  422.9 0.0 all-to-all-done
  422.9 3.0 reshape.204
  426.0 3.9 fusion.3
  429.9 0.0 reduce-scatter.5.cloned.1.call-update
  429.9 39.9 %reduce-scatter.5.cloned.1.call-done = f32[1,27,4096]{2,1,0:T(8,128)} async-done(((f32[8,27,4096]{2,1,0:T(8,128)}), f32[1,27,4096]{2,1,0:T(8,128)}) %reduce-scatter.5.cloned.1.call-update) | async-done | bytes 442384 | tf_op jit(solution)/shard_map/reduce_scatter | solution.py:149
  469.8 2.3 copy.74
  (20 shorter events, 0.2 us)
Async XLA Ops:
  6.5 66.9 %all-gather.2.cloned.1.call-start = ((), (), s32[]{:S(2)}) async-start(), calls=%async_computation.3 | async-start | bytes 6684672 | tf_op jit(solution)/shard_map/all_gather | solution.py:103
  7.3 305.7 %reduce-scatter.3.cloned.1.call-start = ((), (), s32[]{:S(2)}) async-start(), calls=%async_computation.4 | async-start | bytes 7077888 | tf_op jit(solution)/shard_map/reduce_scatter | solution.py:110
  7.3 7.6 %copy-start.2 = (s32[1,1,3,448]{3,1,2,0:T(1,128)S(1)}, s32[1,1,3,448]{3,1,2,0:T(1,128)}, u32[]{:S(2)}) copy-start(s32[1,1,3,448]{3,1,2,0:T(1,128)} %param.12) | copy-start | bytes 16132
  191.5 1.0 copy-start
  191.5 1.3 copy-start.3
  341.4 7.3 %copy-start.1 = (s32[8,3,6]{2,0,1:T(8,128)S(1)}, s32[8,3,6]{2,0,1:T(8,128)}, u32[]{:S(2)}) copy-start(s32[8,3,6]{2,0,1:T(8,128)} %param.17) | copy-start | bytes 1732
  341.4 7.5 %copy-start.4 = (s32[8,3]{0,1:T(4,128)S(1)}, s32[8,3]{0,1:T(4,128)}, u32[]{:S(2)}) copy-start(s32[8,3]{0,1:T(4,128)} %param.16) | copy-start | bytes 292
  341.4 81.5 %all-to-all-start = ((f32[32,6,4096]{2,1,0:T(8,128)}), f32[32,6,4096]{2,1,0:T(8,128)}, u32[]{:S(2)}, u32[]{:S(2)}) async-start(f32[32,6,4096]{2,1,0:T(8,128)} %broadcast_select_fusion), calls=%async_computation.1 | async-start | bytes 8388608 | tf_op jit(solution)/shard_map/all_to_all | solution.py:130
  348.5 121.3 %reduce-scatter.5.cloned.1.call-start = ((), (), s32[]{:S(2)}) async-start(), calls=%async_computation.5 | async-start | bytes 4718592 | tf_op jit(solution)/shard_map/reduce_scatter | solution.py:149
Sparse Core Ops, SparseCore 0:
  9.5 63.8 all-gather.1
  191.6 121.2 reduce-scatter.2
  430.0 39.7 reduce-scatter.4

commit v3 on v2

--- a/solution.py
+++ b/solution.py
@@ -15,10 +15,10 @@
 chunk = 32
 
 
-def ap_kernel(rows_ref, cols_ref, slots_ref, cnt_ref, a_ref, p_ref, o_ref):
+def ap_kernel(rows_ref, cols_ref, slots_ref, cnt_ref, a_ref, p_ref, meta_ref, o_ref):
     c = pl.program_id(0)
     capacity = rows_ref.shape[0]
-    branches = p_ref.shape[2] // LANES
+    branches = p_ref.shape[1]
 
     @pl.when(c == 0)
     def _():
@@ -31,21 +31,22 @@
 
         @pl.when(t < count)
         def _():
+            a = a_ref[u]
             col = cols_ref[t]
             row = rows_ref[t]
-            prod = jnp.dot(
-                a_ref[u], p_ref[col], preferred_element_type=jnp.float32, precision=highest
-            )
             for s in range(branches):
+                prod = jnp.dot(
+                    a, p_ref[col, s], preferred_element_type=jnp.float32, precision=highest
+                )
                 idx = row * TAP + slots_ref[s * capacity + t]
-                o_ref[idx] += prod[:, s * LANES:(s + 1) * LANES]
+                o_ref[idx] += prod
 
         return carry
 
     lax.fori_loop(0, chunk, body, 0)
 
 
-def ap_partial(tiles, rows, cols, slots, count, pdiag, out_rows):
+def ap_partial(tiles, rows, cols, slots, count, panel, meta, out_rows):
     capacity = tiles.shape[0]
     chunks = capacity // chunk
 
@@ -57,29 +58,20 @@
         num_scalar_prefetch=4,
         grid=(chunks,),
         in_specs=[
-            pl.BlockSpec((chunk, HALF, LANES), a_map),
+            pl.BlockSpec((chunk, BLOCK, BLOCK), a_map),
             pl.BlockSpec(memory_space=pltpu.VMEM),
+            pl.BlockSpec(memory_space=pltpu.SMEM),
         ],
         out_specs=pl.BlockSpec(memory_space=pltpu.VMEM),
     )
     return pl.pallas_call(
         ap_kernel,
-        out_shape=jax.ShapeDtypeStruct((out_rows * TAP, HALF, LANES), jnp.float32),
+        out_shape=jax.ShapeDtypeStruct((out_rows * TAP, BLOCK, BLOCK), jnp.float32),
         grid_spec=grid_spec,
         compiler_params=pltpu.CompilerParams(
-            dimension_semantics=("arbitrary",), vmem_limit_bytes=60 * 1024 * 1024
+            dimension_semantics=("arbitrary",), vmem_limit_bytes=56 * 1024 * 1024
         ),
-    )(rows, cols, slots, count, tiles, pdiag)
-
-
-def block_diagonal(panel):
-    cols, branches = panel.shape[:2]
-    p4 = panel.reshape(cols, branches, BLOCK, BLOCK)
-    zero = jnp.zeros_like(p4)
-    top = jnp.concatenate([p4, zero], axis=3)
-    bottom = jnp.concatenate([zero, p4], axis=3)
-    both = jnp.concatenate([top, bottom], axis=2)
-    return both.transpose(0, 2, 1, 3).reshape(cols, 2 * BLOCK, branches * LANES)
+    )(rows, cols, slots, count, tiles, panel, meta)
 
 
 def on_device(a_vals, a_row, a_col, a_slot, a_count, p_vals, p_owner, p_sub, ap_cslot):
@@ -101,14 +93,14 @@
     meta_all = lax.all_gather(meta_local, "row", axis=0, tiled=False)
 
     panel = lax.all_gather(p_vals, "row", axis=0, tiled=True)
-    pdiag = block_diagonal(panel)
-    matrix_tiles = a_vals.reshape(capacity, HALF, LANES)
+    panel_tiles = panel.reshape(rows_dev * row_devices, branches, BLOCK, BLOCK)
     partial_value = ap_partial(
-        matrix_tiles, a_row.reshape(capacity), a_col.reshape(capacity),
-        a_slot.reshape(branches * capacity), a_count.reshape(1), pdiag, group_rows
+        a_vals.reshape(capacity, BLOCK, BLOCK), a_row.reshape(capacity), a_col.reshape(capacity),
+        a_slot.reshape(branches * capacity), a_count.reshape(1), panel_tiles,
+        meta_all.reshape(row_devices * item_count, TAP + 2), group_rows
     )
     ap_rows = lax.psum_scatter(
-        partial_value.reshape(group_rows, TAP, HALF, LANES), "col", scatter_dimension=0, tiled=True
+        partial_value.reshape(group_rows, TAP, tile_len), "col", scatter_dimension=0, tiled=True
     )
 
     p4 = p_vals.reshape(rows_dev, branches, BLOCK, BLOCK)

time: 480 us -> 430 us (0.90)
  Pallas kernels: 44 us -> 119 us
  waiting for transfers between devices: 217 us -> 167 us
  blocking collectives: 73.1 us -> 25.2 us
  other arithmetic: 23.9 us -> 5.79 us
  local copies, waits for them, and re-layouts: 89.5 us -> 82 us
    pallas_call x1, Pallas kernels: 44 us -> 119 us  [ap_partial(): pl.pallas_call(ap_kernel, out_shape=jax.ShapeDtypeStruct((out_rows * TAP,...]
    reduce_scatter x1, waiting for transfers between devices: 120 us -> 50.7 us  [on_device(): lax.psum_scatter(partial_value.reshape(group_rows, TAP, tile_len), 'col',...]
    all_to_all x1, waiting for transfers between devices: 0.01 us -> 53.4 us  [on_device(): lax.all_to_all(outgoing, 'row', split_axis=0, concat_axis=0, tiled=True)]
    all_gather x1, blocking collectives: 73.1 us -> 25.2 us  [on_device(): meta_all = lax.all_gather(meta_local, 'row', axis=0, tiled=False)]
    all_gather x1, waiting for transfers between devices: 57.2 us -> 15.5 us  [on_device(): panel = lax.all_gather(p_vals, 'row', axis=0, tiled=True)]
    transpose x1 -> x0, local copies, waits for them, and re-layouts: 24.8 us -> none  [block_diagonal(): return both.transpose(0, 2, 1, 3).reshape(cols, 2 * BLOCK, branches * LANES)]
    transpose x1 -> x0, other arithmetic: 18.1 us -> none  [block_diagonal(): return both.transpose(0, 2, 1, 3).reshape(cols, 2 * BLOCK, branches * LANES)]
    reshape x1 -> x3, local copies, waits for them, and re-layouts: 24.7 us -> 37.3 us  [the longest x1 12.7 us: on_device(): panel_tiles = panel.reshape(rows_dev * row_devices, branches, BLOCK, BLOCK)]
  transfers between devices with their start and end apart: 4 -> 4, of which waited for: 3 -> 4; matrix products, arithmetic and copies ran while one was open for 2% -> 6% of each run, Pallas kernels for 0% -> 0%
where the time goes in v3:
time: 430 us; the launch traced here: 429 us
  waiting for transfers between devices  167 us (39%)
  Pallas kernels  119 us (28%)
  local copies, waits for them, and re-layouts  82 us (19%)
  blocking collectives  25.2 us (6%)
  between operations  13.9 us (3%)
  matrix products  9.53 us (2%)
  starting transfers between devices  7.27 us (2%)
  other arithmetic  5.79 us (1%)
    pallas_call x1, Pallas kernels, ap_partial(): pl.pallas_call(ap_kernel, out_shape=jax.ShapeDtypeStruct((out_rows * TAP,...  119 us
    all_to_all x1, waiting for transfers between devices, on_device(): lax.all_to_all(outgoing, 'row', split_axis=0, concat_axis=0, tiled=True)  53.4 us
    reduce_scatter x1, waiting for transfers between devices, on_device(): lax.psum_scatter(partial_value.reshape(group_rows, TAP, tile_len), 'col',...  50.7 us
    reduce_scatter x1, waiting for transfers between devices, on_device(): lax.psum_scatter(coarse_part.reshape(col_devices, TC, tile_len), 'col', s...  46.2 us
    all_gather x1, blocking collectives, on_device(): meta_all = lax.all_gather(meta_local, 'row', axis=0, tiled=False)  25.2 us
    all_gather x1, waiting for transfers between devices, on_device(): panel = lax.all_gather(p_vals, 'row', axis=0, tiled=True)  15.5 us
    reshape x1, local copies, waits for them, and re-layouts, on_device(): panel_tiles = panel.reshape(rows_dev * row_devices, branches, BLOCK, BLOCK)  12.7 us
    reshape x1, local copies, waits for them, and re-layouts, on_device(): partial_value.reshape(group_rows, TAP, tile_len)  12.7 us
  transfers between devices with their start and end apart: 4, of which 4 were waited for; matrix products, arithmetic and copies ran while one was open for 6% of the time, Pallas kernels for 0%

profile of v3, /device:TPU:0, one launch (start us, length us, event | category | flops | bytes accessed | tf_op | source)
XLA Modules:
  0.0 429.3 jit_solution(6278763731185864594)
XLA Ops:
  6.5 0.0 all-gather.2.cloned.1.call-start
  6.5 0.7 all-gather.2.cloned.1.call-update
  7.3 0.0 reduce-scatter.3.cloned.1.call-start
  7.3 0.8 copy.69
  8.1 0.1 concatenate.19
  8.1 0.8 copy.71
  9.0 0.1 concatenate.21
  9.1 0.8 copy.70
  9.8 0.1 concatenate.20
  9.9 25.2 %all_gather.7 = f32[16,24,8]{1,2,0:T(8,128)S(1)} all-gather(f32[1,24,8]{1,2,0:T(8,128)S(1)} %add_convert_fusion), channel_id=1, replica_groups=mesh['row'=16,'col'=8] {'row'}, dimensions={0}, use_global_device_ids=true | all-gather | bytes 13056 | tf_op jit(solution)/shard_map/all_gather | solution.py:93
  35.1 0.8 copy.78
  35.9 9.0 %copy.76 = f32[1,1,448,4096]{2,3,1,0:T(8,128)} copy(f32[1,1,448,4096]{3,2,1,0:T(8,128)} %param.9) | data formatting | bytes 14680064 | tf_op args[0]
  44.9 11.9 %copy.79.a_ref = f32[448,64,64]{2,1,0:T(8,128)} copy(f32[448,64,64]{0,2,1:T(8,128)} %bitcast.34) | data formatting | bytes 14680064 | tf_op jit(solution)/shard_map/reshape | solution.py:98
  56.8 0.0 copy-done.1
  56.8 0.7 reshape.184.slots_ref
  58.2 15.5 %all-gather.2.cloned.1.call-done = f32[128,3,4096]{2,0,1:T(8,128)} async-done(((f32[8,3,4096]{2,0,1:T(8,128)}), f32[128,3,4096]{2,0,1:T(8,128)}) %all-gather.2.cloned.1.call-update) | async-done | bytes 6291472 | tf_op jit(solution)/shard_map/all_gather | solution.py:95
  73.6 6.6 %copy.77 = f32[128,3,4096]{0,2,1:T(8,128)} copy(f32[128,3,4096]{2,0,1:T(8,128)} %all-gather.2.cloned.1.call-done) | data formatting | bytes 12582912 | tf_op jit(solution)/shard_map/all_gather | solution.py:95
  80.2 12.7 %copy.80.p_ref = f32[128,3,64,64]{3,2,1,0:T(8,128)} copy(f32[128,3,64,64]{0,3,2,1:T(8,128)} %bitcast.35) | data formatting | bytes 12582912 | tf_op jit(solution)/shard_map/reshape | solution.py:96
  93.0 119.1 %shard_map.91 = f32[384,64,64]{2,1,0:T(8,128)} custom-call(s32[448]{0:T(512)} %bitcast.39, s32[448]{0:T(512)} %bitcast.40, s32[1344]{0:T(1024)} %reshape.184.slots_ref, s32[1]{0:T(128)} %bitcast.33.cnt_ref, f32[448,64,64]{2,1,0:T(8,128)} %copy.79.a_ref, f32[128,3,64,64]{3,2,1,0:T(8,128)} %copy.80.p_ref, f32[384,8]{1,0:T(8,128)} %bitcast.36), custom_call_target="tpu_custom_call" | custom-call | tf_op jit(solution)/shard_map/pallas_call | solution.py:67
  212.1 12.7 %reshape.189 = f32[64,6,4096]{2,1,0:T(8,128)} reshape(f32[384,64,64]{2,1,0:T(8,128)} %shard_map.91) | data formatting | bytes 12582912 | tf_op jit(solution)/shard_map/reshape | solution.py:103
  224.7 0.0 reduce-scatter.3.cloned.1.call-update
  224.8 0.1 reshape.181
  224.8 0.9 copy-done
  225.7 0.3 reshape.191
  226.0 0.2 convert_reduce_fusion
  226.2 0.1 fusion.7
  226.3 0.1 select_reduce_fusion.1
  226.5 50.7 %reduce-scatter.3.cloned.1.call-done = f32[8,6,4096]{2,1,0:T(8,128)} async-done(((f32[64,6,4096]{2,1,0:T(8,128)}), f32[8,6,4096]{2,1,0:T(8,128)}) %reduce-scatter.3.cloned.1.call-update) | async-done | bytes 786448 | tf_op jit(solution)/shard_map/reduce_scatter | solution.py:102
  277.1 1.8 reshape.205
  279.0 5.6 %convolution_bitcast_fusion = f32[8,3,6,64,64]{3,4,1,2,0:T(8,128)} fusion(f32[8,6,64,64]{3,2,1,0:T(8,128)S(1)} %reshape.205, f32[8,3,64,64]{3,2,0,1:T(8,128)S(1)} %reshape.191), kind=kOutput, calls=%fused_computation.1 | convolution fusion | flops 452984832 | bytes 3538944 | tf_op jit(solution)/shard_map/isjk,iqjl->isqkl/dot_general | solution.py:108
  284.6 6.1 %copy.95 = f32[8,3,6,64,64]{4,3,2,1,0:T(8,128)} copy(f32[8,3,6,64,64]{3,4,1,2,0:T(8,128)} %convolution_bitcast_fusion) | data formatting | bytes 4718592 | tf_op jit(solution)/shard_map/reshape | solution.py:109
  290.6 5.3 %reshape.206 = f32[24,6,4096]{2,1,0:T(8,128)} reshape(f32[8,3,6,64,64]{4,3,2,1,0:T(8,128)} %copy.95) | data formatting | bytes 4718592 | tf_op jit(solution)/shard_map/reshape | solution.py:109
  296.0 2.2 concatenate.23
  298.2 2.8 gather_fusion
  301.0 4.9 %broadcast_select_fusion = f32[32,6,4096]{2,1,0:T(8,128)} fusion(f32[32,6,4096]{2,1,0:T(8,128)} %gather_fusion, pred[32]{0:T(512)(128)(4,1)S(1)} %compare_and_fusion), kind=kLoop, calls=%fused_computation.2 | loop fusion | flops 786432 | bytes 6291488 | tf_op jit(solution)/shard_map/jit(_take)/select_n | solution.py:121
  305.9 7.0 %all-to-all-start = ((f32[32,6,4096]{2,1,0:T(8,128)}), f32[32,6,4096]{2,1,0:T(8,128)}, u32[]{:S(2)}, u32[]{:S(2)}) async-start(f32[32,6,4096]{2,1,0:T(8,128)} %broadcast_select_fusion), calls=%async_computation.1 | async-start | bytes 8388608 | tf_op jit(solution)/shard_map/all_to_all | solution.py:122
  312.9 0.2 reduce-scatter.5.cloned.1.call-start
  313.2 0.2 reduce_window_sum.11
  313.4 0.1 fusion.10
  313.5 0.1 select_reduce_fusion
  313.7 0.1 copy.74
  313.8 0.1 select_n.57
  313.9 53.4 %all-to-all-done = f32[32,6,4096]{2,1,0:T(8,128)} async-done(((f32[32,6,4096]{2,1,0:T(8,128)}), f32[32,6,4096]{2,1,0:T(8,128)}, u32[]{:S(2)}, u32[]{:S(2)}) %all-to-all-start) | async-done | bytes 3145760 | tf_op jit(solution)/shard_map/all_to_all | solution.py:122
  367.3 3.0 reshape.204
  370.4 3.9 fusion.2
  374.3 0.0 reduce-scatter.5.cloned.1.call-update
  374.3 46.2 %reduce-scatter.5.cloned.1.call-done = f32[1,27,4096]{2,1,0:T(8,128)} async-done(((f32[8,27,4096]{2,1,0:T(8,128)}), f32[1,27,4096]{2,1,0:T(8,128)}) %reduce-scatter.5.cloned.1.call-update) | async-done | bytes 442384 | tf_op jit(solution)/shard_map/reduce_scatter | solution.py:141
  420.5 2.3 copy.86
  (15 shorter events, 0.1 us)
Async XLA Ops:
  6.5 67.1 %all-gather.2.cloned.1.call-start = ((), (), s32[]{:S(2)}) async-start(), calls=%async_computation.3 | async-start | bytes 6684672 | tf_op jit(solution)/shard_map/all_gather | solution.py:95
  7.3 269.9 %reduce-scatter.3.cloned.1.call-start = ((), (), s32[]{:S(2)}) async-start(), calls=%async_computation.4 | async-start | bytes 9437184 | tf_op jit(solution)/shard_map/reduce_scatter | solution.py:102
  44.9 11.9 %copy-start.1 = (s32[1,1,3,448]{3,1,2,0:T(1,128)S(1)}, s32[1,1,3,448]{3,1,2,0:T(1,128)}, u32[]{:S(2)}) copy-start(s32[1,1,3,448]{3,1,2,0:T(1,128)} %param.12) | copy-start | bytes 16132
  224.7 1.0 copy-start
  305.9 61.4 %all-to-all-start = ((f32[32,6,4096]{2,1,0:T(8,128)}), f32[32,6,4096]{2,1,0:T(8,128)}, u32[]{:S(2)}, u32[]{:S(2)}) async-start(f32[32,6,4096]{2,1,0:T(8,128)} %broadcast_select_fusion), calls=%async_computation.1 | async-start | bytes 8388608 | tf_op jit(solution)/shard_map/all_to_all | solution.py:122
  312.9 107.6 %reduce-scatter.5.cloned.1.call-start = ((), (), s32[]{:S(2)}) async-start(), calls=%async_computation.5 | async-start | bytes 4718592 | tf_op jit(solution)/shard_map/reduce_scatter | solution.py:141
Sparse Core Ops, SparseCore 0:
  9.5 64.0 all-gather.1
  224.9 52.1 reduce-scatter.2
  374.4 46.0 reduce-scatter.4

commit v4 on v3

--- a/solution.py
+++ b/solution.py
@@ -28,22 +28,21 @@
 
     def body(u, carry):
         t = c * chunk + u
-
-        @pl.when(t < count)
-        def _():
-            a = a_ref[u]
-            col = cols_ref[t]
-            row = rows_ref[t]
-            for s in range(branches):
-                prod = jnp.dot(
-                    a, p_ref[col, s], preferred_element_type=jnp.float32, precision=highest
-                )
-                idx = row * TAP + slots_ref[s * capacity + t]
-                o_ref[idx] += prod
-
+        live = t < count
+        a = a_ref[u]
+        col = cols_ref[t]
+        row = rows_ref[t]
+        for s in range(branches):
+            prod = jnp.dot(
+                a, p_ref[col, s], preferred_element_type=jnp.float32, precision=highest
+            )
+            idx = row * TAP + slots_ref[s * capacity + t]
+            o_ref[idx] += jnp.where(live, prod, 0.0)
         return carry
 
-    lax.fori_loop(0, chunk, body, 0)
+    @pl.when(c * chunk < count)
+    def _():
+        lax.fori_loop(0, chunk, body, 0, unroll=True)
 
 
 def ap_partial(tiles, rows, cols, slots, count, panel, meta, out_rows):

time: 430 us -> 360 us (0.84)
  Pallas kernels: 119 us -> 48 us
    pallas_call x1, Pallas kernels: 119 us -> 48 us  [ap_partial(): pl.pallas_call(ap_kernel, out_shape=jax.ShapeDtypeStruct((out_rows * TAP,...]
  transfers between devices with their start and end apart: 4 -> 4, of which waited for: 4 -> 4; matrix products, arithmetic and copies ran while one was open for 6% -> 7% of each run, Pallas kernels for 0% -> 0%
where the time goes in v4:
time: 360 us; the launch traced here: 358 us
  waiting for transfers between devices  167 us (46%)
  local copies, waits for them, and re-layouts  82 us (23%)
  Pallas kernels  48 us (13%)
  blocking collectives  25.2 us (7%)
  between operations  13.9 us (4%)
  matrix products  9.53 us (3%)
  starting transfers between devices  7.08 us (2%)
  other arithmetic  5.79 us (2%)
    all_to_all x1, waiting for transfers between devices, on_device(): lax.all_to_all(outgoing, 'row', split_axis=0, concat_axis=0, tiled=True)  53.6 us
    reduce_scatter x1, waiting for transfers between devices, on_device(): lax.psum_scatter(partial_value.reshape(group_rows, TAP, tile_len), 'col',...  50.5 us
    pallas_call x1, Pallas kernels, ap_partial(): pl.pallas_call(ap_kernel, out_shape=jax.ShapeDtypeStruct((out_rows * TAP,...  48 us
    reduce_scatter x1, waiting for transfers between devices, on_device(): lax.psum_scatter(coarse_part.reshape(col_devices, TC, tile_len), 'col', s...  46.5 us
    all_gather x1, blocking collectives, on_device(): meta_all = lax.all_gather(meta_local, 'row', axis=0, tiled=False)  25.2 us
    all_gather x1, waiting for transfers between devices, on_device(): panel = lax.all_gather(p_vals, 'row', axis=0, tiled=True)  15.5 us
    reshape x1, local copies, waits for them, and re-layouts, on_device(): panel_tiles = panel.reshape(rows_dev * row_devices, branches, BLOCK, BLOCK)  12.7 us
    reshape x1, local copies, waits for them, and re-layouts, on_device(): partial_value.reshape(group_rows, TAP, tile_len)  12.7 us
  transfers between devices with their start and end apart: 4, of which 4 were waited for; matrix products, arithmetic and copies ran while one was open for 7% of the time, Pallas kernels for 0%

profile of v4, /device:TPU:0, one launch (start us, length us, event | category | flops | bytes accessed | tf_op | source)
XLA Modules:
  0.0 358.3 jit_solution(14144202457889175759)
XLA Ops:
  6.5 0.0 all-gather.2.cloned.1.call-start
  6.5 0.7 all-gather.2.cloned.1.call-update
  7.3 0.0 reduce-scatter.3.cloned.1.call-start
  7.3 0.8 copy.69
  8.1 0.1 concatenate.19
  8.1 0.8 copy.71
  9.0 0.1 concatenate.21
  9.1 0.8 copy.70
  9.8 0.1 concatenate.20
  9.9 25.2 %all_gather.7 = f32[16,24,8]{1,2,0:T(8,128)S(1)} all-gather(f32[1,24,8]{1,2,0:T(8,128)S(1)} %add_convert_fusion), channel_id=1, replica_groups=mesh['row'=16,'col'=8] {'row'}, dimensions={0}, use_global_device_ids=true | all-gather | bytes 13056 | tf_op jit(solution)/shard_map/all_gather | solution.py:92
  35.1 0.8 copy.78
  35.9 9.0 %copy.76 = f32[1,1,448,4096]{2,3,1,0:T(8,128)} copy(f32[1,1,448,4096]{3,2,1,0:T(8,128)} %param.9) | data formatting | bytes 14680064 | tf_op args[0]
  44.9 11.9 %copy.79.a_ref = f32[448,64,64]{2,1,0:T(8,128)} copy(f32[448,64,64]{0,2,1:T(8,128)} %bitcast.34) | data formatting | bytes 14680064 | tf_op jit(solution)/shard_map/reshape | solution.py:97
  56.8 0.0 copy-done.1
  56.8 0.7 reshape.184.slots_ref
  58.2 15.5 %all-gather.2.cloned.1.call-done = f32[128,3,4096]{2,0,1:T(8,128)} async-done(((f32[8,3,4096]{2,0,1:T(8,128)}), f32[128,3,4096]{2,0,1:T(8,128)}) %all-gather.2.cloned.1.call-update) | async-done | bytes 6291472 | tf_op jit(solution)/shard_map/all_gather | solution.py:94
  73.6 6.6 %copy.77 = f32[128,3,4096]{0,2,1:T(8,128)} copy(f32[128,3,4096]{2,0,1:T(8,128)} %all-gather.2.cloned.1.call-done) | data formatting | bytes 12582912 | tf_op jit(solution)/shard_map/all_gather | solution.py:94
  80.2 12.7 %copy.80.p_ref = f32[128,3,64,64]{3,2,1,0:T(8,128)} copy(f32[128,3,64,64]{0,3,2,1:T(8,128)} %bitcast.35) | data formatting | bytes 12582912 | tf_op jit(solution)/shard_map/reshape | solution.py:95
  93.0 48.0 %shard_map.91 = f32[384,64,64]{2,1,0:T(8,128)} custom-call(s32[448]{0:T(512)} %bitcast.39, s32[448]{0:T(512)} %bitcast.40, s32[1344]{0:T(1024)} %reshape.184.slots_ref, s32[1]{0:T(128)} %bitcast.33.cnt_ref, f32[448,64,64]{2,1,0:T(8,128)} %copy.79.a_ref, f32[128,3,64,64]{3,2,1,0:T(8,128)} %copy.80.p_ref, f32[384,8]{1,0:T(8,128)} %bitcast.36), custom_call_target="tpu_custom_call" | custom-call | tf_op jit(solution)/shard_map/pallas_call | solution.py:66
  140.9 12.7 %reshape.189 = f32[64,6,4096]{2,1,0:T(8,128)} reshape(f32[384,64,64]{2,1,0:T(8,128)} %shard_map.91) | data formatting | bytes 12582912 | tf_op jit(solution)/shard_map/reshape | solution.py:102
  153.6 0.0 reduce-scatter.3.cloned.1.call-update
  153.6 0.1 reshape.181
  153.7 0.9 copy-done
  154.6 0.3 reshape.191
  154.9 0.2 convert_reduce_fusion
  155.1 0.1 fusion.7
  155.2 0.1 select_reduce_fusion.1
  155.3 50.5 %reduce-scatter.3.cloned.1.call-done = f32[8,6,4096]{2,1,0:T(8,128)} async-done(((f32[64,6,4096]{2,1,0:T(8,128)}), f32[8,6,4096]{2,1,0:T(8,128)}) %reduce-scatter.3.cloned.1.call-update) | async-done | bytes 786448 | tf_op jit(solution)/shard_map/reduce_scatter | solution.py:101
  205.8 1.8 reshape.205
  207.7 5.6 %convolution_bitcast_fusion = f32[8,3,6,64,64]{3,4,1,2,0:T(8,128)} fusion(f32[8,6,64,64]{3,2,1,0:T(8,128)S(1)} %reshape.205, f32[8,3,64,64]{3,2,0,1:T(8,128)S(1)} %reshape.191), kind=kOutput, calls=%fused_computation.1 | convolution fusion | flops 452984832 | bytes 3538944 | tf_op jit(solution)/shard_map/isjk,iqjl->isqkl/dot_general | solution.py:107
  213.3 6.1 %copy.95 = f32[8,3,6,64,64]{4,3,2,1,0:T(8,128)} copy(f32[8,3,6,64,64]{3,4,1,2,0:T(8,128)} %convolution_bitcast_fusion) | data formatting | bytes 4718592 | tf_op jit(solution)/shard_map/reshape | solution.py:108
  219.3 5.3 %reshape.206 = f32[24,6,4096]{2,1,0:T(8,128)} reshape(f32[8,3,6,64,64]{4,3,2,1,0:T(8,128)} %copy.95) | data formatting | bytes 4718592 | tf_op jit(solution)/shard_map/reshape | solution.py:108
  224.7 2.2 concatenate.23
  226.9 2.8 gather_fusion
  229.7 4.9 %broadcast_select_fusion = f32[32,6,4096]{2,1,0:T(8,128)} fusion(f32[32,6,4096]{2,1,0:T(8,128)} %gather_fusion, pred[32]{0:T(512)(128)(4,1)S(1)} %compare_and_fusion), kind=kLoop, calls=%fused_computation.2 | loop fusion | flops 786432 | bytes 6291488 | tf_op jit(solution)/shard_map/jit(_take)/select_n | solution.py:120
  234.6 7.0 %all-to-all-start = ((f32[32,6,4096]{2,1,0:T(8,128)}), f32[32,6,4096]{2,1,0:T(8,128)}, u32[]{:S(2)}, u32[]{:S(2)}) async-start(f32[32,6,4096]{2,1,0:T(8,128)} %broadcast_select_fusion), calls=%async_computation.1 | async-start | bytes 8388608 | tf_op jit(solution)/shard_map/all_to_all | solution.py:121
  241.6 0.0 reduce-scatter.5.cloned.1.call-start
  241.7 0.2 reduce_window_sum.11
  241.9 0.1 fusion.10
  242.1 0.1 select_reduce_fusion
  242.2 0.1 copy.74
  242.3 0.1 select_n.57
  242.4 53.6 %all-to-all-done = f32[32,6,4096]{2,1,0:T(8,128)} async-done(((f32[32,6,4096]{2,1,0:T(8,128)}), f32[32,6,4096]{2,1,0:T(8,128)}, u32[]{:S(2)}, u32[]{:S(2)}) %all-to-all-start) | async-done | bytes 3145760 | tf_op jit(solution)/shard_map/all_to_all | solution.py:121
  296.0 3.0 reshape.204
  299.1 3.9 %fusion.2 = f32[8,27,4096]{2,1,0:T(8,128)} fusion(f32[192,4096,1]{1,0,2:T(8,128)S(1)} %reshape.204, f32[8,27]{1,0:T(8,128)S(1)} %multiply_add_fusion, f32[192]{0:T(256)S(1)} %select_n.57), kind=kOutput, calls=%fused_computation.5 | convolution fusion | flops 2038473216 | bytes 6686304 | tf_op jit(solution)/shard_map/ec,ef->cf/dot_general | solution.py:137
  303.0 0.0 reduce-scatter.5.cloned.1.call-update
  303.0 46.5 %reduce-scatter.5.cloned.1.call-done = f32[1,27,4096]{2,1,0:T(8,128)} async-done(((f32[8,27,4096]{2,1,0:T(8,128)}), f32[1,27,4096]{2,1,0:T(8,128)}) %reduce-scatter.5.cloned.1.call-update) | async-done | bytes 442384 | tf_op jit(solution)/shard_map/reduce_scatter | solution.py:140
  349.5 2.3 copy.86
  (15 shorter events, 0.1 us)
Async XLA Ops:
  6.5 67.1 %all-gather.2.cloned.1.call-start = ((), (), s32[]{:S(2)}) async-start(), calls=%async_computation.3 | async-start | bytes 6684672 | tf_op jit(solution)/shard_map/all_gather | solution.py:94
  7.3 198.6 %reduce-scatter.3.cloned.1.call-start = ((), (), s32[]{:S(2)}) async-start(), calls=%async_computation.4 | async-start | bytes 9437184 | tf_op jit(solution)/shard_map/reduce_scatter | solution.py:101
  44.9 11.9 %copy-start.1 = (s32[1,1,3,448]{3,1,2,0:T(1,128)S(1)}, s32[1,1,3,448]{3,1,2,0:T(1,128)}, u32[]{:S(2)}) copy-start(s32[1,1,3,448]{3,1,2,0:T(1,128)} %param.12) | copy-start | bytes 16132
  153.6 1.0 copy-start
  234.6 61.4 %all-to-all-start = ((f32[32,6,4096]{2,1,0:T(8,128)}), f32[32,6,4096]{2,1,0:T(8,128)}, u32[]{:S(2)}, u32[]{:S(2)}) async-start(f32[32,6,4096]{2,1,0:T(8,128)} %broadcast_select_fusion), calls=%async_computation.1 | async-start | bytes 8388608 | tf_op jit(solution)/shard_map/all_to_all | solution.py:121
  241.6 107.9 %reduce-scatter.5.cloned.1.call-start = ((), (), s32[]{:S(2)}) async-start(), calls=%async_computation.5 | async-start | bytes 4718592 | tf_op jit(solution)/shard_map/reduce_scatter | solution.py:140
Sparse Core Ops, SparseCore 0:
  9.5 64.0 all-gather.1
  153.7 52.0 reduce-scatter.2
  303.1 46.3 reduce-scatter.4

commit v5 on v4

--- a/solution.py
+++ b/solution.py
@@ -15,14 +15,25 @@
 chunk = 32
 
 
-def ap_kernel(rows_ref, cols_ref, slots_ref, cnt_ref, a_ref, p_ref, meta_ref, o_ref):
+def ap_kernel(rows_ref, cols_ref, slots_ref, cnt_ref, a_ref, p2_ref, meta_ref, o_ref, p_scr, acc):
     c = pl.program_id(0)
     capacity = rows_ref.shape[0]
-    branches = p_ref.shape[1]
+    cols, branches = p2_ref.shape[:2]
 
     @pl.when(c == 0)
     def _():
-        o_ref[...] = jnp.zeros(o_ref.shape, o_ref.dtype)
+        acc[...] = jnp.zeros(acc.shape, acc.dtype)
+
+        def unpack(k, carry):
+            col = k // branches
+            s = k % branches
+            x = p2_ref[col, s]
+            even = x[:, :BLOCK]
+            odd = pltpu.roll(x, BLOCK, 1)[:, :BLOCK]
+            p_scr[col, s] = jnp.concatenate([even, odd], axis=0)
+            return carry
+
+        lax.fori_loop(0, cols * branches, unpack, 0, unroll=8)
 
     count = cnt_ref[0]
 
@@ -34,20 +45,31 @@
         row = rows_ref[t]
         for s in range(branches):
             prod = jnp.dot(
-                a, p_ref[col, s], preferred_element_type=jnp.float32, precision=highest
+                a, p_scr[col, s], preferred_element_type=jnp.float32, precision=highest
             )
             idx = row * TAP + slots_ref[s * capacity + t]
-            o_ref[idx] += jnp.where(live, prod, 0.0)
+            acc[idx] += jnp.where(live, prod, 0.0)
         return carry
 
     @pl.when(c * chunk < count)
     def _():
         lax.fori_loop(0, chunk, body, 0, unroll=True)
 
+    @pl.when(c == pl.num_programs(0) - 1)
+    def _():
+        def pack(i, carry):
+            even = acc[i, pl.ds(0, HALF, stride=2), :]
+            odd = acc[i, pl.ds(1, HALF, stride=2), :]
+            o_ref[i] = jnp.concatenate([even, odd], axis=1)
+            return carry
 
-def ap_partial(tiles, rows, cols, slots, count, panel, meta, out_rows):
+        lax.fori_loop(0, acc.shape[0], pack, 0, unroll=8)
+
+
+def ap_partial(tiles, rows, cols, slots, count, panel2, meta, out_rows):
     capacity = tiles.shape[0]
     chunks = capacity // chunk
+    ncols, branches = panel2.shape[:2]
 
     def a_map(c, rows_ref, cols_ref, slots_ref, cnt_ref):
         last = (cnt_ref[0] - 1) // chunk
@@ -62,15 +84,19 @@
             pl.BlockSpec(memory_space=pltpu.SMEM),
         ],
         out_specs=pl.BlockSpec(memory_space=pltpu.VMEM),
+        scratch_shapes=[
+            pltpu.VMEM((ncols, branches, BLOCK, BLOCK), jnp.float32),
+            pltpu.VMEM((out_rows * TAP, BLOCK, BLOCK), jnp.float32),
+        ],
     )
     return pl.pallas_call(
         ap_kernel,
-        out_shape=jax.ShapeDtypeStruct((out_rows * TAP, BLOCK, BLOCK), jnp.float32),
+        out_shape=jax.ShapeDtypeStruct((out_rows * TAP, HALF, LANES), jnp.float32),
         grid_spec=grid_spec,
         compiler_params=pltpu.CompilerParams(
-            dimension_semantics=("arbitrary",), vmem_limit_bytes=56 * 1024 * 1024
+            dimension_semantics=("arbitrary",), vmem_limit_bytes=60 * 1024 * 1024
         ),
-    )(rows, cols, slots, count, tiles, panel, meta)
+    )(rows, cols, slots, count, tiles, panel2, meta)
 
 
 def on_device(a_vals, a_row, a_col, a_slot, a_count, p_vals, p_owner, p_sub, ap_cslot):
@@ -91,22 +117,19 @@
     ).astype(jnp.float32)
     meta_all = lax.all_gather(meta_local, "row", axis=0, tiled=False)
 
-    panel = lax.all_gather(p_vals, "row", axis=0, tiled=True)
-    panel_tiles = panel.reshape(rows_dev * row_devices, branches, BLOCK, BLOCK)
+    p2 = p_vals.reshape(rows_dev, branches, HALF, LANES)
+    panel2 = lax.all_gather(p2, "row", axis=0, tiled=True)
+    a_split = (
+        a_vals.reshape(capacity, BLOCK, HALF, 2).transpose(0, 1, 3, 2).reshape(capacity, BLOCK, BLOCK)
+    )
     partial_value = ap_partial(
-        a_vals.reshape(capacity, BLOCK, BLOCK), a_row.reshape(capacity), a_col.reshape(capacity),
-        a_slot.reshape(branches * capacity), a_count.reshape(1), panel_tiles,
+        a_split, a_row.reshape(capacity), a_col.reshape(capacity),
+        a_slot.reshape(branches * capacity), a_count.reshape(1), panel2,
         meta_all.reshape(row_devices * item_count, TAP + 2), group_rows
     )
     ap_rows = lax.psum_scatter(
-        partial_value.reshape(group_rows, TAP, tile_len), "col", scatter_dimension=0, tiled=True
+        partial_value.reshape(group_rows, TAP, HALF, LANES), "col", scatter_dimension=0, tiled=True
     )
-
-    p4 = p_vals.reshape(rows_dev, branches, BLOCK, BLOCK)
-    ap4 = ap_rows.reshape(rows_dev, TAP, BLOCK, BLOCK)
-    prods = jnp.einsum("isjk,iqjl->isqkl", p4, ap4, precision=highest)
-    prods = prods.reshape(item_count, TAP, tile_len)
-    prods = jnp.concatenate([prods, jnp.zeros((1, TAP, tile_len), jnp.float32)], axis=0)
 
     owners = p_owner.reshape(item_count)
     serial = jnp.arange(item_count, dtype=jnp.int32)
@@ -117,7 +140,17 @@
     source = jnp.where(
         jnp.any(hit, axis=1), jnp.sum(jnp.where(hit, serial[None, :], 0), axis=1), item_count
     )
-    outgoing = jnp.take(prods, source, axis=0)
+    p_items = jnp.concatenate(
+        [p_vals.reshape(item_count, BLOCK, BLOCK), jnp.zeros((1, BLOCK, BLOCK), jnp.float32)], axis=0
+    )
+    left = jnp.take(p_items, source, axis=0)
+    right = jnp.take(
+        ap_rows.reshape(rows_dev, TAP, BLOCK, BLOCK), jnp.minimum(source // branches, rows_dev - 1),
+        axis=0,
+    )
+    outgoing = jnp.einsum("ejk,eqjl->eqkl", left, right, precision=highest).reshape(
+        slots_total, TAP, tile_len
+    )
     incoming = lax.all_to_all(outgoing, "row", split_axis=0, concat_axis=0, tiled=True)
 
     me = lax.axis_index("row").astype(jnp.float32)

time: 360 us -> 332 us (0.922)
  waiting for transfers between devices: 167 us -> 153 us
  local copies, waits for them, and re-layouts: 82 us -> 70.7 us
  matrix products: 9.53 us -> 17.5 us
  Pallas kernels: 48 us -> 40.3 us
  other arithmetic: 5.79 us -> 1.61 us
    all_gather x1, waiting for transfers between devices: 15.5 us -> 0.01 us  [on_device(): panel2 = lax.all_gather(p2, 'row', axis=0, tiled=True)]
    reshape x7, local copies, waits for them, and re-layouts: 50.9 us -> 39.1 us  [the longest x2 22.8 us: on_device(): a_vals.reshape(capacity, BLOCK, HALF, 2).transpose(0, 1, 3, 2)]
    transpose x0 -> x1, local copies, waits for them, and re-layouts: none -> 8.56 us  [on_device(): a_vals.reshape(capacity, BLOCK, HALF, 2).transpose(0, 1, 3, 2)]
    dot_general x1, matrix products: 5.6 us -> 13.5 us  [on_device(): jnp.einsum('ejk,eqjl->eqkl', left, right, precision=highest)]
    pallas_call x1, Pallas kernels: 48 us -> 40.3 us  [ap_partial(): pl.pallas_call(ap_kernel, out_shape=jax.ShapeDtypeStruct((out_rows * TAP,...]
    all_gather x1 -> x0, local copies, waits for them, and re-layouts: 6.62 us -> none  [on_device(): panel = lax.all_gather(p_vals, 'row', axis=0, tiled=True)]
    select_n x2 -> x1, other arithmetic: 4.92 us -> 0.02 us  [on_device(): left = jnp.take(p_items, source, axis=0)]
    unnamed x8 -> x14, local copies, waits for them, and re-layouts: 12.2 us -> 11.5 us
  transfers between devices with their start and end apart: 4 -> 4, of which waited for: 4 -> 3; matrix products, arithmetic and copies ran while one was open for 7% -> 14% of each run, Pallas kernels for 0% -> 0%
where the time goes in v5:
time: 332 us; the launch traced here: 330 us
  waiting for transfers between devices  153 us (46%)
  local copies, waits for them, and re-layouts  70.7 us (21%)
  Pallas kernels  40.3 us (12%)
  blocking collectives  25.8 us (8%)
  matrix products  17.5 us (5%)
  between operations  13.9 us (4%)
  starting transfers between devices  7.32 us (2%)
    reduce_scatter x1, waiting for transfers between devices, on_device(): lax.psum_scatter(partial_value.reshape(group_rows, TAP, HALF, LANES), 'co...  53.5 us
    all_to_all x1, waiting for transfers between devices, on_device(): lax.all_to_all(outgoing, 'row', split_axis=0, concat_axis=0, tiled=True)  53.4 us
    reduce_scatter x1, waiting for transfers between devices, on_device(): lax.psum_scatter(coarse_part.reshape(col_devices, TC, tile_len), 'col', s...  46.1 us
    pallas_call x1, Pallas kernels, ap_partial(): pl.pallas_call(ap_kernel, out_shape=jax.ShapeDtypeStruct((out_rows * TAP,...  40.3 us
    all_gather x1, blocking collectives, on_device(): meta_all = lax.all_gather(meta_local, 'row', axis=0, tiled=False)  25.8 us
    reshape x2, local copies, waits for them, and re-layouts, on_device(): a_vals.reshape(capacity, BLOCK, HALF, 2).transpose(0, 1, 3, 2)  22.8 us
    reshape x2, local copies, waits for them, and re-layouts, on_device(): jnp.einsum('ejk,eqjl->eqkl', left, right, precision=highest)  13.6 us
    dot_general x1, matrix products, on_device(): jnp.einsum('ejk,eqjl->eqkl', left, right, precision=highest)  13.5 us
  transfers between devices with their start and end apart: 4, of which 3 were waited for; matrix products, arithmetic and copies ran while one was open for 14% of the time, Pallas kernels for 0%

profile of v5, /device:TPU:0, one launch (start us, length us, event | category | flops | bytes accessed | tf_op | source)
XLA Modules:
  0.0 330.2 jit_solution(9118824818867721355)
XLA Ops:
  6.5 1.1 copy.90
  7.6 0.8 copy.75
  8.4 0.0 all-gather.2.cloned.1.call-update
  8.4 0.0 reduce-scatter.3.cloned.1.call-start
  8.5 0.7 reduce
  9.2 0.7 reshape.237.slots_ref
  10.5 9.0 %copy.73 = f32[1,1,448,4096]{2,3,1,0:T(8,128)} copy(f32[1,1,448,4096]{3,2,1,0:T(8,128)} %param.9) | data formatting | bytes 14680064 | tf_op args[0]
  19.5 10.9 %reshape.239 = f32[448,64,32,2]{0,3,2,1:T(2,128)} reshape(f32[1,1,448,4096]{2,3,1,0:T(8,128)} %copy.73) | data formatting | bytes 14680064 | tf_op jit(solution)/shard_map/reshape | solution.py:123
  30.3 8.6 %copy.74 = f32[448,64,2,32]{0,3,2,1:T(8,128)} copy(f32[448,64,2,32]{0,2,3,1:T(2,128)} %bitcast.56) | data formatting | bytes 14680064 | tf_op jit(solution)/shard_map/transpose | solution.py:123
  38.9 11.9 %copy.77.a_ref = f32[448,64,64]{2,1,0:T(8,128)} copy(f32[448,64,64]{0,2,1:T(8,128)} %bitcast.57) | data formatting | bytes 14680064 | tf_op jit(solution)/shard_map/reshape | solution.py:123
  50.9 0.1 copy.68
  51.0 0.1 concatenate.21
  51.1 0.1 copy.67
  51.2 0.1 concatenate.20
  51.2 0.1 copy.66
  51.3 0.1 concatenate.19
  51.4 25.8 %all_gather.7 = f32[16,24,8]{1,2,0:T(8,128)S(1)} all-gather(f32[1,24,8]{1,2,0:T(8,128)S(1)} %add_convert_fusion), channel_id=1, replica_groups=mesh['row'=16,'col'=8] {'row'}, dimensions={0}, use_global_device_ids=true | all-gather | bytes 13056 | tf_op jit(solution)/shard_map/all_gather | solution.py:118
  77.2 0.8 copy.76
  78.0 40.3 %shard_map.91 = f32[384,32,128]{2,1,0:T(8,128)} custom-call(s32[448]{0:T(512)} %bitcast.64, s32[448]{0:T(512)} %bitcast.65, s32[1344]{0:T(1024)} %reshape.237.slots_ref, s32[1]{0:T(128)} %bitcast.55.cnt_ref, f32[448,64,64]{2,1,0:T(8,128)} %copy.77.a_ref, f32[128,3,32,128]{3,2,1,0:T(8,128)} %all-gather.2.cloned.1.call-done.p2_ref, f32[384,8]{1,0:T(8,128)} %bitcast.61), custom_call_target="tpu_custom_call" | custom-call | tf_op jit(solution)/shard_map/pallas_call | solution.py:92
  118.3 0.0 reduce-scatter.3.cloned.1.call-update
  118.4 0.1 reshape.234
  118.4 0.9 copy-done
  119.3 0.3 copy.78
  119.6 0.4 reshape.245
  120.0 0.1 concatenate.23
  120.1 0.2 convert_reduce_fusion
  120.3 0.1 fusion.16
  120.4 0.1 select_reduce_fusion.1
  120.5 0.6 gather_fusion.1
  121.2 53.5 %reduce-scatter.3.cloned.1.call-done = f32[8,6,32,128]{3,2,1,0:T(8,128)} async-done(((f32[64,6,32,128]{3,2,1,0:T(8,128)}), f32[8,6,32,128]{3,2,1,0:T(8,128)}) %reduce-scatter.3.cloned.1.call-update) | async-done | bytes 786448 | tf_op jit(solution)/shard_map/reduce_scatter | solution.py:130
  174.6 1.5 reshape.244
  176.1 3.6 %gather_fusion = f32[32,6,64,64]{3,2,1,0:T(8,128)} fusion(f32[8,6,64,64]{3,2,1,0:T(8,128)S(1)} %reshape.244, s32[1024]{0:T(1024)S(1)} %get-tuple-element.16), kind=kCustom, calls=%fused_computation | custom fusion | bytes 6291584 | tf_op jit(solution)/shard_map/jit(_take)/gather | solution.py:147
  179.7 13.5 %fusion.4 = f32[32,6,64,64]{2,3,1,0:T(8,128)} fusion(f32[32,6,64,64]{3,2,1,0:T(8,128)} %gather_fusion, pred[32]{0:T(512)(128)(4,1)S(1)} %compare_and_fusion.1, f32[32,64,64]{2,1,0:T(8,128)S(1)} %gather_fusion.1, pred[32]{0:T(512)(128)(4,1)S(1)} %get-tuple-element.9), kind=kOutput, calls=%fused_computation.6 | convolution fusion | flops 604897280 | bytes 6815808 | tf_op jit(solution)/shard_map/ejk,eqjl->eqkl/dot_general | solution.py:151
  193.3 6.5 %copy.85 = f32[32,6,64,64]{3,2,1,0:T(8,128)} copy(f32[32,6,64,64]{2,3,1,0:T(8,128)} %fusion.4) | data formatting | bytes 6291456 | tf_op jit(solution)/shard_map/reshape | solution.py:151
  199.8 7.1 %reshape.266 = f32[32,6,4096]{2,1,0:T(8,128)} reshape(f32[32,6,64,64]{3,2,1,0:T(8,128)} %copy.85) | data formatting | bytes 6291456 | tf_op jit(solution)/shard_map/reshape | solution.py:151
  206.9 7.0 %all-to-all-start = ((f32[32,6,4096]{2,1,0:T(8,128)}), f32[32,6,4096]{2,1,0:T(8,128)}, u32[]{:S(2)}, u32[]{:S(2)}) async-start(f32[32,6,4096]{2,1,0:T(8,128)} %reshape.266), calls=%async_computation.1 | async-start | bytes 8388608 | tf_op jit(solution)/shard_map/all_to_all | solution.py:154
  213.9 0.3 reduce-scatter.5.cloned.1.call-start
  214.2 0.2 reduce_window_sum.11
  214.4 0.1 fusion.22
  214.5 0.1 select_reduce_fusion
  214.7 0.1 copy.71
  214.8 0.1 select_n.97
  214.9 53.4 %all-to-all-done = f32[32,6,4096]{2,1,0:T(8,128)} async-done(((f32[32,6,4096]{2,1,0:T(8,128)}), f32[32,6,4096]{2,1,0:T(8,128)}, u32[]{:S(2)}, u32[]{:S(2)}) %all-to-all-start) | async-done | bytes 3145760 | tf_op jit(solution)/shard_map/all_to_all | solution.py:154
  268.3 3.0 reshape.265
  271.3 3.9 %fusion.11 = f32[8,27,4096]{2,1,0:T(8,128)} fusion(f32[192,4096,1]{1,0,2:T(8,128)S(1)} %reshape.265, f32[8,27]{1,0:T(8,128)S(1)} %multiply_add_fusion, f32[192]{0:T(256)S(1)} %select_n.97), kind=kOutput, calls=%fused_computation.12 | convolution fusion | flops 2038473216 | bytes 6686304 | tf_op jit(solution)/shard_map/ec,ef->cf/dot_general | solution.py:170
  275.2 0.0 reduce-scatter.5.cloned.1.call-update
  275.3 46.1 %reduce-scatter.5.cloned.1.call-done = f32[1,27,4096]{2,1,0:T(8,128)} async-done(((f32[8,27,4096]{2,1,0:T(8,128)}), f32[1,27,4096]{2,1,0:T(8,128)}) %reduce-scatter.5.cloned.1.call-update) | async-done | bytes 442384 | tf_op jit(solution)/shard_map/reduce_scatter | solution.py:173
  321.4 2.3 copy.82
  (22 shorter events, 0.2 us)
Async XLA Ops:
  6.5 71.5 %all-gather.2.cloned.1.call-start = ((), (), s32[]{:S(2)}) async-start(), calls=%async_computation.3 | async-start | bytes 6684672 | tf_op jit(solution)/shard_map/all_gather | solution.py:121
  8.4 166.2 %reduce-scatter.3.cloned.1.call-start = ((), (), s32[]{:S(2)}) async-start(), calls=%async_computation.4 | async-start | bytes 7077888 | tf_op jit(solution)/shard_map/reduce_scatter | solution.py:130
  38.9 11.9 %copy-start.1 = (s32[8,3,6]{2,0,1:T(8,128)S(1)}, s32[8,3,6]{2,0,1:T(8,128)}, u32[]{:S(2)}) copy-start(s32[8,3,6]{2,0,1:T(8,128)} %param.17) | copy-start | bytes 1732
  38.9 12.2 %copy-start.2 = (s32[8,3]{0,1:T(4,128)S(1)}, s32[8,3]{0,1:T(4,128)}, u32[]{:S(2)}) copy-start(s32[8,3]{0,1:T(4,128)} %param.16) | copy-start | bytes 292
  38.9 12.3 %copy-start.3 = (s32[8,3]{0,1:T(4,128)S(1)}, s32[8,3]{0,1:T(4,128)}, u32[]{:S(2)}) copy-start(s32[8,3]{0,1:T(4,128)} %param.15) | copy-start | bytes 292
  118.3 1.0 copy-start
  206.9 61.4 %all-to-all-start = ((f32[32,6,4096]{2,1,0:T(8,128)}), f32[32,6,4096]{2,1,0:T(8,128)}, u32[]{:S(2)}, u32[]{:S(2)}) async-start(f32[32,6,4096]{2,1,0:T(8,128)} %reshape.266), calls=%async_computation.1 | async-start | bytes 8388608 | tf_op jit(solution)/shard_map/all_to_all | solution.py:154
  213.9 107.5 %reduce-scatter.5.cloned.1.call-start = ((), (), s32[]{:S(2)}) async-start(), calls=%async_computation.5 | async-start | bytes 4718592 | tf_op jit(solution)/shard_map/reduce_scatter | solution.py:173
Sparse Core Ops, SparseCore 0:
  9.5 64.1 all-gather.1
  118.5 56.1 reduce-scatter.2
  275.4 45.9 reduce-scatter.4

commit v6 on v5

--- a/solution.py
+++ b/solution.py
@@ -99,6 +99,52 @@
     )(rows, cols, slots, count, tiles, panel2, meta)
 
 
+def unpack(x):
+    return jnp.concatenate([x[:, :BLOCK], pltpu.roll(x, BLOCK, 1)[:, :BLOCK]], axis=0)
+
+
+def contrib_kernel(src_ref, p2_ref, ap2_ref, o_ref, scr):
+    slots = o_ref.shape[0]
+    items = p2_ref.shape[0]
+    branches = items // ap2_ref.shape[0]
+
+    def body(e, carry):
+        item = src_ref[e]
+        live = item < items
+        it = jnp.minimum(item, items - 1)
+        left = unpack(p2_ref[it])
+        for q in range(TAP):
+            right = unpack(ap2_ref[it // branches, q])
+            prod = lax.dot_general(
+                left, right, (((0,), (0,)), ((), ())),
+                preferred_element_type=jnp.float32, precision=highest,
+            )
+            scr[...] = jnp.where(live, prod, 0.0)
+            even = scr[pl.ds(0, HALF, stride=2), :]
+            odd = scr[pl.ds(1, HALF, stride=2), :]
+            o_ref[e, q] = jnp.concatenate([even, odd], axis=1)
+        return carry
+
+    lax.fori_loop(0, slots, body, 0)
+
+
+def contributions(source, p2, ap2, slots):
+    return pl.pallas_call(
+        contrib_kernel,
+        out_shape=jax.ShapeDtypeStruct((slots, TAP, HALF, LANES), jnp.float32),
+        grid_spec=pltpu.PrefetchScalarGridSpec(
+            num_scalar_prefetch=1,
+            grid=(1,),
+            in_specs=[
+                pl.BlockSpec(memory_space=pltpu.VMEM),
+                pl.BlockSpec(memory_space=pltpu.VMEM),
+            ],
+            out_specs=pl.BlockSpec(memory_space=pltpu.VMEM),
+            scratch_shapes=[pltpu.VMEM((BLOCK, BLOCK), jnp.float32)],
+        ),
+    )(source, p2, ap2)
+
+
 def on_device(a_vals, a_row, a_col, a_slot, a_count, p_vals, p_owner, p_sub, ap_cslot):
     row_devices = lax.axis_size("row")
     col_devices = lax.axis_size("col")
@@ -140,17 +186,7 @@
     source = jnp.where(
         jnp.any(hit, axis=1), jnp.sum(jnp.where(hit, serial[None, :], 0), axis=1), item_count
     )
-    p_items = jnp.concatenate(
-        [p_vals.reshape(item_count, BLOCK, BLOCK), jnp.zeros((1, BLOCK, BLOCK), jnp.float32)], axis=0
-    )
-    left = jnp.take(p_items, source, axis=0)
-    right = jnp.take(
-        ap_rows.reshape(rows_dev, TAP, BLOCK, BLOCK), jnp.minimum(source // branches, rows_dev - 1),
-        axis=0,
-    )
-    outgoing = jnp.einsum("ejk,eqjl->eqkl", left, right, precision=highest).reshape(
-        slots_total, TAP, tile_len
-    )
+    outgoing = contributions(source, p2.reshape(item_count, HALF, LANES), ap_rows, slots_total)
     incoming = lax.all_to_all(outgoing, "row", split_axis=0, concat_axis=0, tiled=True)
 
     me = lax.axis_index("row").astype(jnp.float32)
@@ -167,12 +203,12 @@
     onehot = (
         dest_slot[:, None] == jnp.arange(group_coarse, dtype=jnp.float32)[None, :]
     ).astype(jnp.float32)
-    coarse_part = jnp.einsum(
-        "ec,ef->cf", onehot, incoming.reshape(slots_total * TAP, tile_len), precision=highest
-    )
+    coarse_part = jnp.einsum("ec,eml->cml", onehot, incoming.reshape(slots_total * TAP, HALF, LANES),
+                             precision=highest)
     coarse = lax.psum_scatter(
-        coarse_part.reshape(col_devices, TC, tile_len), "col", scatter_dimension=0, tiled=True
-    )
+        coarse_part.reshape(col_devices, TC, HALF, LANES), "col", scatter_dimension=0, tiled=True
+    )
+    coarse = coarse.reshape(1, TC, tile_len)
     return coarse
 
 

time: 332 us -> 302 us (0.910)
  local copies, waits for them, and re-layouts: 70.7 us -> 50.8 us
  Pallas kernels: 40.3 us -> 59.9 us
  waiting for transfers between devices: 153 us -> 137 us
  matrix products: 17.5 us -> 5.79 us
    pallas_call x0 -> x1, Pallas kernels: none -> 19.6 us  [contributions(): pl.pallas_call(contrib_kernel, out_shape=jax.ShapeDtypeStruct((slots, TAP...]
    reshape x5 -> x0, local copies, waits for them, and re-layouts: 18.5 us -> none  [the longest x2 13.6 us: on_device(): jnp.einsum('ejk,eqjl->eqkl', left, right, precision=highest)]
    all_to_all x1, waiting for transfers between devices: 53.4 us -> 41.7 us  [on_device(): lax.all_to_all(outgoing, 'row', split_axis=0, concat_axis=0, tiled=True)]
    dot_general x2 -> x1, matrix products: 17.5 us -> 5.79 us  [on_device(): jnp.einsum('ec,eml->cml', onehot, incoming.reshape(slots_total * TAP, HAL...]
    reduce_scatter x1, waiting for transfers between devices: 46.1 us -> 41.5 us  [on_device(): lax.psum_scatter(coarse_part.reshape(col_devices, TC, HALF, LANES), 'col'...]
    gather x2 -> x0, local copies, waits for them, and re-layouts: 4.22 us -> none  [the longest x1 3.61 us: on_device(): jnp.take(ap_rows.reshape(rows_dev, TAP, BLOCK, BLOCK), jnp.minimum(source...]
    unnamed x14 -> x10, local copies, waits for them, and re-layouts: 11.5 us -> 13.5 us
  transfers between devices with their start and end apart: 4 -> 4, of which waited for: 3 -> 3; matrix products, arithmetic and copies ran while one was open for 14% -> 16% of each run, Pallas kernels for 0% -> 0%
where the time goes in v6:
time: 302 us; the launch traced here: 301 us
  waiting for transfers between devices  137 us (45%)
  Pallas kernels  59.9 us (20%)
  local copies, waits for them, and re-layouts  50.8 us (17%)
  blocking collectives  25.2 us (8%)
  between operations  13.9 us (5%)
  starting transfers between devices  7.22 us (2%)
  matrix products  5.79 us (2%)
    reduce_scatter x1, waiting for transfers between devices, on_device(): lax.psum_scatter(partial_value.reshape(group_rows, TAP, HALF, LANES), 'co...  53.4 us
    all_to_all x1, waiting for transfers between devices, on_device(): lax.all_to_all(outgoing, 'row', split_axis=0, concat_axis=0, tiled=True)  41.7 us
    reduce_scatter x1, waiting for transfers between devices, on_device(): lax.psum_scatter(coarse_part.reshape(col_devices, TC, HALF, LANES), 'col'...  41.5 us
    pallas_call x1, Pallas kernels, ap_partial(): pl.pallas_call(ap_kernel, out_shape=jax.ShapeDtypeStruct((out_rows * TAP,...  40.3 us
    all_gather x1, blocking collectives, on_device(): meta_all = lax.all_gather(meta_local, 'row', axis=0, tiled=False)  25.2 us
    reshape x2, local copies, waits for them, and re-layouts, on_device(): a_vals.reshape(capacity, BLOCK, HALF, 2).transpose(0, 1, 3, 2)  22.7 us
    pallas_call x1, Pallas kernels, contributions(): pl.pallas_call(contrib_kernel, out_shape=jax.ShapeDtypeStruct((slots, TAP...  19.6 us
    unnamed x10, local copies, waits for them, and re-layouts  13.5 us
  transfers between devices with their start and end apart: 4, of which 3 were waited for; matrix products, arithmetic and copies ran while one was open for 16% of the time, Pallas kernels for 0%

profile of v6, /device:TPU:0, one launch (start us, length us, event | category | flops | bytes accessed | tf_op | source)
XLA Modules:
  0.0 300.8 jit_solution(7125750558861730404)
XLA Ops:
  6.5 0.0 all-gather.2.cloned.1.call-start
  6.5 1.1 copy.84
  7.6 0.8 copy.71
  8.4 0.0 all-gather.2.cloned.1.call-update
  8.4 0.0 reduce-scatter.3.cloned.1.call-start
  8.5 0.8 copy.61
  9.2 0.1 concatenate.16
  9.3 0.8 copy.63
  10.1 0.1 concatenate.18
  10.2 0.8 copy.62
  11.0 0.1 concatenate.17
  11.1 25.2 %all_gather.7 = f32[16,24,8]{1,2,0:T(8,128)S(1)} all-gather(f32[1,24,8]{1,2,0:T(8,128)S(1)} %add_convert_fusion), channel_id=1, replica_groups=mesh['row'=16,'col'=8] {'row'}, dimensions={0}, use_global_device_ids=true | all-gather | bytes 13056 | tf_op jit(solution)/shard_map/all_gather | solution.py:164
  36.3 0.8 copy.72
  37.1 8.9 %copy.69 = f32[1,1,448,4096]{2,3,1,0:T(8,128)} copy(f32[1,1,448,4096]{3,2,1,0:T(8,128)} %param.9) | data formatting | bytes 14680064 | tf_op args[0]
  46.0 10.8 %reshape.155 = f32[448,64,32,2]{0,3,2,1:T(2,128)} reshape(f32[1,1,448,4096]{2,3,1,0:T(8,128)} %copy.69) | data formatting | bytes 14680064 | tf_op jit(solution)/shard_map/reshape | solution.py:169
  56.9 8.7 %copy.70 = f32[448,64,2,32]{0,3,2,1:T(8,128)} copy(f32[448,64,2,32]{0,2,3,1:T(2,128)} %bitcast.37) | data formatting | bytes 14680064 | tf_op jit(solution)/shard_map/transpose | solution.py:169
  65.5 0.0 copy-start.1
  65.6 11.9 %copy.73.a_ref = f32[448,64,64]{2,1,0:T(8,128)} copy(f32[448,64,64]{0,2,1:T(8,128)} %bitcast.38) | data formatting | bytes 14680064 | tf_op jit(solution)/shard_map/reshape | solution.py:169
  77.4 0.0 copy-done.1
  77.5 0.7 reshape.153.slots_ref
  78.8 0.0 all-gather.2.cloned.1.call-done.p2_ref
  78.8 40.3 %shard_map.91 = f32[384,32,128]{2,1,0:T(8,128)} custom-call(s32[448]{0:T(512)} %bitcast.46, s32[448]{0:T(512)} %bitcast.47, s32[1344]{0:T(1024)} %reshape.153.slots_ref, s32[1]{0:T(128)} %bitcast.36.cnt_ref, f32[448,64,64]{2,1,0:T(8,128)} %copy.73.a_ref, f32[128,3,32,128]{3,2,1,0:T(8,128)} %all-gather.2.cloned.1.call-done.p2_ref, f32[384,8]{1,0:T(8,128)} %bitcast.43), custom_call_target="tpu_custom_call" | custom-call | tf_op jit(solution)/shard_map/pallas_call | solution.py:92
  119.1 0.0 copy-start
  119.1 0.0 reduce-scatter.3.cloned.1.call-update
  119.2 0.1 reshape.150
  119.2 0.9 copy-done
  120.1 0.3 copy.68
  120.4 1.0 reshape_reshape.3.p2_ref
  121.4 0.2 convert_reduce_fusion
  121.6 0.1 fusion.8
  121.7 0.1 select_reduce_fusion.1
  121.8 0.5 broadcast_select_fusion.1.src_ref
  122.4 53.4 %reduce-scatter.3.cloned.1.call-done.ap2_ref = f32[8,6,32,128]{3,2,1,0:T(8,128)} async-done(((f32[64,6,32,128]{3,2,1,0:T(8,128)}), f32[8,6,32,128]{3,2,1,0:T(8,128)}) %reduce-scatter.3.cloned.1.call-update) | async-done | bytes 786448 | tf_op jit(solution)/shard_map/reduce_scatter | solution.py:176
  175.7 19.6 %shard_map.92 = f32[32,6,32,128]{3,2,1,0:T(8,128)} custom-call(s32[32]{0:T(128)} %broadcast_select_fusion.1.src_ref, f32[24,32,128]{2,1,0:T(8,128)} %reshape_reshape.3.p2_ref, f32[8,6,32,128]{3,2,1,0:T(8,128)} %reduce-scatter.3.cloned.1.call-done.ap2_ref), custom_call_target="tpu_custom_call" | custom-call | tf_op jit(solution)/shard_map/pallas_call | solution.py:132
  195.3 7.0 %all-to-all-start = ((f32[32,6,32,128]{3,2,1,0:T(8,128)}), f32[32,6,32,128]{3,2,1,0:T(8,128)S(1)}, u32[]{:S(2)}, u32[]{:S(2)}) async-start(f32[32,6,32,128]{3,2,1,0:T(8,128)} %shard_map.92), calls=%async_computation.1 | async-start | bytes 6291456 | tf_op jit(solution)/shard_map/all_to_all | solution.py:190
  202.2 0.2 reduce-scatter.5.cloned.1.call-start
  202.5 0.2 reduce_window_sum.11
  202.7 0.1 fusion.10
  202.9 0.1 select_reduce_fusion
  203.0 0.1 copy.66
  203.1 0.1 select_n.25
  203.2 41.7 %all-to-all-done = f32[32,6,32,128]{3,2,1,0:T(8,128)S(1)} async-done(((f32[32,6,32,128]{3,2,1,0:T(8,128)}), f32[32,6,32,128]{3,2,1,0:T(8,128)S(1)}, u32[]{:S(2)}, u32[]{:S(2)}) %all-to-all-start) | async-done | bytes 3145760 | tf_op jit(solution)/shard_map/all_to_all | solution.py:190
  244.9 5.8 %fusion = f32[8,27,32,128]{3,1,2,0:T(8,128)} fusion(f32[192,32,128]{2,1,0:T(8,128)S(1)} %bitcast.40, f32[8,27]{1,0:T(8,128)S(1)} %multiply_add_fusion, f32[192]{0:T(256)S(1)} %select_n.25), kind=kOutput, calls=%fused_computation | convolution fusion | flops 2038473216 | bytes 6686304 | tf_op jit(solution)/shard_map/ec,eml->cml/dot_general | solution.py:206
  250.7 0.0 reduce-scatter.5.cloned.1.call-update
  250.7 41.5 %reduce-scatter.5.cloned.1.call-done = f32[1,27,32,128]{3,1,2,0:T(8,128)} async-done(((f32[8,27,32,128]{3,1,2,0:T(8,128)}), f32[1,27,32,128]{3,1,2,0:T(8,128)}) %reduce-scatter.5.cloned.1.call-update) | async-done | bytes 442384 | tf_op jit(solution)/shard_map/reduce_scatter | solution.py:208
  292.2 2.1 copy.75
  (10 shorter events, 0.1 us)
Async XLA Ops:
  6.5 72.3 %all-gather.2.cloned.1.call-start = ((), (), s32[]{:S(2)}) async-start(), calls=%async_computation.3 | async-start | bytes 6684672 | tf_op jit(solution)/shard_map/all_gather | solution.py:167
  8.4 167.3 %reduce-scatter.3.cloned.1.call-start = ((), (), s32[]{:S(2)}) async-start(), calls=%async_computation.4 | async-start | bytes 7077888 | tf_op jit(solution)/shard_map/reduce_scatter | solution.py:176
  65.5 11.9 %copy-start.1 = (s32[1,1,3,448]{3,1,2,0:T(1,128)S(1)}, s32[1,1,3,448]{3,1,2,0:T(1,128)}, u32[]{:S(2)}) copy-start(s32[1,1,3,448]{3,1,2,0:T(1,128)} %param.12) | copy-start | bytes 16132
  119.1 1.0 copy-start
  195.3 49.6 %all-to-all-start = ((f32[32,6,32,128]{3,2,1,0:T(8,128)}), f32[32,6,32,128]{3,2,1,0:T(8,128)S(1)}, u32[]{:S(2)}, u32[]{:S(2)}) async-start(f32[32,6,32,128]{3,2,1,0:T(8,128)} %shard_map.92), calls=%async_computation.1 | async-start | bytes 6291456 | tf_op jit(solution)/shard_map/all_to_all | solution.py:190
  202.2 89.9 %reduce-scatter.5.cloned.1.call-start = ((), (), s32[]{:S(2)}) async-start(), calls=%async_computation.5 | async-start | bytes 4718592 | tf_op jit(solution)/shard_map/reduce_scatter | solution.py:208
Sparse Core Ops, SparseCore 0:
  9.5 64.0 all-gather.1
  119.3 56.3 reduce-scatter.2
  250.8 41.3 reduce-scatter.4

commit v7 on v6

--- a/solution.py
+++ b/solution.py
@@ -9,16 +9,18 @@
 TAP = 6
 TC = 27
 LANES = 128
+RPD = 8
 HALF = BLOCK * BLOCK // LANES
 
 highest = lax.Precision.HIGHEST
 chunk = 32
 
 
-def ap_kernel(rows_ref, cols_ref, slots_ref, cnt_ref, a_ref, p2_ref, meta_ref, o_ref, p_scr, acc):
+def ap_kernel(rows_ref, cols_ref, slots_ref, cnt_ref, a_ref, p2_ref, o_ref, p_scr, acc):
     c = pl.program_id(0)
     capacity = rows_ref.shape[0]
-    cols, branches = p2_ref.shape[:2]
+    cols, branches = p_scr.shape[:2]
+    per_peer_tiles = p2_ref.shape[0] // (cols // RPD)
 
     @pl.when(c == 0)
     def _():
@@ -27,7 +29,7 @@
         def unpack(k, carry):
             col = k // branches
             s = k % branches
-            x = p2_ref[col, s]
+            x = p2_ref[(col // RPD) * per_peer_tiles + (col % RPD) * branches + s]
             even = x[:, :BLOCK]
             odd = pltpu.roll(x, BLOCK, 1)[:, :BLOCK]
             p_scr[col, s] = jnp.concatenate([even, odd], axis=0)
@@ -66,10 +68,9 @@
         lax.fori_loop(0, acc.shape[0], pack, 0, unroll=8)
 
 
-def ap_partial(tiles, rows, cols, slots, count, panel2, meta, out_rows):
+def ap_partial(tiles, rows, cols, slots, count, panel2, ncols, branches, out_rows):
     capacity = tiles.shape[0]
     chunks = capacity // chunk
-    ncols, branches = panel2.shape[:2]
 
     def a_map(c, rows_ref, cols_ref, slots_ref, cnt_ref):
         last = (cnt_ref[0] - 1) // chunk
@@ -81,7 +82,6 @@
         in_specs=[
             pl.BlockSpec((chunk, BLOCK, BLOCK), a_map),
             pl.BlockSpec(memory_space=pltpu.VMEM),
-            pl.BlockSpec(memory_space=pltpu.SMEM),
         ],
         out_specs=pl.BlockSpec(memory_space=pltpu.VMEM),
         scratch_shapes=[
@@ -96,7 +96,7 @@
         compiler_params=pltpu.CompilerParams(
             dimension_semantics=("arbitrary",), vmem_limit_bytes=60 * 1024 * 1024
         ),
-    )(rows, cols, slots, count, tiles, panel2, meta)
+    )(rows, cols, slots, count, tiles, panel2)
 
 
 def unpack(x):
@@ -112,13 +112,10 @@
         item = src_ref[e]
         live = item < items
         it = jnp.minimum(item, items - 1)
-        left = unpack(p2_ref[it])
+        left = unpack(p2_ref[it]).T
         for q in range(TAP):
             right = unpack(ap2_ref[it // branches, q])
-            prod = lax.dot_general(
-                left, right, (((0,), (0,)), ((), ())),
-                preferred_element_type=jnp.float32, precision=highest,
-            )
+            prod = jnp.dot(left, right, preferred_element_type=jnp.float32, precision=highest)
             scr[...] = jnp.where(live, prod, 0.0)
             even = scr[pl.ds(0, HALF, stride=2), :]
             odd = scr[pl.ds(1, HALF, stride=2), :]
@@ -161,17 +158,18 @@
         [p_owner.reshape(item_count, 1), p_sub.reshape(item_count, 1),
          ap_cslot.reshape(item_count, TAP)], axis=1
     ).astype(jnp.float32)
-    meta_all = lax.all_gather(meta_local, "row", axis=0, tiled=False)
-
-    p2 = p_vals.reshape(rows_dev, branches, HALF, LANES)
-    panel2 = lax.all_gather(p2, "row", axis=0, tiled=True)
+    meta_tile = jnp.pad(meta_local.reshape(-1), (0, tile_len - item_count * (TAP + 2)))
+    p2 = p_vals.reshape(item_count, HALF, LANES)
+    sent = jnp.concatenate([p2, meta_tile.reshape(1, HALF, LANES)], axis=0)
+    panel2 = lax.all_gather(sent, "row", axis=0, tiled=True)
+    meta_all = panel2.reshape(row_devices, item_count + 1, tile_len)[:, item_count, :item_count * (TAP + 2)]
     a_split = (
         a_vals.reshape(capacity, BLOCK, HALF, 2).transpose(0, 1, 3, 2).reshape(capacity, BLOCK, BLOCK)
     )
     partial_value = ap_partial(
         a_split, a_row.reshape(capacity), a_col.reshape(capacity),
         a_slot.reshape(branches * capacity), a_count.reshape(1), panel2,
-        meta_all.reshape(row_devices * item_count, TAP + 2), group_rows
+        rows_dev * row_devices, branches, group_rows
     )
     ap_rows = lax.psum_scatter(
         partial_value.reshape(group_rows, TAP, HALF, LANES), "col", scatter_dimension=0, tiled=True
@@ -186,7 +184,7 @@
     source = jnp.where(
         jnp.any(hit, axis=1), jnp.sum(jnp.where(hit, serial[None, :], 0), axis=1), item_count
     )
-    outgoing = contributions(source, p2.reshape(item_count, HALF, LANES), ap_rows, slots_total)
+    outgoing = contributions(source, p2, ap_rows, slots_total)
     incoming = lax.all_to_all(outgoing, "row", split_axis=0, concat_axis=0, tiled=True)
 
     me = lax.axis_index("row").astype(jnp.float32)

time: 302 us -> 302 us (level)
  blocking collectives: 25.2 us -> 0 us
  waiting for transfers between devices: 137 us -> 153 us
  local copies, waits for them, and re-layouts: 50.8 us -> 56.8 us
    all_gather x1 -> x0, blocking collectives: 25.2 us -> none  [on_device(): meta_all = lax.all_gather(meta_local, 'row', axis=0, tiled=False)]
    all_gather x1, waiting for transfers between devices: 0.02 us -> 22.8 us  [on_device(): panel2 = lax.all_gather(sent, 'row', axis=0, tiled=True)]
    all_to_all x1, waiting for transfers between devices: 41.7 us -> 32.7 us  [on_device(): lax.all_to_all(outgoing, 'row', split_axis=0, concat_axis=0, tiled=True)]
    reshape x1 -> x6, local copies, waits for them, and re-layouts: 0.77 us -> 8.42 us  [the longest x1 7.88 us: on_device(): panel2.reshape(row_devices, item_count + 1, tile_len)]
    unnamed x10 -> x8, local copies, waits for them, and re-layouts: 13.5 us -> 12.7 us
  transfers between devices with their start and end apart: 4 -> 4, of which waited for: 3 -> 4; matrix products, arithmetic and copies ran while one was open for 16% -> 17% of each run, Pallas kernels for 0% -> 0%
where the time goes in v7:
time: 302 us; the launch traced here: 300 us
  waiting for transfers between devices  153 us (51%)
  Pallas kernels  60.8 us (20%)
  local copies, waits for them, and re-layouts  56.8 us (19%)
  between operations  13.9 us (5%)
  starting transfers between devices  7.21 us (2%)
  matrix products  5.79 us (2%)
    reduce_scatter x1, waiting for transfers between devices, on_device(): lax.psum_scatter(partial_value.reshape(group_rows, TAP, HALF, LANES), 'co...  55.6 us
    reduce_scatter x1, waiting for transfers between devices, on_device(): lax.psum_scatter(coarse_part.reshape(col_devices, TC, HALF, LANES), 'col'...  41.4 us
    pallas_call x1, Pallas kernels, ap_partial(): pl.pallas_call(ap_kernel, out_shape=jax.ShapeDtypeStruct((out_rows * TAP,...  41.1 us
    all_to_all x1, waiting for transfers between devices, on_device(): lax.all_to_all(outgoing, 'row', split_axis=0, concat_axis=0, tiled=True)  32.7 us
    all_gather x1, waiting for transfers between devices, on_device(): panel2 = lax.all_gather(sent, 'row', axis=0, tiled=True)  22.8 us
    reshape x2, local copies, waits for them, and re-layouts, on_device(): a_vals.reshape(capacity, BLOCK, HALF, 2).transpose(0, 1, 3, 2)  22.8 us
    pallas_call x1, Pallas kernels, contributions(): pl.pallas_call(contrib_kernel, out_shape=jax.ShapeDtypeStruct((slots, TAP...  19.7 us
    unnamed x8, local copies, waits for them, and re-layouts  12.7 us
  transfers between devices with their start and end apart: 4, of which 4 were waited for; matrix products, arithmetic and copies ran while one was open for 17% of the time, Pallas kernels for 0%

profile of v7, /device:TPU:0, one launch (start us, length us, event | category | flops | bytes accessed | tf_op | source)
XLA Modules:
  0.0 299.9 jit_solution(17522446372689448670)
XLA Ops:
  6.5 0.0 all-gather.2.cloned.1.call-start
  6.5 0.8 copy.78
  7.3 1.3 copy.77
  8.6 0.3 reshape.117.p2_ref
  8.9 0.0 copy-start
  8.9 0.9 copy.80
  9.7 0.1 reshape.120
  9.8 0.8 copy.79
  10.6 0.1 reshape.119
  10.7 0.1 reshape.118
  10.8 0.1 copy.81
  10.8 0.1 convert_element_type.24
  10.9 0.8 pad_maximum_fusion
  11.7 0.0 all-gather.2.cloned.1.call-update
  11.7 0.0 reduce-scatter.3.cloned.1.call-start
  11.8 0.7 reduce
  12.5 0.7 reshape.126.slots_ref
  13.8 9.0 %copy.87 = f32[1,1,448,4096]{2,3,1,0:T(8,128)} copy(f32[1,1,448,4096]{3,2,1,0:T(8,128)} %param.9) | data formatting | bytes 14680064 | tf_op args[0]
  22.8 10.8 %reshape.128 = f32[448,64,32,2]{0,3,2,1:T(2,128)} reshape(f32[1,1,448,4096]{2,3,1,0:T(8,128)} %copy.87) | data formatting | bytes 14680064 | tf_op jit(solution)/shard_map/reshape | solution.py:167
  33.6 8.6 %copy.88 = f32[448,64,2,32]{0,3,2,1:T(8,128)} copy(f32[448,64,2,32]{0,2,3,1:T(2,128)} %bitcast.30) | data formatting | bytes 14680064 | tf_op jit(solution)/shard_map/transpose | solution.py:167
  42.2 11.9 %copy.89.a_ref = f32[448,64,64]{2,1,0:T(8,128)} copy(f32[448,64,64]{0,2,1:T(8,128)} %bitcast.31) | data formatting | bytes 14680064 | tf_op jit(solution)/shard_map/reshape | solution.py:167
  54.2 22.8 %all-gather.2.cloned.1.call-done.p2_ref = f32[400,32,128]{2,1,0:T(8,128)} async-done(((f32[25,32,128]{2,1,0:T(8,128)}), f32[400,32,128]{2,1,0:T(8,128)}) %all-gather.2.cloned.1.call-update) | async-done | bytes 6553616 | tf_op jit(solution)/shard_map/all_gather | solution.py:164
  77.0 41.1 %shard_map.91 = f32[384,32,128]{2,1,0:T(8,128)} custom-call(s32[448]{0:T(512)} %bitcast.37, s32[448]{0:T(512)} %bitcast.38, s32[1344]{0:T(1024)} %reshape.126.slots_ref, s32[1]{0:T(128)} %bitcast.29.cnt_ref, f32[448,64,64]{2,1,0:T(8,128)} %copy.89.a_ref, f32[400,32,128]{2,1,0:T(8,128)} %all-gather.2.cloned.1.call-done.p2_ref), custom_call_target="tpu_custom_call" | custom-call | tf_op jit(solution)/shard_map/pallas_call | solution.py:92
  118.2 0.0 reduce-scatter.3.cloned.1.call-update
  118.2 0.1 reshape.123
  118.3 0.2 convert_reduce_fusion
  118.4 0.1 fusion.8
  118.5 0.1 select_reduce_fusion.1
  118.6 0.5 broadcast_select_fusion.1.src_ref
  119.2 55.6 %reduce-scatter.3.cloned.1.call-done.ap2_ref = f32[8,6,32,128]{3,2,1,0:T(8,128)} async-done(((f32[64,6,32,128]{3,2,1,0:T(8,128)}), f32[8,6,32,128]{3,2,1,0:T(8,128)}) %reduce-scatter.3.cloned.1.call-update) | async-done | bytes 786448 | tf_op jit(solution)/shard_map/reduce_scatter | solution.py:174
  174.8 19.7 %shard_map.92 = f32[32,6,32,128]{3,2,1,0:T(8,128)} custom-call(s32[32]{0:T(128)} %broadcast_select_fusion.1.src_ref, f32[24,32,128]{2,1,0:T(8,128)} %copy-done, f32[8,6,32,128]{3,2,1,0:T(8,128)} %reduce-scatter.3.cloned.1.call-done.ap2_ref), custom_call_target="tpu_custom_call" | custom-call | tf_op jit(solution)/shard_map/pallas_call | solution.py:129
  194.5 6.9 %all-to-all-start = ((f32[32,6,32,128]{3,2,1,0:T(8,128)}), f32[32,6,32,128]{3,2,1,0:T(8,128)S(1)}, u32[]{:S(2)}, u32[]{:S(2)}) async-start(f32[32,6,32,128]{3,2,1,0:T(8,128)} %shard_map.92), calls=%async_computation.1 | async-start | bytes 6291456 | tf_op jit(solution)/shard_map/all_to_all | solution.py:188
  201.4 0.2 reduce-scatter.5.cloned.1.call-start
  201.7 7.9 %reshape.122 = f32[16,25,4096]{2,1,0:T(8,128)} reshape(f32[400,32,128]{2,1,0:T(8,128)} %all-gather.2.cloned.1.call-done.p2_ref) | data formatting | bytes 13107200 | tf_op jit(solution)/shard_map/reshape | solution.py:165
  209.5 0.9 slice.16
  210.5 0.1 copy.82
  210.6 0.1 copy.84
  210.7 0.1 copy.93
  210.8 0.2 reduce_window_sum.11
  211.0 0.1 fusion.10
  211.1 0.1 select_reduce_fusion
  211.2 0.1 copy.85
  211.3 0.1 select_n.25
  211.4 32.7 %all-to-all-done = f32[32,6,32,128]{3,2,1,0:T(8,128)S(1)} async-done(((f32[32,6,32,128]{3,2,1,0:T(8,128)}), f32[32,6,32,128]{3,2,1,0:T(8,128)S(1)}, u32[]{:S(2)}, u32[]{:S(2)}) %all-to-all-start) | async-done | bytes 3145760 | tf_op jit(solution)/shard_map/all_to_all | solution.py:188
  244.1 5.8 %fusion = f32[8,27,32,128]{3,1,2,0:T(8,128)} fusion(f32[192,32,128]{2,1,0:T(8,128)S(1)} %bitcast.33, f32[8,27]{1,0:T(8,128)S(1)} %multiply_add_fusion, f32[192]{0:T(256)S(1)} %select_n.25), kind=kOutput, calls=%fused_computation | convolution fusion | flops 2038473216 | bytes 6686304 | tf_op jit(solution)/shard_map/ec,eml->cml/dot_general | solution.py:204
  249.9 0.0 reduce-scatter.5.cloned.1.call-update
  249.9 41.4 %reduce-scatter.5.cloned.1.call-done = f32[1,27,32,128]{3,1,2,0:T(8,128)} async-done(((f32[8,27,32,128]{3,1,2,0:T(8,128)}), f32[1,27,32,128]{3,1,2,0:T(8,128)}) %reduce-scatter.5.cloned.1.call-update) | async-done | bytes 442384 | tf_op jit(solution)/shard_map/reduce_scatter | solution.py:206
  291.3 2.1 copy.91
  (10 shorter events, 0.1 us)
Async XLA Ops:
  6.5 70.5 %all-gather.2.cloned.1.call-start = ((), (), s32[]{:S(2)}) async-start(), calls=%async_computation.3 | async-start | bytes 6963200 | tf_op jit(solution)/shard_map/all_gather | solution.py:164
  8.9 13.9 %copy-start = (f32[24,32,128]{2,1,0:T(8,128)}, f32[24,32,128]{2,1,0:T(8,128)S(1)}, u32[]{:S(2)}) copy-start(f32[24,32,128]{2,1,0:T(8,128)S(1)} %reshape.117.p2_ref) | copy-start | bytes 1179652
  11.7 163.0 %reduce-scatter.3.cloned.1.call-start = ((), (), s32[]{:S(2)}) async-start(), calls=%async_computation.4 | async-start | bytes 7077888 | tf_op jit(solution)/shard_map/reduce_scatter | solution.py:174
  194.5 49.6 %all-to-all-start = ((f32[32,6,32,128]{3,2,1,0:T(8,128)}), f32[32,6,32,128]{3,2,1,0:T(8,128)S(1)}, u32[]{:S(2)}, u32[]{:S(2)}) async-start(f32[32,6,32,128]{3,2,1,0:T(8,128)} %shard_map.92), calls=%async_computation.1 | async-start | bytes 6291456 | tf_op jit(solution)/shard_map/all_to_all | solution.py:188
  201.4 89.9 %reduce-scatter.5.cloned.1.call-start = ((), (), s32[]{:S(2)}) async-start(), calls=%async_computation.5 | async-start | bytes 4718592 | tf_op jit(solution)/shard_map/reduce_scatter | solution.py:206
Sparse Core Ops, SparseCore 0:
  11.9 65.1 all-gather.1
  118.3 56.4 reduce-scatter.2
  250.0 41.2 reduce-scatter.4

commit v8 on v7

--- a/solution.py
+++ b/solution.py
@@ -110,16 +110,21 @@
 
     def body(e, carry):
         item = src_ref[e]
-        live = item < items
-        it = jnp.minimum(item, items - 1)
-        left = unpack(p2_ref[it]).T
-        for q in range(TAP):
-            right = unpack(ap2_ref[it // branches, q])
-            prod = jnp.dot(left, right, preferred_element_type=jnp.float32, precision=highest)
-            scr[...] = jnp.where(live, prod, 0.0)
-            even = scr[pl.ds(0, HALF, stride=2), :]
-            odd = scr[pl.ds(1, HALF, stride=2), :]
-            o_ref[e, q] = jnp.concatenate([even, odd], axis=1)
+
+        @pl.when(item < items)
+        def _():
+            left = unpack(p2_ref[item]).T
+            for q in range(TAP):
+                right = unpack(ap2_ref[item // branches, q])
+                scr[...] = jnp.dot(left, right, preferred_element_type=jnp.float32, precision=highest)
+                even = scr[pl.ds(0, HALF, stride=2), :]
+                odd = scr[pl.ds(1, HALF, stride=2), :]
+                o_ref[e, q] = jnp.concatenate([even, odd], axis=1)
+
+        @pl.when(item >= items)
+        def _():
+            o_ref[e] = jnp.zeros(o_ref.shape[1:], o_ref.dtype)
+
         return carry
 
     lax.fori_loop(0, slots, body, 0)
@@ -184,8 +189,12 @@
     source = jnp.where(
         jnp.any(hit, axis=1), jnp.sum(jnp.where(hit, serial[None, :], 0), axis=1), item_count
     )
-    outgoing = contributions(source, p2, ap_rows, slots_total)
-    incoming = lax.all_to_all(outgoing, "row", split_axis=0, concat_axis=0, tiled=True)
+    by_rank = source.reshape(row_devices, per_peer)
+    incoming = []
+    for k in range(per_peer):
+        outgoing = contributions(by_rank[:, k], p2, ap_rows, row_devices)
+        incoming.append(lax.all_to_all(outgoing, "row", split_axis=0, concat_axis=0, tiled=True))
+    incoming = jnp.stack(incoming, axis=1)
 
     me = lax.axis_index("row").astype(jnp.float32)
     meta_all = meta_all.reshape(row_devices, item_count, TAP + 2)

time: 302 us -> 294 us (0.974)
  waiting for transfers between devices: 153 us -> 127 us
  Pallas kernels: 60.8 us -> 75 us
  starting transfers between devices: 7.21 us -> 10.9 us
    pallas_call x1, Pallas kernels: 41.1 us -> 56.7 us  [ap_partial(): pl.pallas_call(ap_kernel, out_shape=jax.ShapeDtypeStruct((out_rows * TAP,...]
    reduce_scatter x1, waiting for transfers between devices: 55.6 us -> 40.6 us  [on_device(): lax.psum_scatter(partial_value.reshape(group_rows, TAP, HALF, LANES), 'co...]
    all_to_all x1 -> x2, waiting for transfers between devices: 32.7 us -> 22.7 us  [on_device(): lax.all_to_all(outgoing, 'row', split_axis=0, concat_axis=0, tiled=True)]
    all_to_all x1 -> x2, starting transfers between devices: 6.94 us -> 10.6 us  [on_device(): lax.all_to_all(outgoing, 'row', split_axis=0, concat_axis=0, tiled=True)]
    pallas_call x1 -> x2, Pallas kernels: 19.7 us -> 18.4 us  [contributions(): pl.pallas_call(contrib_kernel, out_shape=jax.ShapeDtypeStruct((slots, TAP...]
    unnamed x8 -> x10, local copies, waits for them, and re-layouts: 12.7 us -> 12.7 us
  transfers between devices with their start and end apart: 4 -> 5, of which waited for: 4 -> 5; matrix products, arithmetic and copies ran while one was open for 17% -> 18% of each run, Pallas kernels for 0% -> 4%
where the time goes in v8:
time: 294 us; the launch traced here: 293 us
  waiting for transfers between devices  127 us (43%)
  Pallas kernels  75 us (26%)
  local copies, waits for them, and re-layouts  58.1 us (20%)
  between operations  13.9 us (5%)
  starting transfers between devices  10.9 us (4%)
  matrix products  5.81 us (2%)
    pallas_call x1, Pallas kernels, ap_partial(): pl.pallas_call(ap_kernel, out_shape=jax.ShapeDtypeStruct((out_rows * TAP,...  56.7 us
    reduce_scatter x1, waiting for transfers between devices, on_device(): lax.psum_scatter(partial_value.reshape(group_rows, TAP, HALF, LANES), 'co...  40.6 us
    reduce_scatter x1, waiting for transfers between devices, on_device(): lax.psum_scatter(coarse_part.reshape(col_devices, TC, HALF, LANES), 'col'...  40.3 us
    all_gather x1, waiting for transfers between devices, on_device(): panel2 = lax.all_gather(sent, 'row', axis=0, tiled=True)  23.6 us
    reshape x2, local copies, waits for them, and re-layouts, on_device(): a_vals.reshape(capacity, BLOCK, HALF, 2).transpose(0, 1, 3, 2)  22.8 us
    all_to_all x2, waiting for transfers between devices, on_device(): lax.all_to_all(outgoing, 'row', split_axis=0, concat_axis=0, tiled=True)  22.7 us
    pallas_call x2, Pallas kernels, contributions(): pl.pallas_call(contrib_kernel, out_shape=jax.ShapeDtypeStruct((slots, TAP...  18.4 us
    unnamed x10, local copies, waits for them, and re-layouts  12.7 us
  transfers between devices with their start and end apart: 5, of which 5 were waited for; matrix products, arithmetic and copies ran while one was open for 18% of the time, Pallas kernels for 4%

profile of v8, /device:TPU:0, one launch (start us, length us, event | category | flops | bytes accessed | tf_op | source)
XLA Modules:
  0.0 292.9 jit_solution(7972839485504499627)
XLA Ops:
  6.5 0.8 copy.81
  7.3 1.3 copy.80
  8.6 0.3 reshape.122.p2_ref
  8.9 0.9 copy.83
  9.8 0.1 reshape.125
  9.8 0.8 copy.82
  10.6 0.1 reshape.124
  10.7 0.1 reshape.123
  10.8 0.1 copy.84
  10.8 0.1 convert_element_type.24
  10.9 0.8 pad_maximum_fusion.1
  11.8 0.0 reduce-scatter.3.cloned.1.call-start
  11.8 0.7 reshape.131.slots_ref
  13.2 9.0 %copy.90 = f32[1,1,448,4096]{2,3,1,0:T(8,128)} copy(f32[1,1,448,4096]{3,2,1,0:T(8,128)} %param.9) | data formatting | bytes 14680064 | tf_op args[0]
  22.1 10.9 %reshape.133 = f32[448,64,32,2]{0,3,2,1:T(2,128)} reshape(f32[1,1,448,4096]{2,3,1,0:T(8,128)} %copy.90) | data formatting | bytes 14680064 | tf_op jit(solution)/shard_map/reshape | solution.py:172
  33.0 8.6 %copy.91 = f32[448,64,2,32]{0,3,2,1:T(8,128)} copy(f32[448,64,2,32]{0,2,3,1:T(2,128)} %bitcast.32) | data formatting | bytes 14680064 | tf_op jit(solution)/shard_map/transpose | solution.py:172
  41.6 11.9 %copy.92.a_ref = f32[448,64,64]{2,1,0:T(8,128)} copy(f32[448,64,64]{0,2,1:T(8,128)} %bitcast.33) | data formatting | bytes 14680064 | tf_op jit(solution)/shard_map/reshape | solution.py:172
  53.5 23.6 %all-gather.2.cloned.1.call-done.p2_ref = f32[400,32,128]{2,1,0:T(8,128)} async-done(((f32[25,32,128]{2,1,0:T(8,128)}), f32[400,32,128]{2,1,0:T(8,128)}) %all-gather.2.cloned.1.call-update) | async-done | bytes 6553616 | tf_op jit(solution)/shard_map/all_gather | solution.py:169
  77.0 56.7 %shard_map.91 = f32[384,32,128]{2,1,0:T(8,128)} custom-call(s32[448]{0:T(512)} %bitcast.41, s32[448]{0:T(512)} %bitcast.42, s32[1344]{0:T(1024)} %reshape.131.slots_ref, s32[1]{0:T(128)} %bitcast.31.cnt_ref, f32[448,64,64]{2,1,0:T(8,128)} %copy.92.a_ref, f32[400,32,128]{2,1,0:T(8,128)} %all-gather.2.cloned.1.call-done.p2_ref), custom_call_target="tpu_custom_call" | custom-call | tf_op jit(solution)/shard_map/pallas_call | solution.py:92
  133.7 0.1 reshape.128
  133.8 0.2 convert_reduce_fusion
  134.0 0.1 fusion.8
  134.1 0.1 select_reduce_fusion.1
  134.2 0.1 select_n.32
  134.3 0.8 slice_reduce_fusion.1
  135.0 40.6 %reduce-scatter.3.cloned.1.call-done.ap2_ref = f32[8,6,32,128]{3,2,1,0:T(8,128)} async-done(((f32[64,6,32,128]{3,2,1,0:T(8,128)}), f32[8,6,32,128]{3,2,1,0:T(8,128)}) %reduce-scatter.3.cloned.1.call-update) | async-done | bytes 786448 | tf_op jit(solution)/shard_map/reduce_scatter | solution.py:179
  175.7 7.2 %shard_map.93 = f32[16,6,32,128]{3,2,1,0:T(8,128)} custom-call(s32[16]{0:T(128)} %get-tuple-element.6.src_ref, f32[24,32,128]{2,1,0:T(8,128)} %copy-done, f32[8,6,32,128]{3,2,1,0:T(8,128)} %reduce-scatter.3.cloned.1.call-done.ap2_ref), custom_call_target="tpu_custom_call" | custom-call | tf_op jit(solution)/shard_map/pallas_call | solution.py:134
  182.9 6.9 %all-to-all-start.1 = ((f32[16,6,32,128]{3,2,1,0:T(8,128)}), f32[16,6,32,128]{3,2,1,0:T(8,128)S(1)}, u32[]{:S(2)}, u32[]{:S(2)}) async-start(f32[16,6,32,128]{3,2,1,0:T(8,128)} %shard_map.93), calls=%async_computation.2 | async-start | bytes 3145728 | tf_op jit(solution)/shard_map/all_to_all | solution.py:196
  189.8 11.2 %shard_map.92 = f32[16,6,32,128]{3,2,1,0:T(8,128)} custom-call(s32[16]{0:T(128)} %get-tuple-element.5.src_ref, f32[24,32,128]{2,1,0:T(8,128)} %copy-done, f32[8,6,32,128]{3,2,1,0:T(8,128)} %reduce-scatter.3.cloned.1.call-done.ap2_ref), custom_call_target="tpu_custom_call" | custom-call | tf_op jit(solution)/shard_map/pallas_call | solution.py:134
  201.0 12.1 %all-to-all-done.1 = f32[16,6,32,128]{3,2,1,0:T(8,128)S(1)} async-done(((f32[16,6,32,128]{3,2,1,0:T(8,128)}), f32[16,6,32,128]{3,2,1,0:T(8,128)S(1)}, u32[]{:S(2)}, u32[]{:S(2)}) %all-to-all-start.1) | async-done | bytes 1572896 | tf_op jit(solution)/shard_map/all_to_all | solution.py:196
  213.1 3.7 %all-to-all-start = ((f32[16,6,32,128]{3,2,1,0:T(8,128)}), f32[16,6,32,128]{3,2,1,0:T(8,128)S(1)}, u32[]{:S(2)}, u32[]{:S(2)}) async-start(f32[16,6,32,128]{3,2,1,0:T(8,128)} %shard_map.92), calls=%async_computation.1 | async-start | bytes 3145728 | tf_op jit(solution)/shard_map/all_to_all | solution.py:196
  216.8 0.2 reduce-scatter.5.cloned.1.call-start
  217.0 7.9 %reshape.127 = f32[16,25,4096]{2,1,0:T(8,128)} reshape(f32[400,32,128]{2,1,0:T(8,128)} %all-gather.2.cloned.1.call-done.p2_ref) | data formatting | bytes 13107200 | tf_op jit(solution)/shard_map/reshape | solution.py:170
  224.9 0.9 slice.24
  225.8 0.1 copy.85
  226.0 0.1 copy.87
  226.1 0.1 copy.97
  226.1 0.2 reduce_window_sum.11
  226.3 0.1 fusion.10
  226.4 0.1 select_reduce_fusion
  226.6 0.1 copy.88
  226.7 0.1 select_n.29
  226.8 10.6 %all-to-all-done = f32[16,6,32,128]{3,2,1,0:T(8,128)S(1)} async-done(((f32[16,6,32,128]{3,2,1,0:T(8,128)}), f32[16,6,32,128]{3,2,1,0:T(8,128)S(1)}, u32[]{:S(2)}, u32[]{:S(2)}) %all-to-all-start) | async-done | bytes 1572896 | tf_op jit(solution)/shard_map/all_to_all | solution.py:196
  237.4 0.3 pad_maximum_fusion
  237.7 0.5 copy.93
  238.2 5.8 %fusion = f32[8,27,32,128]{3,1,2,0:T(8,128)} fusion(f32[192,32,128]{2,1,0:T(8,128)S(1)} %bitcast.35, f32[8,27]{1,0:T(8,128)S(1)} %multiply_add_fusion, f32[192]{0:T(256)S(1)} %select_n.29), kind=kOutput, calls=%fused_computation.1 | convolution fusion | flops 2038473216 | bytes 6686304 | tf_op jit(solution)/shard_map/ec,eml->cml/dot_general | solution.py:213
  244.0 40.3 %reduce-scatter.5.cloned.1.call-done = f32[1,27,32,128]{3,1,2,0:T(8,128)} async-done(((f32[8,27,32,128]{3,1,2,0:T(8,128)}), f32[1,27,32,128]{3,1,2,0:T(8,128)}) %reduce-scatter.5.cloned.1.call-update) | async-done | bytes 442384 | tf_op jit(solution)/shard_map/reduce_scatter | solution.py:215
  284.3 2.1 copy.95
  (19 shorter events, 0.2 us)
Async XLA Ops:
  6.5 5.3 %copy-start.1 = (s32[1,1,3,448]{3,1,2,0:T(1,128)S(1)}, s32[1,1,3,448]{3,1,2,0:T(1,128)}, u32[]{:S(2)}) copy-start(s32[1,1,3,448]{3,1,2,0:T(1,128)} %param.12) | copy-start | bytes 16132
  6.5 70.5 %all-gather.2.cloned.1.call-start = ((), (), s32[]{:S(2)}) async-start(), calls=%async_computation.4 | async-start | bytes 6963200 | tf_op jit(solution)/shard_map/all_gather | solution.py:169
  8.9 13.2 %copy-start = (f32[24,32,128]{2,1,0:T(8,128)}, f32[24,32,128]{2,1,0:T(8,128)S(1)}, u32[]{:S(2)}) copy-start(f32[24,32,128]{2,1,0:T(8,128)S(1)} %reshape.122.p2_ref) | copy-start | bytes 1179652
  11.8 163.9 %reduce-scatter.3.cloned.1.call-start = ((), (), s32[]{:S(2)}) async-start(), calls=%async_computation.5 | async-start | bytes 7077888 | tf_op jit(solution)/shard_map/reduce_scatter | solution.py:179
  182.9 30.2 %all-to-all-start.1 = ((f32[16,6,32,128]{3,2,1,0:T(8,128)}), f32[16,6,32,128]{3,2,1,0:T(8,128)S(1)}, u32[]{:S(2)}, u32[]{:S(2)}) async-start(f32[16,6,32,128]{3,2,1,0:T(8,128)} %shard_map.93), calls=%async_computation.2 | async-start | bytes 3145728 | tf_op jit(solution)/shard_map/all_to_all | solution.py:196
  213.1 24.3 %all-to-all-start = ((f32[16,6,32,128]{3,2,1,0:T(8,128)}), f32[16,6,32,128]{3,2,1,0:T(8,128)S(1)}, u32[]{:S(2)}, u32[]{:S(2)}) async-start(f32[16,6,32,128]{3,2,1,0:T(8,128)} %shard_map.92), calls=%async_computation.1 | async-start | bytes 3145728 | tf_op jit(solution)/shard_map/all_to_all | solution.py:196
  216.8 67.5 %reduce-scatter.5.cloned.1.call-start = ((), (), s32[]{:S(2)}) async-start(), calls=%async_computation.6 | async-start | bytes 4718592 | tf_op jit(solution)/shard_map/reduce_scatter | solution.py:215
Sparse Core Ops, SparseCore 0:
  11.9 65.1 all-gather.1
  133.8 41.7 reduce-scatter.2
  244.1 40.1 reduce-scatter.4

commit v9 on v8

--- a/solution.py
+++ b/solution.py
@@ -47,7 +47,7 @@
         row = rows_ref[t]
         for s in range(branches):
             prod = jnp.dot(
-                a, p_scr[col, s], preferred_element_type=jnp.float32, precision=highest
+                a, p_scr[col, s], preferred_element_type=jnp.float32, precision=lax.Precision.HIGH
             )
             idx = row * TAP + slots_ref[s * capacity + t]
             acc[idx] += jnp.where(live, prod, 0.0)

time: 294 us -> 277 us (0.942)
  Pallas kernels: 75 us -> 58.1 us
    pallas_call x1, Pallas kernels: 56.7 us -> 39.7 us  [ap_partial(): pl.pallas_call(ap_kernel, out_shape=jax.ShapeDtypeStruct((out_rows * TAP,...]
  transfers between devices with their start and end apart: 5 -> 5, of which waited for: 5 -> 5; matrix products, arithmetic and copies ran while one was open for 18% -> 19% of each run, Pallas kernels for 4% -> 4%
where the time goes in v9:
time: 277 us; the launch traced here: 276 us
  waiting for transfers between devices  127 us (46%)
  local copies, waits for them, and re-layouts  58.1 us (21%)
  Pallas kernels  58.1 us (21%)
  between operations  13.9 us (5%)
  starting transfers between devices  10.9 us (4%)
  matrix products  5.81 us (2%)
    reduce_scatter x1, waiting for transfers between devices, on_device(): lax.psum_scatter(partial_value.reshape(group_rows, TAP, HALF, LANES), 'co...  40.6 us
    reduce_scatter x1, waiting for transfers between devices, on_device(): lax.psum_scatter(coarse_part.reshape(col_devices, TC, HALF, LANES), 'col'...  40.3 us
    pallas_call x1, Pallas kernels, ap_partial(): pl.pallas_call(ap_kernel, out_shape=jax.ShapeDtypeStruct((out_rows * TAP,...  39.7 us
    all_gather x1, waiting for transfers between devices, on_device(): panel2 = lax.all_gather(sent, 'row', axis=0, tiled=True)  23.6 us
    reshape x2, local copies, waits for them, and re-layouts, on_device(): a_vals.reshape(capacity, BLOCK, HALF, 2).transpose(0, 1, 3, 2)  22.8 us
    all_to_all x2, waiting for transfers between devices, on_device(): lax.all_to_all(outgoing, 'row', split_axis=0, concat_axis=0, tiled=True)  22.7 us
    pallas_call x2, Pallas kernels, contributions(): pl.pallas_call(contrib_kernel, out_shape=jax.ShapeDtypeStruct((slots, TAP...  18.4 us
    unnamed x10, local copies, waits for them, and re-layouts  12.7 us
  transfers between devices with their start and end apart: 5, of which 5 were waited for; matrix products, arithmetic and copies ran while one was open for 19% of the time, Pallas kernels for 4%

profile of v9, /device:TPU:0, one launch (start us, length us, event | category | flops | bytes accessed | tf_op | source)
XLA Modules:
  0.0 275.9 jit_solution(13746668888854144065)
XLA Ops:
  6.5 0.8 copy.81
  7.3 1.3 copy.80
  8.6 0.3 reshape.122.p2_ref
  8.9 0.9 copy.83
  9.8 0.1 reshape.125
  9.8 0.8 copy.82
  10.6 0.1 reshape.124
  10.7 0.1 reshape.123
  10.8 0.1 copy.84
  10.8 0.1 convert_element_type.24
  10.9 0.8 pad_maximum_fusion.1
  11.8 0.0 reduce-scatter.3.cloned.1.call-start
  11.8 0.7 reshape.131.slots_ref
  13.2 9.0 %copy.90 = f32[1,1,448,4096]{2,3,1,0:T(8,128)} copy(f32[1,1,448,4096]{3,2,1,0:T(8,128)} %param.9) | data formatting | bytes 14680064 | tf_op args[0]
  22.1 10.9 %reshape.133 = f32[448,64,32,2]{0,3,2,1:T(2,128)} reshape(f32[1,1,448,4096]{2,3,1,0:T(8,128)} %copy.90) | data formatting | bytes 14680064 | tf_op jit(solution)/shard_map/reshape | solution.py:172
  33.0 8.6 %copy.91 = f32[448,64,2,32]{0,3,2,1:T(8,128)} copy(f32[448,64,2,32]{0,2,3,1:T(2,128)} %bitcast.32) | data formatting | bytes 14680064 | tf_op jit(solution)/shard_map/transpose | solution.py:172
  41.6 11.9 %copy.92.a_ref = f32[448,64,64]{2,1,0:T(8,128)} copy(f32[448,64,64]{0,2,1:T(8,128)} %bitcast.33) | data formatting | bytes 14680064 | tf_op jit(solution)/shard_map/reshape | solution.py:172
  53.5 23.6 %all-gather.2.cloned.1.call-done.p2_ref = f32[400,32,128]{2,1,0:T(8,128)} async-done(((f32[25,32,128]{2,1,0:T(8,128)}), f32[400,32,128]{2,1,0:T(8,128)}) %all-gather.2.cloned.1.call-update) | async-done | bytes 6553616 | tf_op jit(solution)/shard_map/all_gather | solution.py:169
  77.0 39.7 %shard_map.91 = f32[384,32,128]{2,1,0:T(8,128)} custom-call(s32[448]{0:T(512)} %bitcast.41, s32[448]{0:T(512)} %bitcast.42, s32[1344]{0:T(1024)} %reshape.131.slots_ref, s32[1]{0:T(128)} %bitcast.31.cnt_ref, f32[448,64,64]{2,1,0:T(8,128)} %copy.92.a_ref, f32[400,32,128]{2,1,0:T(8,128)} %all-gather.2.cloned.1.call-done.p2_ref), custom_call_target="tpu_custom_call" | custom-call | tf_op jit(solution)/shard_map/pallas_call | solution.py:92
  116.8 0.1 reshape.128
  116.8 0.2 convert_reduce_fusion
  117.0 0.1 fusion.8
  117.1 0.1 select_reduce_fusion.1
  117.2 0.1 select_n.32
  117.3 0.8 slice_reduce_fusion.1
  118.1 40.6 %reduce-scatter.3.cloned.1.call-done.ap2_ref = f32[8,6,32,128]{3,2,1,0:T(8,128)} async-done(((f32[64,6,32,128]{3,2,1,0:T(8,128)}), f32[8,6,32,128]{3,2,1,0:T(8,128)}) %reduce-scatter.3.cloned.1.call-update) | async-done | bytes 786448 | tf_op jit(solution)/shard_map/reduce_scatter | solution.py:179
  158.7 7.2 %shard_map.93 = f32[16,6,32,128]{3,2,1,0:T(8,128)} custom-call(s32[16]{0:T(128)} %get-tuple-element.6.src_ref, f32[24,32,128]{2,1,0:T(8,128)} %copy-done, f32[8,6,32,128]{3,2,1,0:T(8,128)} %reduce-scatter.3.cloned.1.call-done.ap2_ref), custom_call_target="tpu_custom_call" | custom-call | tf_op jit(solution)/shard_map/pallas_call | solution.py:134
  165.9 6.9 %all-to-all-start.1 = ((f32[16,6,32,128]{3,2,1,0:T(8,128)}), f32[16,6,32,128]{3,2,1,0:T(8,128)S(1)}, u32[]{:S(2)}, u32[]{:S(2)}) async-start(f32[16,6,32,128]{3,2,1,0:T(8,128)} %shard_map.93), calls=%async_computation.2 | async-start | bytes 3145728 | tf_op jit(solution)/shard_map/all_to_all | solution.py:196
  172.8 11.2 %shard_map.92 = f32[16,6,32,128]{3,2,1,0:T(8,128)} custom-call(s32[16]{0:T(128)} %get-tuple-element.5.src_ref, f32[24,32,128]{2,1,0:T(8,128)} %copy-done, f32[8,6,32,128]{3,2,1,0:T(8,128)} %reduce-scatter.3.cloned.1.call-done.ap2_ref), custom_call_target="tpu_custom_call" | custom-call | tf_op jit(solution)/shard_map/pallas_call | solution.py:134
  184.0 12.1 %all-to-all-done.1 = f32[16,6,32,128]{3,2,1,0:T(8,128)S(1)} async-done(((f32[16,6,32,128]{3,2,1,0:T(8,128)}), f32[16,6,32,128]{3,2,1,0:T(8,128)S(1)}, u32[]{:S(2)}, u32[]{:S(2)}) %all-to-all-start.1) | async-done | bytes 1572896 | tf_op jit(solution)/shard_map/all_to_all | solution.py:196
  196.1 3.7 %all-to-all-start = ((f32[16,6,32,128]{3,2,1,0:T(8,128)}), f32[16,6,32,128]{3,2,1,0:T(8,128)S(1)}, u32[]{:S(2)}, u32[]{:S(2)}) async-start(f32[16,6,32,128]{3,2,1,0:T(8,128)} %shard_map.92), calls=%async_computation.1 | async-start | bytes 3145728 | tf_op jit(solution)/shard_map/all_to_all | solution.py:196
  199.8 0.2 reduce-scatter.5.cloned.1.call-start
  200.0 7.9 %reshape.127 = f32[16,25,4096]{2,1,0:T(8,128)} reshape(f32[400,32,128]{2,1,0:T(8,128)} %all-gather.2.cloned.1.call-done.p2_ref) | data formatting | bytes 13107200 | tf_op jit(solution)/shard_map/reshape | solution.py:170
  207.9 0.9 slice.24
  208.8 0.1 copy.85
  209.0 0.1 copy.87
  209.1 0.1 copy.97
  209.1 0.2 reduce_window_sum.11
  209.3 0.1 fusion.10
  209.5 0.1 select_reduce_fusion
  209.6 0.1 copy.88
  209.7 0.1 select_n.29
  209.8 10.6 %all-to-all-done = f32[16,6,32,128]{3,2,1,0:T(8,128)S(1)} async-done(((f32[16,6,32,128]{3,2,1,0:T(8,128)}), f32[16,6,32,128]{3,2,1,0:T(8,128)S(1)}, u32[]{:S(2)}, u32[]{:S(2)}) %all-to-all-start) | async-done | bytes 1572896 | tf_op jit(solution)/shard_map/all_to_all | solution.py:196
  220.4 0.3 pad_maximum_fusion
  220.7 0.5 copy.93
  221.2 5.8 %fusion = f32[8,27,32,128]{3,1,2,0:T(8,128)} fusion(f32[192,32,128]{2,1,0:T(8,128)S(1)} %bitcast.35, f32[8,27]{1,0:T(8,128)S(1)} %multiply_add_fusion, f32[192]{0:T(256)S(1)} %select_n.29), kind=kOutput, calls=%fused_computation.1 | convolution fusion | flops 2038473216 | bytes 6686304 | tf_op jit(solution)/shard_map/ec,eml->cml/dot_general | solution.py:213
  227.0 40.3 %reduce-scatter.5.cloned.1.call-done = f32[1,27,32,128]{3,1,2,0:T(8,128)} async-done(((f32[8,27,32,128]{3,1,2,0:T(8,128)}), f32[1,27,32,128]{3,1,2,0:T(8,128)}) %reduce-scatter.5.cloned.1.call-update) | async-done | bytes 442384 | tf_op jit(solution)/shard_map/reduce_scatter | solution.py:215
  267.3 2.1 copy.95
  (19 shorter events, 0.2 us)
Async XLA Ops:
  6.5 5.3 %copy-start.1 = (s32[1,1,3,448]{3,1,2,0:T(1,128)S(1)}, s32[1,1,3,448]{3,1,2,0:T(1,128)}, u32[]{:S(2)}) copy-start(s32[1,1,3,448]{3,1,2,0:T(1,128)} %param.12) | copy-start | bytes 16132
  6.5 70.5 %all-gather.2.cloned.1.call-start = ((), (), s32[]{:S(2)}) async-start(), calls=%async_computation.4 | async-start | bytes 6963200 | tf_op jit(solution)/shard_map/all_gather | solution.py:169
  8.9 13.2 %copy-start = (f32[24,32,128]{2,1,0:T(8,128)}, f32[24,32,128]{2,1,0:T(8,128)S(1)}, u32[]{:S(2)}) copy-start(f32[24,32,128]{2,1,0:T(8,128)S(1)} %reshape.122.p2_ref) | copy-start | bytes 1179652
  11.8 146.9 %reduce-scatter.3.cloned.1.call-start = ((), (), s32[]{:S(2)}) async-start(), calls=%async_computation.5 | async-start | bytes 7077888 | tf_op jit(solution)/shard_map/reduce_scatter | solution.py:179
  165.9 30.2 %all-to-all-start.1 = ((f32[16,6,32,128]{3,2,1,0:T(8,128)}), f32[16,6,32,128]{3,2,1,0:T(8,128)S(1)}, u32[]{:S(2)}, u32[]{:S(2)}) async-start(f32[16,6,32,128]{3,2,1,0:T(8,128)} %shard_map.93), calls=%async_computation.2 | async-start | bytes 3145728 | tf_op jit(solution)/shard_map/all_to_all | solution.py:196
  196.1 24.3 %all-to-all-start = ((f32[16,6,32,128]{3,2,1,0:T(8,128)}), f32[16,6,32,128]{3,2,1,0:T(8,128)S(1)}, u32[]{:S(2)}, u32[]{:S(2)}) async-start(f32[16,6,32,128]{3,2,1,0:T(8,128)} %shard_map.92), calls=%async_computation.1 | async-start | bytes 3145728 | tf_op jit(solution)/shard_map/all_to_all | solution.py:196
  199.8 67.6 %reduce-scatter.5.cloned.1.call-start = ((), (), s32[]{:S(2)}) async-start(), calls=%async_computation.6 | async-start | bytes 4718592 | tf_op jit(solution)/shard_map/reduce_scatter | solution.py:215
Sparse Core Ops, SparseCore 0:
  11.9 65.1 all-gather.1
  116.9 41.7 reduce-scatter.2
  227.1 40.1 reduce-scatter.4

commit v10 on v9

--- a/solution.py
+++ b/solution.py
@@ -13,7 +13,7 @@
 HALF = BLOCK * BLOCK // LANES
 
 highest = lax.Precision.HIGHEST
-chunk = 32
+chunk = 64
 
 
 def ap_kernel(rows_ref, cols_ref, slots_ref, cnt_ref, a_ref, p2_ref, o_ref, p_scr, acc):
@@ -116,7 +116,9 @@
             left = unpack(p2_ref[item]).T
             for q in range(TAP):
                 right = unpack(ap2_ref[item // branches, q])
-                scr[...] = jnp.dot(left, right, preferred_element_type=jnp.float32, precision=highest)
+                scr[...] = jnp.dot(
+                    left, right, preferred_element_type=jnp.float32, precision=lax.Precision.HIGH
+                )
                 even = scr[pl.ds(0, HALF, stride=2), :]
                 odd = scr[pl.ds(1, HALF, stride=2), :]
                 o_ref[e, q] = jnp.concatenate([even, odd], axis=1)
@@ -211,7 +213,7 @@
         dest_slot[:, None] == jnp.arange(group_coarse, dtype=jnp.float32)[None, :]
     ).astype(jnp.float32)
     coarse_part = jnp.einsum("ec,eml->cml", onehot, incoming.reshape(slots_total * TAP, HALF, LANES),
-                             precision=highest)
+                             precision=lax.Precision.HIGH)
     coarse = lax.psum_scatter(
         coarse_part.reshape(col_devices, TC, HALF, LANES), "col", scatter_dimension=0, tiled=True
     )

time: 277 us -> 274 us (0.989)
  Pallas kernels: 58.1 us -> 47.3 us
  waiting for transfers between devices: 127 us -> 136 us
    pallas_call x1, Pallas kernels: 39.7 us -> 30.8 us  [ap_partial(): pl.pallas_call(ap_kernel, out_shape=jax.ShapeDtypeStruct((out_rows * TAP,...]
    reduce_scatter x1, waiting for transfers between devices: 40.6 us -> 47.8 us  [on_device(): lax.psum_scatter(partial_value.reshape(group_rows, TAP, HALF, LANES), 'co...]
where the time goes in v10:
time: 274 us; the launch traced here: 273 us
  waiting for transfers between devices  136 us (50%)
  local copies, waits for them, and re-layouts  58.1 us (21%)
  Pallas kernels  47.3 us (17%)
  between operations  13.9 us (5%)
  starting transfers between devices  10.9 us (4%)
  matrix products  4.89 us (2%)
    reduce_scatter x1, waiting for transfers between devices, on_device(): lax.psum_scatter(partial_value.reshape(group_rows, TAP, HALF, LANES), 'co...  47.8 us
    reduce_scatter x1, waiting for transfers between devices, on_device(): lax.psum_scatter(coarse_part.reshape(col_devices, TC, HALF, LANES), 'col'...  40.4 us
    pallas_call x1, Pallas kernels, ap_partial(): pl.pallas_call(ap_kernel, out_shape=jax.ShapeDtypeStruct((out_rows * TAP,...  30.8 us
    all_to_all x2, waiting for transfers between devices, on_device(): lax.all_to_all(outgoing, 'row', split_axis=0, concat_axis=0, tiled=True)  23.9 us
    all_gather x1, waiting for transfers between devices, on_device(): panel2 = lax.all_gather(sent, 'row', axis=0, tiled=True)  23.6 us
    reshape x2, local copies, waits for them, and re-layouts, on_device(): a_vals.reshape(capacity, BLOCK, HALF, 2).transpose(0, 1, 3, 2)  22.8 us
    pallas_call x2, Pallas kernels, contributions(): pl.pallas_call(contrib_kernel, out_shape=jax.ShapeDtypeStruct((slots, TAP...  16.5 us
    unnamed x10, local copies, waits for them, and re-layouts  12.7 us
  transfers between devices with their start and end apart: 5, of which 5 were waited for; matrix products, arithmetic and copies ran while one was open for 19% of the time, Pallas kernels for 4%

profile of v10, /device:TPU:0, one launch (start us, length us, event | category | flops | bytes accessed | tf_op | source)
XLA Modules:
  0.0 272.7 jit_solution(5801230822216728169)
XLA Ops:
  6.5 0.8 copy.81
  7.3 1.3 copy.80
  8.6 0.3 reshape.122.p2_ref
  8.9 0.9 copy.83
  9.8 0.1 reshape.125
  9.8 0.8 copy.82
  10.6 0.1 reshape.124
  10.7 0.1 reshape.123
  10.8 0.1 copy.84
  10.8 0.1 convert_element_type.24
  10.9 0.8 pad_maximum_fusion.1
  11.8 0.0 reduce-scatter.3.cloned.1.call-start
  11.8 0.7 reshape.131.slots_ref
  13.2 9.0 %copy.90 = f32[1,1,448,4096]{2,3,1,0:T(8,128)} copy(f32[1,1,448,4096]{3,2,1,0:T(8,128)} %param.9) | data formatting | bytes 14680064 | tf_op args[0]
  22.1 10.9 %reshape.133 = f32[448,64,32,2]{0,3,2,1:T(2,128)} reshape(f32[1,1,448,4096]{2,3,1,0:T(8,128)} %copy.90) | data formatting | bytes 14680064 | tf_op jit(solution)/shard_map/reshape | solution.py:174
  33.0 8.6 %copy.91 = f32[448,64,2,32]{0,3,2,1:T(8,128)} copy(f32[448,64,2,32]{0,2,3,1:T(2,128)} %bitcast.32) | data formatting | bytes 14680064 | tf_op jit(solution)/shard_map/transpose | solution.py:174
  41.6 11.9 %copy.92.a_ref = f32[448,64,64]{2,1,0:T(8,128)} copy(f32[448,64,64]{0,2,1:T(8,128)} %bitcast.33) | data formatting | bytes 14680064 | tf_op jit(solution)/shard_map/reshape | solution.py:174
  53.5 23.6 %all-gather.2.cloned.1.call-done.p2_ref = f32[400,32,128]{2,1,0:T(8,128)} async-done(((f32[25,32,128]{2,1,0:T(8,128)}), f32[400,32,128]{2,1,0:T(8,128)}) %all-gather.2.cloned.1.call-update) | async-done | bytes 6553616 | tf_op jit(solution)/shard_map/all_gather | solution.py:171
  77.0 30.8 %shard_map.91 = f32[384,32,128]{2,1,0:T(8,128)} custom-call(s32[448]{0:T(512)} %bitcast.41, s32[448]{0:T(512)} %bitcast.42, s32[1344]{0:T(1024)} %reshape.131.slots_ref, s32[1]{0:T(128)} %bitcast.31.cnt_ref, f32[448,64,64]{2,1,0:T(8,128)} %copy.92.a_ref, f32[400,32,128]{2,1,0:T(8,128)} %all-gather.2.cloned.1.call-done.p2_ref), custom_call_target="tpu_custom_call" | custom-call | tf_op jit(solution)/shard_map/pallas_call | solution.py:92
  107.8 0.1 reshape.128
  107.9 0.2 convert_reduce_fusion
  108.1 0.1 fusion.8
  108.2 0.1 select_reduce_fusion.1
  108.3 0.1 select_n.32
  108.4 0.8 slice_reduce_fusion.1
  109.1 47.8 %reduce-scatter.3.cloned.1.call-done.ap2_ref = f32[8,6,32,128]{3,2,1,0:T(8,128)} async-done(((f32[64,6,32,128]{3,2,1,0:T(8,128)}), f32[8,6,32,128]{3,2,1,0:T(8,128)}) %reduce-scatter.3.cloned.1.call-update) | async-done | bytes 786448 | tf_op jit(solution)/shard_map/reduce_scatter | solution.py:181
  156.9 6.6 %shard_map.93 = f32[16,6,32,128]{3,2,1,0:T(8,128)} custom-call(s32[16]{0:T(128)} %get-tuple-element.6.src_ref, f32[24,32,128]{2,1,0:T(8,128)} %copy-done, f32[8,6,32,128]{3,2,1,0:T(8,128)} %reduce-scatter.3.cloned.1.call-done.ap2_ref), custom_call_target="tpu_custom_call" | custom-call | tf_op jit(solution)/shard_map/pallas_call | solution.py:136
  163.5 7.0 %all-to-all-start.1 = ((f32[16,6,32,128]{3,2,1,0:T(8,128)}), f32[16,6,32,128]{3,2,1,0:T(8,128)S(1)}, u32[]{:S(2)}, u32[]{:S(2)}) async-start(f32[16,6,32,128]{3,2,1,0:T(8,128)} %shard_map.93), calls=%async_computation.2 | async-start | bytes 3145728 | tf_op jit(solution)/shard_map/all_to_all | solution.py:198
  170.5 9.9 %shard_map.92 = f32[16,6,32,128]{3,2,1,0:T(8,128)} custom-call(s32[16]{0:T(128)} %get-tuple-element.5.src_ref, f32[24,32,128]{2,1,0:T(8,128)} %copy-done, f32[8,6,32,128]{3,2,1,0:T(8,128)} %reduce-scatter.3.cloned.1.call-done.ap2_ref), custom_call_target="tpu_custom_call" | custom-call | tf_op jit(solution)/shard_map/pallas_call | solution.py:136
  180.4 13.3 %all-to-all-done.1 = f32[16,6,32,128]{3,2,1,0:T(8,128)S(1)} async-done(((f32[16,6,32,128]{3,2,1,0:T(8,128)}), f32[16,6,32,128]{3,2,1,0:T(8,128)S(1)}, u32[]{:S(2)}, u32[]{:S(2)}) %all-to-all-start.1) | async-done | bytes 1572896 | tf_op jit(solution)/shard_map/all_to_all | solution.py:198
  193.7 3.7 %all-to-all-start = ((f32[16,6,32,128]{3,2,1,0:T(8,128)}), f32[16,6,32,128]{3,2,1,0:T(8,128)S(1)}, u32[]{:S(2)}, u32[]{:S(2)}) async-start(f32[16,6,32,128]{3,2,1,0:T(8,128)} %shard_map.92), calls=%async_computation.1 | async-start | bytes 3145728 | tf_op jit(solution)/shard_map/all_to_all | solution.py:198
  197.4 0.2 reduce-scatter.5.cloned.1.call-start
  197.7 7.9 %reshape.127 = f32[16,25,4096]{2,1,0:T(8,128)} reshape(f32[400,32,128]{2,1,0:T(8,128)} %all-gather.2.cloned.1.call-done.p2_ref) | data formatting | bytes 13107200 | tf_op jit(solution)/shard_map/reshape | solution.py:172
  205.6 0.9 slice.24
  206.5 0.1 copy.85
  206.6 0.1 copy.87
  206.7 0.1 copy.97
  206.8 0.2 reduce_window_sum.11
  207.0 0.1 fusion.10
  207.1 0.1 select_reduce_fusion
  207.2 0.1 copy.88
  207.3 0.1 select_n.29
  207.4 10.6 %all-to-all-done = f32[16,6,32,128]{3,2,1,0:T(8,128)S(1)} async-done(((f32[16,6,32,128]{3,2,1,0:T(8,128)}), f32[16,6,32,128]{3,2,1,0:T(8,128)S(1)}, u32[]{:S(2)}, u32[]{:S(2)}) %all-to-all-start) | async-done | bytes 1572896 | tf_op jit(solution)/shard_map/all_to_all | solution.py:198
  218.0 0.3 pad_maximum_fusion
  218.3 0.5 copy.93
  218.8 4.9 %fusion = f32[8,27,32,128]{3,1,2,0:T(8,128)} fusion(f32[192,32,128]{2,1,0:T(8,128)S(1)} %bitcast.35, f32[8,27]{1,0:T(8,128)S(1)} %multiply_add_fusion, f32[192]{0:T(256)S(1)} %select_n.29), kind=kOutput, calls=%fused_computation.1 | convolution fusion | flops 1019257344 | bytes 6686304 | tf_op jit(solution)/shard_map/ec,eml->cml/dot_general | solution.py:215
  223.7 40.4 %reduce-scatter.5.cloned.1.call-done = f32[1,27,32,128]{3,1,2,0:T(8,128)} async-done(((f32[8,27,32,128]{3,1,2,0:T(8,128)}), f32[1,27,32,128]{3,1,2,0:T(8,128)}) %reduce-scatter.5.cloned.1.call-update) | async-done | bytes 442384 | tf_op jit(solution)/shard_map/reduce_scatter | solution.py:217
  264.1 2.1 copy.95
  (19 shorter events, 0.2 us)
Async XLA Ops:
  6.5 5.3 %copy-start.1 = (s32[1,1,3,448]{3,1,2,0:T(1,128)S(1)}, s32[1,1,3,448]{3,1,2,0:T(1,128)}, u32[]{:S(2)}) copy-start(s32[1,1,3,448]{3,1,2,0:T(1,128)} %param.12) | copy-start | bytes 16132
  6.5 70.5 %all-gather.2.cloned.1.call-start = ((), (), s32[]{:S(2)}) async-start(), calls=%async_computation.4 | async-start | bytes 6963200 | tf_op jit(solution)/shard_map/all_gather | solution.py:171
  8.9 13.2 %copy-start = (f32[24,32,128]{2,1,0:T(8,128)}, f32[24,32,128]{2,1,0:T(8,128)S(1)}, u32[]{:S(2)}) copy-start(f32[24,32,128]{2,1,0:T(8,128)S(1)} %reshape.122.p2_ref) | copy-start | bytes 1179652
  11.8 145.2 %reduce-scatter.3.cloned.1.call-start = ((), (), s32[]{:S(2)}) async-start(), calls=%async_computation.5 | async-start | bytes 7077888 | tf_op jit(solution)/shard_map/reduce_scatter | solution.py:181
  163.5 30.2 %all-to-all-start.1 = ((f32[16,6,32,128]{3,2,1,0:T(8,128)}), f32[16,6,32,128]{3,2,1,0:T(8,128)S(1)}, u32[]{:S(2)}, u32[]{:S(2)}) async-start(f32[16,6,32,128]{3,2,1,0:T(8,128)} %shard_map.93), calls=%async_computation.2 | async-start | bytes 3145728 | tf_op jit(solution)/shard_map/all_to_all | solution.py:198
  193.7 24.3 %all-to-all-start = ((f32[16,6,32,128]{3,2,1,0:T(8,128)}), f32[16,6,32,128]{3,2,1,0:T(8,128)S(1)}, u32[]{:S(2)}, u32[]{:S(2)}) async-start(f32[16,6,32,128]{3,2,1,0:T(8,128)} %shard_map.92), calls=%async_computation.1 | async-start | bytes 3145728 | tf_op jit(solution)/shard_map/all_to_all | solution.py:198
  197.4 66.7 %reduce-scatter.5.cloned.1.call-start = ((), (), s32[]{:S(2)}) async-start(), calls=%async_computation.6 | async-start | bytes 4718592 | tf_op jit(solution)/shard_map/reduce_scatter | solution.py:217
Sparse Core Ops, SparseCore 0:
  11.9 65.1 all-gather.1
  108.0 48.9 reduce-scatter.2
  223.9 40.2 reduce-scatter.4

commit v11 on v10

--- a/solution.py
+++ b/solution.py
@@ -16,6 +16,10 @@
 chunk = 64
 
 
+def unpack(x):
+    return jnp.concatenate([x[:, :BLOCK], pltpu.roll(x, BLOCK, 1)[:, :BLOCK]], axis=0)
+
+
 def ap_kernel(rows_ref, cols_ref, slots_ref, cnt_ref, a_ref, p2_ref, o_ref, p_scr, acc):
     c = pl.program_id(0)
     capacity = rows_ref.shape[0]
@@ -30,9 +34,8 @@
             col = k // branches
             s = k % branches
             x = p2_ref[(col // RPD) * per_peer_tiles + (col % RPD) * branches + s]
-            even = x[:, :BLOCK]
-            odd = pltpu.roll(x, BLOCK, 1)[:, :BLOCK]
-            p_scr[col, s] = jnp.concatenate([even, odd], axis=0)
+            p_scr[col, s, pl.ds(0, HALF, stride=2), :] = x[:, :BLOCK]
+            p_scr[col, s, pl.ds(1, HALF, stride=2), :] = pltpu.roll(x, BLOCK, 1)[:, :BLOCK]
             return carry
 
         lax.fori_loop(0, cols * branches, unpack, 0, unroll=8)
@@ -42,7 +45,7 @@
     def body(u, carry):
         t = c * chunk + u
         live = t < count
-        a = a_ref[u]
+        a = unpack(a_ref[u])
         col = cols_ref[t]
         row = rows_ref[t]
         for s in range(branches):
@@ -60,9 +63,7 @@
     @pl.when(c == pl.num_programs(0) - 1)
     def _():
         def pack(i, carry):
-            even = acc[i, pl.ds(0, HALF, stride=2), :]
-            odd = acc[i, pl.ds(1, HALF, stride=2), :]
-            o_ref[i] = jnp.concatenate([even, odd], axis=1)
+            o_ref[i] = jnp.concatenate([acc[i, :HALF, :], acc[i, HALF:, :]], axis=1)
             return carry
 
         lax.fori_loop(0, acc.shape[0], pack, 0, unroll=8)
@@ -80,7 +81,7 @@
         num_scalar_prefetch=4,
         grid=(chunks,),
         in_specs=[
-            pl.BlockSpec((chunk, BLOCK, BLOCK), a_map),
+            pl.BlockSpec((chunk, HALF, LANES), a_map),
             pl.BlockSpec(memory_space=pltpu.VMEM),
         ],
         out_specs=pl.BlockSpec(memory_space=pltpu.VMEM),
@@ -97,10 +98,6 @@
             dimension_semantics=("arbitrary",), vmem_limit_bytes=60 * 1024 * 1024
         ),
     )(rows, cols, slots, count, tiles, panel2)
-
-
-def unpack(x):
-    return jnp.concatenate([x[:, :BLOCK], pltpu.roll(x, BLOCK, 1)[:, :BLOCK]], axis=0)
 
 
 def contrib_kernel(src_ref, p2_ref, ap2_ref, o_ref, scr):
@@ -170,9 +167,7 @@
     sent = jnp.concatenate([p2, meta_tile.reshape(1, HALF, LANES)], axis=0)
     panel2 = lax.all_gather(sent, "row", axis=0, tiled=True)
     meta_all = panel2.reshape(row_devices, item_count + 1, tile_len)[:, item_count, :item_count * (TAP + 2)]
-    a_split = (
-        a_vals.reshape(capacity, BLOCK, HALF, 2).transpose(0, 1, 3, 2).reshape(capacity, BLOCK, BLOCK)
-    )
+    a_split = a_vals.reshape(capacity, HALF, LANES)
     partial_value = ap_partial(
         a_split, a_row.reshape(capacity), a_col.reshape(capacity),
         a_slot.reshape(branches * capacity), a_count.reshape(1), panel2,

time: 274 us -> 274 us (level)
  waiting for transfers between devices: 136 us -> 175 us
  local copies, waits for them, and re-layouts: 58.1 us -> 25.4 us
  Pallas kernels: 47.3 us -> 41.9 us
    all_gather x1, waiting for transfers between devices: 23.6 us -> 56.2 us  [on_device(): panel2 = lax.all_gather(sent, 'row', axis=0, tiled=True)]
    reshape x2 -> x0, local copies, waits for them, and re-layouts: 22.8 us -> none  [on_device(): a_vals.reshape(capacity, BLOCK, HALF, 2).transpose(0, 1, 3, 2)]
    transpose x1 -> x0, local copies, waits for them, and re-layouts: 8.56 us -> none  [on_device(): a_vals.reshape(capacity, BLOCK, HALF, 2).transpose(0, 1, 3, 2)]
    reduce_scatter x1, waiting for transfers between devices: 47.8 us -> 54.1 us  [on_device(): lax.psum_scatter(partial_value.reshape(group_rows, TAP, HALF, LANES), 'co...]
    pallas_call x1, Pallas kernels: 30.8 us -> 25.5 us  [ap_partial(): pl.pallas_call(ap_kernel, out_shape=jax.ShapeDtypeStruct((out_rows * TAP,...]
  transfers between devices with their start and end apart: 5 -> 5, of which waited for: 5 -> 5; matrix products, arithmetic and copies ran while one was open for 19% -> 7% of each run, Pallas kernels for 4% -> 4%
where the time goes in v11:
time: 274 us
  waiting for transfers between devices  175 us (64%)
  Pallas kernels  41.9 us (15%)
  local copies, waits for them, and re-layouts  25.4 us (9%)
  between operations  13.9 us (5%)
  starting transfers between devices  10.9 us (4%)
  matrix products  4.9 us (2%)
    all_gather x1, waiting for transfers between devices, on_device(): panel2 = lax.all_gather(sent, 'row', axis=0, tiled=True)  56.2 us
    reduce_scatter x1, waiting for transfers between devices, on_device(): lax.psum_scatter(partial_value.reshape(group_rows, TAP, HALF, LANES), 'co...  54.1 us
    reduce_scatter x1, waiting for transfers between devices, on_device(): lax.psum_scatter(coarse_part.reshape(col_devices, TC, HALF, LANES), 'col'...  40.3 us
    pallas_call x1, Pallas kernels, ap_partial(): pl.pallas_call(ap_kernel, out_shape=jax.ShapeDtypeStruct((out_rows * TAP,...  25.5 us
    all_to_all x2, waiting for transfers between devices, on_device(): lax.all_to_all(outgoing, 'row', split_axis=0, concat_axis=0, tiled=True)  24 us
    pallas_call x2, Pallas kernels, contributions(): pl.pallas_call(contrib_kernel, out_shape=jax.ShapeDtypeStruct((slots, TAP...  16.4 us
    unnamed x10, local copies, waits for them, and re-layouts  11.3 us
    all_to_all x2, starting transfers between devices, on_device(): lax.all_to_all(outgoing, 'row', split_axis=0, concat_axis=0, tiled=True)  10.6 us
  transfers between devices with their start and end apart: 5, of which 5 were waited for; matrix products, arithmetic and copies ran while one was open for 7% of the time, Pallas kernels for 4%

profile of v11, /device:TPU:0, one launch (start us, length us, event | category | flops | bytes accessed | tf_op | source)
XLA Modules:
  0.0 273.7 jit_solution(8860824195992873038)
XLA Ops:
  6.5 0.8 copy.68
  7.3 1.3 copy.67
  8.6 0.3 reshape.119.p2_ref
  8.9 0.9 copy.70
  9.8 0.1 reshape.122
  9.8 0.8 copy.69
  10.6 0.1 reshape.121
  10.7 0.1 reshape.120
  10.8 0.1 copy.71
  10.8 0.1 convert_element_type.24
  10.9 0.8 pad_maximum_fusion.1
  11.7 0.0 all-gather.2.cloned.1.call-update
  11.8 0.0 reduce-scatter.3.cloned.1.call-start
  11.8 0.7 reshape.128.slots_ref
  13.2 7.6 %copy.82 = f32[56,8,32,128]{3,2,1,0:T(8,128)} copy(f32[56,8,32,128]{3,1,2,0:T(8,128)} %bitcast.33) | data formatting | bytes 14680064
  20.8 56.2 %all-gather.2.cloned.1.call-done.p2_ref = f32[400,32,128]{2,1,0:T(8,128)} async-done(((f32[25,32,128]{2,1,0:T(8,128)}), f32[400,32,128]{2,1,0:T(8,128)}) %all-gather.2.cloned.1.call-update) | async-done | bytes 6553616 | tf_op jit(solution)/shard_map/all_gather | solution.py:168
  77.0 25.5 %shard_map.91 = f32[384,32,128]{2,1,0:T(8,128)} custom-call(s32[448]{0:T(512)} %bitcast.39, s32[448]{0:T(512)} %bitcast.40, s32[1344]{0:T(1024)} %reshape.128.slots_ref, s32[1]{0:T(128)} %bitcast.29.cnt_ref, f32[448,32,128]{2,1,0:T(8,128)} %bitcast.30, f32[400,32,128]{2,1,0:T(8,128)} %all-gather.2.cloned.1.call-done.p2_ref), custom_call_target="tpu_custom_call" | custom-call | tf_op jit(solution)/shard_map/pallas_call | solution.py:93
  102.5 0.0 reduce-scatter.3.cloned.1.call-update
  102.5 0.1 reshape.125
  102.6 0.2 convert_reduce_fusion
  102.8 0.1 fusion.8
  102.9 0.1 select_reduce_fusion.1
  103.0 0.1 select_n.32
  103.1 0.8 slice_reduce_fusion.1
  103.8 54.1 %reduce-scatter.3.cloned.1.call-done.ap2_ref = f32[8,6,32,128]{3,2,1,0:T(8,128)} async-done(((f32[64,6,32,128]{3,2,1,0:T(8,128)}), f32[8,6,32,128]{3,2,1,0:T(8,128)}) %reduce-scatter.3.cloned.1.call-update) | async-done | bytes 786448 | tf_op jit(solution)/shard_map/reduce_scatter | solution.py:176
  158.0 6.6 %shard_map.93 = f32[16,6,32,128]{3,2,1,0:T(8,128)} custom-call(s32[16]{0:T(128)} %get-tuple-element.6.src_ref, f32[24,32,128]{2,1,0:T(8,128)} %copy-done, f32[8,6,32,128]{3,2,1,0:T(8,128)} %reduce-scatter.3.cloned.1.call-done.ap2_ref), custom_call_target="tpu_custom_call" | custom-call | tf_op jit(solution)/shard_map/pallas_call | solution.py:133
  164.6 6.9 %all-to-all-start.1 = ((f32[16,6,32,128]{3,2,1,0:T(8,128)}), f32[16,6,32,128]{3,2,1,0:T(8,128)S(1)}, u32[]{:S(2)}, u32[]{:S(2)}) async-start(f32[16,6,32,128]{3,2,1,0:T(8,128)} %shard_map.93), calls=%async_computation.2 | async-start | bytes 3145728 | tf_op jit(solution)/shard_map/all_to_all | solution.py:193
  171.5 9.8 %shard_map.92 = f32[16,6,32,128]{3,2,1,0:T(8,128)} custom-call(s32[16]{0:T(128)} %get-tuple-element.5.src_ref, f32[24,32,128]{2,1,0:T(8,128)} %copy-done, f32[8,6,32,128]{3,2,1,0:T(8,128)} %reduce-scatter.3.cloned.1.call-done.ap2_ref), custom_call_target="tpu_custom_call" | custom-call | tf_op jit(solution)/shard_map/pallas_call | solution.py:133
  181.3 13.4 %all-to-all-done.1 = f32[16,6,32,128]{3,2,1,0:T(8,128)S(1)} async-done(((f32[16,6,32,128]{3,2,1,0:T(8,128)}), f32[16,6,32,128]{3,2,1,0:T(8,128)S(1)}, u32[]{:S(2)}, u32[]{:S(2)}) %all-to-all-start.1) | async-done | bytes 1572896 | tf_op jit(solution)/shard_map/all_to_all | solution.py:193
  194.8 3.7 %all-to-all-start = ((f32[16,6,32,128]{3,2,1,0:T(8,128)}), f32[16,6,32,128]{3,2,1,0:T(8,128)S(1)}, u32[]{:S(2)}, u32[]{:S(2)}) async-start(f32[16,6,32,128]{3,2,1,0:T(8,128)} %shard_map.92), calls=%async_computation.1 | async-start | bytes 3145728 | tf_op jit(solution)/shard_map/all_to_all | solution.py:193
  198.5 0.2 reduce-scatter.5.cloned.1.call-start
  198.7 7.9 %reshape.124 = f32[16,25,4096]{2,1,0:T(8,128)} reshape(f32[400,32,128]{2,1,0:T(8,128)} %all-gather.2.cloned.1.call-done.p2_ref) | data formatting | bytes 13107200 | tf_op jit(solution)/shard_map/reshape | solution.py:169
  206.6 0.9 slice.24
  207.5 0.1 copy.72
  207.7 0.1 copy.74
  207.8 0.1 copy.81
  207.9 0.2 reduce_window_sum.11
  208.0 0.1 fusion.10
  208.2 0.1 select_reduce_fusion
  208.3 0.1 copy.75
  208.4 0.1 select_n.29
  208.5 10.6 %all-to-all-done = f32[16,6,32,128]{3,2,1,0:T(8,128)S(1)} async-done(((f32[16,6,32,128]{3,2,1,0:T(8,128)}), f32[16,6,32,128]{3,2,1,0:T(8,128)S(1)}, u32[]{:S(2)}, u32[]{:S(2)}) %all-to-all-start) | async-done | bytes 1572896 | tf_op jit(solution)/shard_map/all_to_all | solution.py:193
  219.1 0.3 pad_maximum_fusion
  219.4 0.5 copy.77
  219.9 4.9 %fusion = f32[8,27,32,128]{3,1,2,0:T(8,128)} fusion(f32[192,32,128]{2,1,0:T(8,128)S(1)} %bitcast.32, f32[8,27]{1,0:T(8,128)S(1)} %multiply_add_fusion, f32[192]{0:T(256)S(1)} %select_n.29), kind=kOutput, calls=%fused_computation.1 | convolution fusion | flops 1019257344 | bytes 6686304 | tf_op jit(solution)/shard_map/ec,eml->cml/dot_general | solution.py:210
  224.8 0.0 reduce-scatter.5.cloned.1.call-update
  224.8 40.3 %reduce-scatter.5.cloned.1.call-done = f32[1,27,32,128]{3,1,2,0:T(8,128)} async-done(((f32[8,27,32,128]{3,1,2,0:T(8,128)}), f32[1,27,32,128]{3,1,2,0:T(8,128)}) %reduce-scatter.5.cloned.1.call-update) | async-done | bytes 442384 | tf_op jit(solution)/shard_map/reduce_scatter | solution.py:212
  265.1 2.1 copy.79
  (16 shorter events, 0.1 us)
Async XLA Ops:
  6.5 5.3 %copy-start.1 = (s32[1,1,3,448]{3,1,2,0:T(1,128)S(1)}, s32[1,1,3,448]{3,1,2,0:T(1,128)}, u32[]{:S(2)}) copy-start(s32[1,1,3,448]{3,1,2,0:T(1,128)} %param.12) | copy-start | bytes 16132
  6.5 70.5 %all-gather.2.cloned.1.call-start = ((), (), s32[]{:S(2)}) async-start(), calls=%async_computation.4 | async-start | bytes 6963200 | tf_op jit(solution)/shard_map/all_gather | solution.py:168
  8.9 11.9 %copy-start = (f32[24,32,128]{2,1,0:T(8,128)}, f32[24,32,128]{2,1,0:T(8,128)S(1)}, u32[]{:S(2)}) copy-start(f32[24,32,128]{2,1,0:T(8,128)S(1)} %reshape.119.p2_ref) | copy-start | bytes 1179652
  11.8 146.2 %reduce-scatter.3.cloned.1.call-start = ((), (), s32[]{:S(2)}) async-start(), calls=%async_computation.5 | async-start | bytes 7077888 | tf_op jit(solution)/shard_map/reduce_scatter | solution.py:176
  164.6 30.2 %all-to-all-start.1 = ((f32[16,6,32,128]{3,2,1,0:T(8,128)}), f32[16,6,32,128]{3,2,1,0:T(8,128)S(1)}, u32[]{:S(2)}, u32[]{:S(2)}) async-start(f32[16,6,32,128]{3,2,1,0:T(8,128)} %shard_map.93), calls=%async_computation.2 | async-start | bytes 3145728 | tf_op jit(solution)/shard_map/all_to_all | solution.py:193
  194.8 24.3 %all-to-all-start = ((f32[16,6,32,128]{3,2,1,0:T(8,128)}), f32[16,6,32,128]{3,2,1,0:T(8,128)S(1)}, u32[]{:S(2)}, u32[]{:S(2)}) async-start(f32[16,6,32,128]{3,2,1,0:T(8,128)} %shard_map.92), calls=%async_computation.1 | async-start | bytes 3145728 | tf_op jit(solution)/shard_map/all_to_all | solution.py:193
  198.5 66.6 %reduce-scatter.5.cloned.1.call-start = ((), (), s32[]{:S(2)}) async-start(), calls=%async_computation.6 | async-start | bytes 4718592 | tf_op jit(solution)/shard_map/reduce_scatter | solution.py:212
Sparse Core Ops, SparseCore 0:
  11.9 65.1 all-gather.1
  102.6 55.2 reduce-scatter.2
  224.9 40.1 reduce-scatter.4

commit v12 on v10

--- a/solution.py
+++ b/solution.py
@@ -191,12 +191,8 @@
     source = jnp.where(
         jnp.any(hit, axis=1), jnp.sum(jnp.where(hit, serial[None, :], 0), axis=1), item_count
     )
-    by_rank = source.reshape(row_devices, per_peer)
-    incoming = []
-    for k in range(per_peer):
-        outgoing = contributions(by_rank[:, k], p2, ap_rows, row_devices)
-        incoming.append(lax.all_to_all(outgoing, "row", split_axis=0, concat_axis=0, tiled=True))
-    incoming = jnp.stack(incoming, axis=1)
+    outgoing = contributions(source, p2, ap_rows, slots_total)
+    incoming = lax.all_to_all(outgoing, "row", split_axis=0, concat_axis=0, tiled=True)
 
     me = lax.axis_index("row").astype(jnp.float32)
     meta_all = meta_all.reshape(row_devices, item_count, TAP + 2)

time: 274 us -> 277 us (1.011)
  Pallas kernels: 47.3 us -> 52.5 us
  starting transfers between devices: 10.9 us -> 7.2 us
    all_to_all x2 -> x1, waiting for transfers between devices: 23.9 us -> 32.6 us  [on_device(): lax.all_to_all(outgoing, 'row', split_axis=0, concat_axis=0, tiled=True)]
    pallas_call x1, Pallas kernels: 30.8 us -> 38.6 us  [ap_partial(): pl.pallas_call(ap_kernel, out_shape=jax.ShapeDtypeStruct((out_rows * TAP,...]
    reduce_scatter x1, waiting for transfers between devices: 47.8 us -> 40.7 us  [on_device(): lax.psum_scatter(partial_value.reshape(group_rows, TAP, HALF, LANES), 'co...]
    all_to_all x2 -> x1, starting transfers between devices: 10.7 us -> 6.93 us  [on_device(): lax.all_to_all(outgoing, 'row', split_axis=0, concat_axis=0, tiled=True)]
    pallas_call x2 -> x1, Pallas kernels: 16.5 us -> 14 us  [contributions(): pl.pallas_call(contrib_kernel, out_shape=jax.ShapeDtypeStruct((slots, TAP...]
    unnamed x10 -> x8, local copies, waits for them, and re-layouts: 12.7 us -> 12.7 us
  transfers between devices with their start and end apart: 5 -> 4, of which waited for: 5 -> 4; matrix products, arithmetic and copies ran while one was open for 19% -> 19% of each run, Pallas kernels for 4% -> 0%
where the time goes in v12:
time: 277 us; the launch traced here: 276 us
  waiting for transfers between devices  138 us (50%)
  local copies, waits for them, and re-layouts  56.8 us (21%)
  Pallas kernels  52.5 us (19%)
  between operations  13.9 us (5%)
  starting transfers between devices  7.2 us (3%)
  matrix products  4.89 us (2%)
  other arithmetic  2.88 us (1%)
    reduce_scatter x1, waiting for transfers between devices, on_device(): lax.psum_scatter(coarse_part.reshape(col_devices, TC, HALF, LANES), 'col'...  41.6 us
    reduce_scatter x1, waiting for transfers between devices, on_device(): lax.psum_scatter(partial_value.reshape(group_rows, TAP, HALF, LANES), 'co...  40.7 us
    pallas_call x1, Pallas kernels, ap_partial(): pl.pallas_call(ap_kernel, out_shape=jax.ShapeDtypeStruct((out_rows * TAP,...  38.6 us
    all_to_all x1, waiting for transfers between devices, on_device(): lax.all_to_all(outgoing, 'row', split_axis=0, concat_axis=0, tiled=True)  32.6 us
    all_gather x1, waiting for transfers between devices, on_device(): panel2 = lax.all_gather(sent, 'row', axis=0, tiled=True)  22.8 us
    reshape x2, local copies, waits for them, and re-layouts, on_device(): a_vals.reshape(capacity, BLOCK, HALF, 2).transpose(0, 1, 3, 2)  22.8 us
    pallas_call x1, Pallas kernels, contributions(): pl.pallas_call(contrib_kernel, out_shape=jax.ShapeDtypeStruct((slots, TAP...  14 us
    unnamed x8, local copies, waits for them, and re-layouts  12.7 us
  transfers between devices with their start and end apart: 4, of which 4 were waited for; matrix products, arithmetic and copies ran while one was open for 19% of the time, Pallas kernels for 0%

profile of v12, /device:TPU:0, one launch (start us, length us, event | category | flops | bytes accessed | tf_op | source)
XLA Modules:
  0.0 275.9 jit_solution(6735054060037341913)
XLA Ops:
  6.5 0.0 all-gather.2.cloned.1.call-start
  6.5 0.8 copy.78
  7.3 1.3 copy.77
  8.6 0.3 reshape.117.p2_ref
  8.9 0.0 copy-start
  8.9 0.9 copy.80
  9.7 0.1 reshape.120
  9.8 0.8 copy.79
  10.6 0.1 reshape.119
  10.7 0.1 reshape.118
  10.8 0.1 copy.81
  10.8 0.1 convert_element_type.24
  10.9 0.8 pad_maximum_fusion
  11.7 0.0 all-gather.2.cloned.1.call-update
  11.7 0.0 reduce-scatter.3.cloned.1.call-start
  11.8 0.7 reduce
  12.5 0.7 reshape.126.slots_ref
  13.8 9.0 %copy.87 = f32[1,1,448,4096]{2,3,1,0:T(8,128)} copy(f32[1,1,448,4096]{3,2,1,0:T(8,128)} %param.9) | data formatting | bytes 14680064 | tf_op args[0]
  22.8 10.8 %reshape.128 = f32[448,64,32,2]{0,3,2,1:T(2,128)} reshape(f32[1,1,448,4096]{2,3,1,0:T(8,128)} %copy.87) | data formatting | bytes 14680064 | tf_op jit(solution)/shard_map/reshape | solution.py:174
  33.6 8.6 %copy.88 = f32[448,64,2,32]{0,3,2,1:T(8,128)} copy(f32[448,64,2,32]{0,2,3,1:T(2,128)} %bitcast.30) | data formatting | bytes 14680064 | tf_op jit(solution)/shard_map/transpose | solution.py:174
  42.2 11.9 %copy.89.a_ref = f32[448,64,64]{2,1,0:T(8,128)} copy(f32[448,64,64]{0,2,1:T(8,128)} %bitcast.31) | data formatting | bytes 14680064 | tf_op jit(solution)/shard_map/reshape | solution.py:174
  54.2 22.8 %all-gather.2.cloned.1.call-done.p2_ref = f32[400,32,128]{2,1,0:T(8,128)} async-done(((f32[25,32,128]{2,1,0:T(8,128)}), f32[400,32,128]{2,1,0:T(8,128)}) %all-gather.2.cloned.1.call-update) | async-done | bytes 6553616 | tf_op jit(solution)/shard_map/all_gather | solution.py:171
  77.0 38.6 %shard_map.91 = f32[384,32,128]{2,1,0:T(8,128)} custom-call(s32[448]{0:T(512)} %bitcast.37, s32[448]{0:T(512)} %bitcast.38, s32[1344]{0:T(1024)} %reshape.126.slots_ref, s32[1]{0:T(128)} %bitcast.29.cnt_ref, f32[448,64,64]{2,1,0:T(8,128)} %copy.89.a_ref, f32[400,32,128]{2,1,0:T(8,128)} %all-gather.2.cloned.1.call-done.p2_ref), custom_call_target="tpu_custom_call" | custom-call | tf_op jit(solution)/shard_map/pallas_call | solution.py:92
  115.6 0.0 reduce-scatter.3.cloned.1.call-update
  115.6 0.1 reshape.123
  115.7 0.2 convert_reduce_fusion
  115.9 0.1 fusion.8
  116.0 0.1 select_reduce_fusion.1
  116.1 0.5 broadcast_select_fusion.1.src_ref
  116.6 40.7 %reduce-scatter.3.cloned.1.call-done.ap2_ref = f32[8,6,32,128]{3,2,1,0:T(8,128)} async-done(((f32[64,6,32,128]{3,2,1,0:T(8,128)}), f32[8,6,32,128]{3,2,1,0:T(8,128)}) %reduce-scatter.3.cloned.1.call-update) | async-done | bytes 786448 | tf_op jit(solution)/shard_map/reduce_scatter | solution.py:181
  157.3 14.0 %shard_map.92 = f32[32,6,32,128]{3,2,1,0:T(8,128)} custom-call(s32[32]{0:T(128)} %broadcast_select_fusion.1.src_ref, f32[24,32,128]{2,1,0:T(8,128)} %copy-done, f32[8,6,32,128]{3,2,1,0:T(8,128)} %reduce-scatter.3.cloned.1.call-done.ap2_ref), custom_call_target="tpu_custom_call" | custom-call | tf_op jit(solution)/shard_map/pallas_call | solution.py:136
  171.3 6.9 %all-to-all-start = ((f32[32,6,32,128]{3,2,1,0:T(8,128)}), f32[32,6,32,128]{3,2,1,0:T(8,128)S(1)}, u32[]{:S(2)}, u32[]{:S(2)}) async-start(f32[32,6,32,128]{3,2,1,0:T(8,128)} %shard_map.92), calls=%async_computation.1 | async-start | bytes 6291456 | tf_op jit(solution)/shard_map/all_to_all | solution.py:195
  178.2 0.2 reduce-scatter.5.cloned.1.call-start
  178.5 7.9 %reshape.122 = f32[16,25,4096]{2,1,0:T(8,128)} reshape(f32[400,32,128]{2,1,0:T(8,128)} %all-gather.2.cloned.1.call-done.p2_ref) | data formatting | bytes 13107200 | tf_op jit(solution)/shard_map/reshape | solution.py:172
  186.3 0.9 slice.16
  187.3 0.1 copy.82
  187.4 0.1 copy.84
  187.5 0.1 copy.93
  187.6 0.2 reduce_window_sum.11
  187.8 0.1 fusion.10
  187.9 0.1 select_reduce_fusion
  188.0 0.1 copy.85
  188.1 0.1 select_n.25
  188.2 32.6 %all-to-all-done = f32[32,6,32,128]{3,2,1,0:T(8,128)S(1)} async-done(((f32[32,6,32,128]{3,2,1,0:T(8,128)}), f32[32,6,32,128]{3,2,1,0:T(8,128)S(1)}, u32[]{:S(2)}, u32[]{:S(2)}) %all-to-all-start) | async-done | bytes 3145760 | tf_op jit(solution)/shard_map/all_to_all | solution.py:195
  220.9 4.9 %fusion = f32[8,27,32,128]{3,1,2,0:T(8,128)} fusion(f32[192,32,128]{2,1,0:T(8,128)S(1)} %bitcast.33, f32[8,27]{1,0:T(8,128)S(1)} %multiply_add_fusion, f32[192]{0:T(256)S(1)} %select_n.25), kind=kOutput, calls=%fused_computation | convolution fusion | flops 1019257344 | bytes 6686304 | tf_op jit(solution)/shard_map/ec,eml->cml/dot_general | solution.py:211
  225.8 0.0 reduce-scatter.5.cloned.1.call-update
  225.8 41.6 %reduce-scatter.5.cloned.1.call-done = f32[1,27,32,128]{3,1,2,0:T(8,128)} async-done(((f32[8,27,32,128]{3,1,2,0:T(8,128)}), f32[1,27,32,128]{3,1,2,0:T(8,128)}) %reduce-scatter.5.cloned.1.call-update) | async-done | bytes 442384 | tf_op jit(solution)/shard_map/reduce_scatter | solution.py:213
  267.4 2.1 copy.91
  (10 shorter events, 0.1 us)
Async XLA Ops:
  6.5 70.5 %all-gather.2.cloned.1.call-start = ((), (), s32[]{:S(2)}) async-start(), calls=%async_computation.3 | async-start | bytes 6963200 | tf_op jit(solution)/shard_map/all_gather | solution.py:171
  8.9 13.9 %copy-start = (f32[24,32,128]{2,1,0:T(8,128)}, f32[24,32,128]{2,1,0:T(8,128)S(1)}, u32[]{:S(2)}) copy-start(f32[24,32,128]{2,1,0:T(8,128)S(1)} %reshape.117.p2_ref) | copy-start | bytes 1179652
  11.7 145.6 %reduce-scatter.3.cloned.1.call-start = ((), (), s32[]{:S(2)}) async-start(), calls=%async_computation.4 | async-start | bytes 7077888 | tf_op jit(solution)/shard_map/reduce_scatter | solution.py:181
  171.3 49.6 %all-to-all-start = ((f32[32,6,32,128]{3,2,1,0:T(8,128)}), f32[32,6,32,128]{3,2,1,0:T(8,128)S(1)}, u32[]{:S(2)}, u32[]{:S(2)}) async-start(f32[32,6,32,128]{3,2,1,0:T(8,128)} %shard_map.92), calls=%async_computation.1 | async-start | bytes 6291456 | tf_op jit(solution)/shard_map/all_to_all | solution.py:195
  178.2 89.1 %reduce-scatter.5.cloned.1.call-start = ((), (), s32[]{:S(2)}) async-start(), calls=%async_computation.5 | async-start | bytes 4718592 | tf_op jit(solution)/shard_map/reduce_scatter | solution.py:213
Sparse Core Ops, SparseCore 0:
  11.9 65.1 all-gather.1
  115.7 41.5 reduce-scatter.2
  225.9 41.4 reduce-scatter.4

commit v13 on v10

--- a/solution.py
+++ b/solution.py
@@ -196,7 +196,6 @@
     for k in range(per_peer):
         outgoing = contributions(by_rank[:, k], p2, ap_rows, row_devices)
         incoming.append(lax.all_to_all(outgoing, "row", split_axis=0, concat_axis=0, tiled=True))
-    incoming = jnp.stack(incoming, axis=1)
 
     me = lax.axis_index("row").astype(jnp.float32)
     meta_all = meta_all.reshape(row_devices, item_count, TAP + 2)
@@ -207,13 +206,19 @@
     dest = meta_all[:, :, 1:2] * TC + meta_all[:, :, 2:]
     dest_slot = jnp.sum(jnp.where(pick[..., None], dest[:, None, :, :], 0.0), axis=2)
     valid = jnp.any(pick, axis=2)
-    dest_slot = jnp.where(valid[..., None], dest_slot, -1.0).reshape(slots_total * TAP)
+    dest_slot = jnp.where(valid[..., None], dest_slot, -1.0)
     group_coarse = col_devices * TC
-    onehot = (
-        dest_slot[:, None] == jnp.arange(group_coarse, dtype=jnp.float32)[None, :]
-    ).astype(jnp.float32)
-    coarse_part = jnp.einsum("ec,eml->cml", onehot, incoming.reshape(slots_total * TAP, HALF, LANES),
-                             precision=lax.Precision.HIGH)
+    coarse_part = None
+    for k in range(per_peer):
+        onehot = (
+            dest_slot[:, k].reshape(row_devices * TAP, 1)
+            == jnp.arange(group_coarse, dtype=jnp.float32)[None, :]
+        ).astype(jnp.float32)
+        part = jnp.einsum(
+            "ec,eml->cml", onehot, incoming[k].reshape(row_devices * TAP, HALF, LANES),
+            precision=lax.Precision.HIGH,
+        )
+        coarse_part = part if coarse_part is None else coarse_part + part
     coarse = lax.psum_scatter(
         coarse_part.reshape(col_devices, TC, HALF, LANES), "col", scatter_dimension=0, tiled=True
     )

time: 274 us -> 275 us (level)
  Pallas kernels: 47.3 us -> 39.5 us
  waiting for transfers between devices: 136 us -> 142 us
    reduce_scatter x1, waiting for transfers between devices: 47.8 us -> 56.5 us  [on_device(): lax.psum_scatter(partial_value.reshape(group_rows, TAP, HALF, LANES), 'co...]
    pallas_call x1, Pallas kernels: 30.8 us -> 23 us  [ap_partial(): pl.pallas_call(ap_kernel, out_shape=jax.ShapeDtypeStruct((out_rows * TAP,...]
    dot_general x1 -> x2, matrix products: 4.89 us -> 6.66 us  [on_device(): jnp.einsum('ec,eml->cml', onehot, incoming[k].reshape(row_devices * TAP,...]
  transfers between devices with their start and end apart: 5 -> 5, of which waited for: 5 -> 5; matrix products, arithmetic and copies ran while one was open for 19% -> 21% of each run, Pallas kernels for 4% -> 2%
where the time goes in v13:
time: 275 us; the launch traced here: 274 us
  waiting for transfers between devices  142 us (52%)
  local copies, waits for them, and re-layouts  58.1 us (21%)
  Pallas kernels  39.5 us (14%)
  between operations  13.9 us (5%)
  starting transfers between devices  11.6 us (4%)
  matrix products  6.66 us (2%)
    reduce_scatter x1, waiting for transfers between devices, on_device(): lax.psum_scatter(partial_value.reshape(group_rows, TAP, HALF, LANES), 'co...  56.5 us
    reduce_scatter x1, waiting for transfers between devices, on_device(): lax.psum_scatter(coarse_part.reshape(col_devices, TC, HALF, LANES), 'col'...  38.7 us
    all_to_all x2, waiting for transfers between devices, on_device(): lax.all_to_all(outgoing, 'row', split_axis=0, concat_axis=0, tiled=True)  23.6 us
    pallas_call x1, Pallas kernels, ap_partial(): pl.pallas_call(ap_kernel, out_shape=jax.ShapeDtypeStruct((out_rows * TAP,...  23 us
    all_gather x1, waiting for transfers between devices, on_device(): panel2 = lax.all_gather(sent, 'row', axis=0, tiled=True)  22.8 us
    reshape x2, local copies, waits for them, and re-layouts, on_device(): a_vals.reshape(capacity, BLOCK, HALF, 2).transpose(0, 1, 3, 2)  22.8 us
    pallas_call x2, Pallas kernels, contributions(): pl.pallas_call(contrib_kernel, out_shape=jax.ShapeDtypeStruct((slots, TAP...  16.5 us
    unnamed x10, local copies, waits for them, and re-layouts  12.7 us
  transfers between devices with their start and end apart: 5, of which 5 were waited for; matrix products, arithmetic and copies ran while one was open for 21% of the time, Pallas kernels for 2%

profile of v13, /device:TPU:0, one launch (start us, length us, event | category | flops | bytes accessed | tf_op | source)
XLA Modules:
  0.0 273.8 jit_solution(2668516877865382069)
XLA Ops:
  6.5 0.8 copy.86
  7.3 1.3 copy.85
  8.6 0.3 reshape.99.p2_ref
  8.9 0.9 copy.88
  9.7 0.1 reshape.102
  9.8 0.8 copy.87
  10.6 0.1 reshape.101
  10.7 0.1 reshape.100
  10.8 0.1 copy.89
  10.8 0.1 convert_element_type.25
  10.9 0.8 pad_maximum_fusion
  11.8 0.7 reduce.1
  12.5 0.7 reshape.108.slots_ref
  13.8 9.0 %copy.95 = f32[1,1,448,4096]{2,3,1,0:T(8,128)} copy(f32[1,1,448,4096]{3,2,1,0:T(8,128)} %param.9) | data formatting | bytes 14680064 | tf_op args[0]
  22.8 10.8 %reshape.110 = f32[448,64,32,2]{0,3,2,1:T(2,128)} reshape(f32[1,1,448,4096]{2,3,1,0:T(8,128)} %copy.95) | data formatting | bytes 14680064 | tf_op jit(solution)/shard_map/reshape | solution.py:174
  33.6 8.6 %copy.96 = f32[448,64,2,32]{0,3,2,1:T(8,128)} copy(f32[448,64,2,32]{0,2,3,1:T(2,128)} %bitcast.34) | data formatting | bytes 14680064 | tf_op jit(solution)/shard_map/transpose | solution.py:174
  42.2 11.9 %copy.97.a_ref = f32[448,64,64]{2,1,0:T(8,128)} copy(f32[448,64,64]{0,2,1:T(8,128)} %bitcast.35) | data formatting | bytes 14680064 | tf_op jit(solution)/shard_map/reshape | solution.py:174
  54.2 22.8 %all-gather.2.cloned.1.call-done.p2_ref = f32[400,32,128]{2,1,0:T(8,128)} async-done(((f32[25,32,128]{2,1,0:T(8,128)}), f32[400,32,128]{2,1,0:T(8,128)}) %all-gather.2.cloned.1.call-update) | async-done | bytes 6553616 | tf_op jit(solution)/shard_map/all_gather | solution.py:171
  77.0 23.0 %shard_map.91 = f32[384,32,128]{2,1,0:T(8,128)} custom-call(s32[448]{0:T(512)} %bitcast.42, s32[448]{0:T(512)} %bitcast.43, s32[1344]{0:T(1024)} %reshape.108.slots_ref, s32[1]{0:T(128)} %bitcast.33.cnt_ref, f32[448,64,64]{2,1,0:T(8,128)} %copy.97.a_ref, f32[400,32,128]{2,1,0:T(8,128)} %all-gather.2.cloned.1.call-done.p2_ref), custom_call_target="tpu_custom_call" | custom-call | tf_op jit(solution)/shard_map/pallas_call | solution.py:92
  100.0 0.1 reshape.105
  100.1 0.2 convert_reduce_fusion
  100.3 0.1 fusion.10
  100.4 0.1 select_reduce_fusion.1
  100.5 0.1 select_n.24
  100.6 0.8 slice_reduce_fusion
  101.4 56.5 %reduce-scatter.3.cloned.1.call-done.ap2_ref = f32[8,6,32,128]{3,2,1,0:T(8,128)} async-done(((f32[64,6,32,128]{3,2,1,0:T(8,128)}), f32[8,6,32,128]{3,2,1,0:T(8,128)}) %reduce-scatter.3.cloned.1.call-update) | async-done | bytes 786448 | tf_op jit(solution)/shard_map/reduce_scatter | solution.py:181
  157.9 9.9 %shard_map.92 = f32[16,6,32,128]{3,2,1,0:T(8,128)} custom-call(s32[16]{0:T(128)} %get-tuple-element.6.src_ref, f32[24,32,128]{2,1,0:T(8,128)} %copy-done.1, f32[8,6,32,128]{3,2,1,0:T(8,128)} %reduce-scatter.3.cloned.1.call-done.ap2_ref), custom_call_target="tpu_custom_call" | custom-call | tf_op jit(solution)/shard_map/pallas_call | solution.py:136
  167.7 6.9 %all-to-all-start = ((f32[16,6,32,128]{3,2,1,0:T(8,128)}), f32[16,6,32,128]{3,2,1,0:T(8,128)S(1)}, u32[]{:S(2)}, u32[]{:S(2)}) async-start(f32[16,6,32,128]{3,2,1,0:T(8,128)} %shard_map.92), calls=%async_computation.1 | async-start | bytes 3145728 | tf_op jit(solution)/shard_map/all_to_all | solution.py:198
  174.7 7.9 %reshape.104 = f32[16,25,4096]{2,1,0:T(8,128)} reshape(f32[400,32,128]{2,1,0:T(8,128)} %all-gather.2.cloned.1.call-done.p2_ref) | data formatting | bytes 13107200 | tf_op jit(solution)/shard_map/reshape | solution.py:172
  182.6 0.9 slice.32
  183.5 0.1 copy.90
  183.7 6.6 %shard_map.93 = f32[16,6,32,128]{3,2,1,0:T(8,128)} custom-call(s32[16]{0:T(128)} %get-tuple-element.5.src_ref, f32[24,32,128]{2,1,0:T(8,128)} %copy-done.1, f32[8,6,32,128]{3,2,1,0:T(8,128)} %reduce-scatter.3.cloned.1.call-done.ap2_ref), custom_call_target="tpu_custom_call" | custom-call | tf_op jit(solution)/shard_map/pallas_call | solution.py:136
  190.4 7.6 %all-to-all-done = f32[16,6,32,128]{3,2,1,0:T(8,128)S(1)} async-done(((f32[16,6,32,128]{3,2,1,0:T(8,128)}), f32[16,6,32,128]{3,2,1,0:T(8,128)S(1)}, u32[]{:S(2)}, u32[]{:S(2)}) %all-to-all-start) | async-done | bytes 1572896 | tf_op jit(solution)/shard_map/all_to_all | solution.py:198
  197.9 4.4 %all-to-all-start.1 = ((f32[16,6,32,128]{3,2,1,0:T(8,128)}), f32[16,6,32,128]{3,2,1,0:T(8,128)}, u32[]{:S(2)}, u32[]{:S(2)}) async-start(f32[16,6,32,128]{3,2,1,0:T(8,128)} %shard_map.93), calls=%async_computation.2 | async-start | bytes 3145728 | tf_op jit(solution)/shard_map/all_to_all | solution.py:198
  202.3 0.2 reduce-scatter.5.cloned.1.call-start
  202.6 0.1 copy.92
  202.7 0.2 reduce_window_sum.11
  202.9 0.1 fusion.12
  203.0 0.1 select_reduce_fusion
  203.1 0.1 copy.93
  203.2 0.1 eq.96
  203.3 0.1 copy.99
  203.4 0.1 eq.106
  203.5 3.3 %fusion.1 = f32[216,32,128]{2,0,1:T(8,128)S(1)} fusion(f32[96,32,128]{2,1,0:T(8,128)} %bitcast.38, f32[96]{0:T(128)S(1)} %eq.96), kind=kOutput, calls=%fused_computation.2 | convolution fusion | flops 509628672 | bytes 5112192 | tf_op jit(solution)/shard_map/ec,eml->cml/dot_general | solution.py:217
  206.7 16.0 %all-to-all-done.1 = f32[16,6,32,128]{3,2,1,0:T(8,128)} async-done(((f32[16,6,32,128]{3,2,1,0:T(8,128)}), f32[16,6,32,128]{3,2,1,0:T(8,128)}, u32[]{:S(2)}, u32[]{:S(2)}) %all-to-all-start.1) | async-done | bytes 1572896 | tf_op jit(solution)/shard_map/all_to_all | solution.py:198
  222.8 3.4 %convolution_add_fusion = f32[216,32,128]{2,0,1:T(8,128)S(1)} fusion(f32[216,32,128]{2,0,1:T(8,128)S(1)} %fusion.1, f32[96,32,128]{2,1,0:T(8,128)} %bitcast.13, f32[96]{0:T(128)S(1)} %eq.106), kind=kOutput, calls=%fused_computation | convolution fusion | flops 510513408 | bytes 8651136 | tf_op jit(solution)/shard_map/ec,eml->cml/dot_general | solution.py:217
  226.2 2.4 copy.101
  228.6 38.7 %reduce-scatter.5.cloned.1.call-done = f32[1,27,32,128]{3,2,1,0:T(8,128)} async-done(((f32[8,27,32,128]{3,2,1,0:T(8,128)}), f32[1,27,32,128]{3,2,1,0:T(8,128)}) %reduce-scatter.5.cloned.1.call-update) | async-done | bytes 442384 | tf_op jit(solution)/shard_map/reduce_scatter | solution.py:222
  (20 shorter events, 0.3 us)
Async XLA Ops:
  6.5 70.5 %all-gather.2.cloned.1.call-start = ((), (), s32[]{:S(2)}) async-start(), calls=%async_computation.4 | async-start | bytes 6963200 | tf_op jit(solution)/shard_map/all_gather | solution.py:171
  8.9 13.9 %copy-start.1 = (f32[24,32,128]{2,1,0:T(8,128)}, f32[24,32,128]{2,1,0:T(8,128)S(1)}, u32[]{:S(2)}) copy-start(f32[24,32,128]{2,1,0:T(8,128)S(1)} %reshape.99.p2_ref) | copy-start | bytes 1179652
  11.7 146.1 %reduce-scatter.3.cloned.1.call-start = ((), (), s32[]{:S(2)}) async-start(), calls=%async_computation.5 | async-start | bytes 7077888 | tf_op jit(solution)/shard_map/reduce_scatter | solution.py:181
  167.7 30.2 %all-to-all-start = ((f32[16,6,32,128]{3,2,1,0:T(8,128)}), f32[16,6,32,128]{3,2,1,0:T(8,128)S(1)}, u32[]{:S(2)}, u32[]{:S(2)}) async-start(f32[16,6,32,128]{3,2,1,0:T(8,128)} %shard_map.92), calls=%async_computation.1 | async-start | bytes 3145728 | tf_op jit(solution)/shard_map/all_to_all | solution.py:198
  197.9 5.5 %copy-start = (f32[16,6,32,128]{3,2,1,0:T(8,128)}, f32[16,6,32,128]{3,2,1,0:T(8,128)S(1)}, u32[]{:S(2)}) copy-start(f32[16,6,32,128]{3,2,1,0:T(8,128)S(1)} %all-to-all-done) | copy-start | bytes 4718596
  197.9 24.8 %all-to-all-start.1 = ((f32[16,6,32,128]{3,2,1,0:T(8,128)}), f32[16,6,32,128]{3,2,1,0:T(8,128)}, u32[]{:S(2)}, u32[]{:S(2)}) async-start(f32[16,6,32,128]{3,2,1,0:T(8,128)} %shard_map.93), calls=%async_computation.2 | async-start | bytes 3145728 | tf_op jit(solution)/shard_map/all_to_all | solution.py:198
  202.3 64.9 %reduce-scatter.5.cloned.1.call-start = ((), (), s32[]{:S(2)}) async-start(), calls=%async_computation.6 | async-start | bytes 3981312 | tf_op jit(solution)/shard_map/reduce_scatter | solution.py:222
Sparse Core Ops, SparseCore 0:
  11.9 65.1 all-gather.1
  100.2 57.6 reduce-scatter.2
  228.7 38.4 reduce-scatter.4

commit v14 on v10

--- a/solution.py
+++ b/solution.py
@@ -13,7 +13,7 @@
 HALF = BLOCK * BLOCK // LANES
 
 highest = lax.Precision.HIGHEST
-chunk = 64
+chunk = 112
 
 
 def ap_kernel(rows_ref, cols_ref, slots_ref, cnt_ref, a_ref, p2_ref, o_ref, p_scr, acc):

time: 274 us -> 275 us (level)
  Pallas kernels: 47.3 us -> 50.5 us
  waiting for transfers between devices: 136 us -> 133 us
    pallas_call x1, Pallas kernels: 30.8 us -> 34 us  [ap_partial(): pl.pallas_call(ap_kernel, out_shape=jax.ShapeDtypeStruct((out_rows * TAP,...]
where the time goes in v14:
time: 275 us; the launch traced here: 273 us
  waiting for transfers between devices  133 us (48%)
  local copies, waits for them, and re-layouts  58.1 us (21%)
  Pallas kernels  50.5 us (18%)
  between operations  13.9 us (5%)
  starting transfers between devices  10.9 us (4%)
  matrix products  4.89 us (2%)
    reduce_scatter x1, waiting for transfers between devices, on_device(): lax.psum_scatter(partial_value.reshape(group_rows, TAP, HALF, LANES), 'co...  45.1 us
    reduce_scatter x1, waiting for transfers between devices, on_device(): lax.psum_scatter(coarse_part.reshape(col_devices, TC, HALF, LANES), 'col'...  40.3 us
    pallas_call x1, Pallas kernels, ap_partial(): pl.pallas_call(ap_kernel, out_shape=jax.ShapeDtypeStruct((out_rows * TAP,...  34 us
    all_to_all x2, waiting for transfers between devices, on_device(): lax.all_to_all(outgoing, 'row', split_axis=0, concat_axis=0, tiled=True)  23.9 us
    all_gather x1, waiting for transfers between devices, on_device(): panel2 = lax.all_gather(sent, 'row', axis=0, tiled=True)  23.6 us
    reshape x2, local copies, waits for them, and re-layouts, on_device(): a_vals.reshape(capacity, BLOCK, HALF, 2).transpose(0, 1, 3, 2)  22.8 us
    pallas_call x2, Pallas kernels, contributions(): pl.pallas_call(contrib_kernel, out_shape=jax.ShapeDtypeStruct((slots, TAP...  16.5 us
    unnamed x10, local copies, waits for them, and re-layouts  12.7 us
  transfers between devices with their start and end apart: 5, of which 5 were waited for; matrix products, arithmetic and copies ran while one was open for 19% of the time, Pallas kernels for 4%

profile of v14, /device:TPU:0, one launch (start us, length us, event | category | flops | bytes accessed | tf_op | source)
XLA Modules:
  0.0 273.2 jit_solution(17056709747988749875)
XLA Ops:
  6.5 0.8 copy.81
  7.3 1.3 copy.80
  8.6 0.3 reshape.122.p2_ref
  8.9 0.9 copy.83
  9.8 0.1 reshape.125
  9.8 0.8 copy.82
  10.6 0.1 reshape.124
  10.7 0.1 reshape.123
  10.8 0.1 copy.84
  10.8 0.1 convert_element_type.24
  10.9 0.8 pad_maximum_fusion.1
  11.8 0.0 reduce-scatter.3.cloned.1.call-start
  11.8 0.7 reshape.131.slots_ref
  13.2 9.0 %copy.90 = f32[1,1,448,4096]{2,3,1,0:T(8,128)} copy(f32[1,1,448,4096]{3,2,1,0:T(8,128)} %param.9) | data formatting | bytes 14680064 | tf_op args[0]
  22.1 10.9 %reshape.133 = f32[448,64,32,2]{0,3,2,1:T(2,128)} reshape(f32[1,1,448,4096]{2,3,1,0:T(8,128)} %copy.90) | data formatting | bytes 14680064 | tf_op jit(solution)/shard_map/reshape | solution.py:174
  33.0 8.6 %copy.91 = f32[448,64,2,32]{0,3,2,1:T(8,128)} copy(f32[448,64,2,32]{0,2,3,1:T(2,128)} %bitcast.32) | data formatting | bytes 14680064 | tf_op jit(solution)/shard_map/transpose | solution.py:174
  41.6 11.9 %copy.92.a_ref = f32[448,64,64]{2,1,0:T(8,128)} copy(f32[448,64,64]{0,2,1:T(8,128)} %bitcast.33) | data formatting | bytes 14680064 | tf_op jit(solution)/shard_map/reshape | solution.py:174
  53.5 23.6 %all-gather.2.cloned.1.call-done.p2_ref = f32[400,32,128]{2,1,0:T(8,128)} async-done(((f32[25,32,128]{2,1,0:T(8,128)}), f32[400,32,128]{2,1,0:T(8,128)}) %all-gather.2.cloned.1.call-update) | async-done | bytes 6553616 | tf_op jit(solution)/shard_map/all_gather | solution.py:171
  77.0 34.0 %shard_map.91 = f32[384,32,128]{2,1,0:T(8,128)} custom-call(s32[448]{0:T(512)} %bitcast.41, s32[448]{0:T(512)} %bitcast.42, s32[1344]{0:T(1024)} %reshape.131.slots_ref, s32[1]{0:T(128)} %bitcast.31.cnt_ref, f32[448,64,64]{2,1,0:T(8,128)} %copy.92.a_ref, f32[400,32,128]{2,1,0:T(8,128)} %all-gather.2.cloned.1.call-done.p2_ref), custom_call_target="tpu_custom_call" | custom-call | tf_op jit(solution)/shard_map/pallas_call | solution.py:92
  111.1 0.1 reshape.128
  111.2 0.2 convert_reduce_fusion
  111.4 0.1 fusion.8
  111.5 0.1 select_reduce_fusion.1
  111.6 0.1 select_n.32
  111.6 0.8 slice_reduce_fusion.1
  112.4 45.1 %reduce-scatter.3.cloned.1.call-done.ap2_ref = f32[8,6,32,128]{3,2,1,0:T(8,128)} async-done(((f32[64,6,32,128]{3,2,1,0:T(8,128)}), f32[8,6,32,128]{3,2,1,0:T(8,128)}) %reduce-scatter.3.cloned.1.call-update) | async-done | bytes 786448 | tf_op jit(solution)/shard_map/reduce_scatter | solution.py:181
  157.5 6.6 %shard_map.93 = f32[16,6,32,128]{3,2,1,0:T(8,128)} custom-call(s32[16]{0:T(128)} %get-tuple-element.6.src_ref, f32[24,32,128]{2,1,0:T(8,128)} %copy-done, f32[8,6,32,128]{3,2,1,0:T(8,128)} %reduce-scatter.3.cloned.1.call-done.ap2_ref), custom_call_target="tpu_custom_call" | custom-call | tf_op jit(solution)/shard_map/pallas_call | solution.py:136
  164.1 6.9 %all-to-all-start.1 = ((f32[16,6,32,128]{3,2,1,0:T(8,128)}), f32[16,6,32,128]{3,2,1,0:T(8,128)S(1)}, u32[]{:S(2)}, u32[]{:S(2)}) async-start(f32[16,6,32,128]{3,2,1,0:T(8,128)} %shard_map.93), calls=%async_computation.2 | async-start | bytes 3145728 | tf_op jit(solution)/shard_map/all_to_all | solution.py:198
  171.0 9.9 %shard_map.92 = f32[16,6,32,128]{3,2,1,0:T(8,128)} custom-call(s32[16]{0:T(128)} %get-tuple-element.5.src_ref, f32[24,32,128]{2,1,0:T(8,128)} %copy-done, f32[8,6,32,128]{3,2,1,0:T(8,128)} %reduce-scatter.3.cloned.1.call-done.ap2_ref), custom_call_target="tpu_custom_call" | custom-call | tf_op jit(solution)/shard_map/pallas_call | solution.py:136
  180.9 13.3 %all-to-all-done.1 = f32[16,6,32,128]{3,2,1,0:T(8,128)S(1)} async-done(((f32[16,6,32,128]{3,2,1,0:T(8,128)}), f32[16,6,32,128]{3,2,1,0:T(8,128)S(1)}, u32[]{:S(2)}, u32[]{:S(2)}) %all-to-all-start.1) | async-done | bytes 1572896 | tf_op jit(solution)/shard_map/all_to_all | solution.py:198
  194.3 3.7 %all-to-all-start = ((f32[16,6,32,128]{3,2,1,0:T(8,128)}), f32[16,6,32,128]{3,2,1,0:T(8,128)S(1)}, u32[]{:S(2)}, u32[]{:S(2)}) async-start(f32[16,6,32,128]{3,2,1,0:T(8,128)} %shard_map.92), calls=%async_computation.1 | async-start | bytes 3145728 | tf_op jit(solution)/shard_map/all_to_all | solution.py:198
  198.0 0.2 reduce-scatter.5.cloned.1.call-start
  198.2 7.9 %reshape.127 = f32[16,25,4096]{2,1,0:T(8,128)} reshape(f32[400,32,128]{2,1,0:T(8,128)} %all-gather.2.cloned.1.call-done.p2_ref) | data formatting | bytes 13107200 | tf_op jit(solution)/shard_map/reshape | solution.py:172
  206.1 0.9 slice.24
  207.0 0.1 copy.85
  207.2 0.1 copy.87
  207.3 0.1 copy.97
  207.3 0.2 reduce_window_sum.11
  207.5 0.1 fusion.10
  207.7 0.1 select_reduce_fusion
  207.8 0.1 copy.88
  207.9 0.1 select_n.29
  208.0 10.6 %all-to-all-done = f32[16,6,32,128]{3,2,1,0:T(8,128)S(1)} async-done(((f32[16,6,32,128]{3,2,1,0:T(8,128)}), f32[16,6,32,128]{3,2,1,0:T(8,128)S(1)}, u32[]{:S(2)}, u32[]{:S(2)}) %all-to-all-start) | async-done | bytes 1572896 | tf_op jit(solution)/shard_map/all_to_all | solution.py:198
  218.6 0.3 pad_maximum_fusion
  218.9 0.5 copy.93
  219.4 4.9 %fusion = f32[8,27,32,128]{3,1,2,0:T(8,128)} fusion(f32[192,32,128]{2,1,0:T(8,128)S(1)} %bitcast.35, f32[8,27]{1,0:T(8,128)S(1)} %multiply_add_fusion, f32[192]{0:T(256)S(1)} %select_n.29), kind=kOutput, calls=%fused_computation.1 | convolution fusion | flops 1019257344 | bytes 6686304 | tf_op jit(solution)/shard_map/ec,eml->cml/dot_general | solution.py:215
  224.3 40.3 %reduce-scatter.5.cloned.1.call-done = f32[1,27,32,128]{3,1,2,0:T(8,128)} async-done(((f32[8,27,32,128]{3,1,2,0:T(8,128)}), f32[1,27,32,128]{3,1,2,0:T(8,128)}) %reduce-scatter.5.cloned.1.call-update) | async-done | bytes 442384 | tf_op jit(solution)/shard_map/reduce_scatter | solution.py:217
  264.6 2.1 copy.95
  (19 shorter events, 0.2 us)
Async XLA Ops:
  6.5 5.3 %copy-start.1 = (s32[1,1,3,448]{3,1,2,0:T(1,128)S(1)}, s32[1,1,3,448]{3,1,2,0:T(1,128)}, u32[]{:S(2)}) copy-start(s32[1,1,3,448]{3,1,2,0:T(1,128)} %param.12) | copy-start | bytes 16132
  6.5 70.5 %all-gather.2.cloned.1.call-start = ((), (), s32[]{:S(2)}) async-start(), calls=%async_computation.4 | async-start | bytes 6963200 | tf_op jit(solution)/shard_map/all_gather | solution.py:171
  8.9 13.2 %copy-start = (f32[24,32,128]{2,1,0:T(8,128)}, f32[24,32,128]{2,1,0:T(8,128)S(1)}, u32[]{:S(2)}) copy-start(f32[24,32,128]{2,1,0:T(8,128)S(1)} %reshape.122.p2_ref) | copy-start | bytes 1179652
  11.8 145.7 %reduce-scatter.3.cloned.1.call-start = ((), (), s32[]{:S(2)}) async-start(), calls=%async_computation.5 | async-start | bytes 7077888 | tf_op jit(solution)/shard_map/reduce_scatter | solution.py:181
  164.1 30.2 %all-to-all-start.1 = ((f32[16,6,32,128]{3,2,1,0:T(8,128)}), f32[16,6,32,128]{3,2,1,0:T(8,128)S(1)}, u32[]{:S(2)}, u32[]{:S(2)}) async-start(f32[16,6,32,128]{3,2,1,0:T(8,128)} %shard_map.93), calls=%async_computation.2 | async-start | bytes 3145728 | tf_op jit(solution)/shard_map/all_to_all | solution.py:198
  194.3 24.3 %all-to-all-start = ((f32[16,6,32,128]{3,2,1,0:T(8,128)}), f32[16,6,32,128]{3,2,1,0:T(8,128)S(1)}, u32[]{:S(2)}, u32[]{:S(2)}) async-start(f32[16,6,32,128]{3,2,1,0:T(8,128)} %shard_map.92), calls=%async_computation.1 | async-start | bytes 3145728 | tf_op jit(solution)/shard_map/all_to_all | solution.py:198
  198.0 66.6 %reduce-scatter.5.cloned.1.call-start = ((), (), s32[]{:S(2)}) async-start(), calls=%async_computation.6 | async-start | bytes 4718592 | tf_op jit(solution)/shard_map/reduce_scatter | solution.py:217
Sparse Core Ops, SparseCore 0:
  11.9 65.1 all-gather.1
  111.2 46.2 reduce-scatter.2
  224.4 40.1 reduce-scatter.4
